TPU v7x, 128 devices: a whole 4x4x4 slice. The times are simulated.
128 devices in a mesh: dp: 8 (over z, core), expert: 16 (over x, y).
Axes of the slice: x: 4, y: 4, z: 4, core: 2. Of those that a mesh axis runs over, the one named last changes fastest.
Arguments:
- tokens: bfloat16 [1024, 6144], P('dp'), may hold values from -6 to 6
- query_weight: bfloat16 [6144, 6144], P(None, 'expert'), may hold values from -1.03593 to 1.03593
- key_value_weight: bfloat16 [6144, 2048], P(None, 'expert'), may hold values from -0.05103104 to 0.05103104
- out_weight: bfloat16 [6144, 6144], P('expert'), may hold values from -0.078125 to 0.078125
- doc_lengths: int32 [8], replicated, may hold values from 1 to 512, 1024 in all
- expert_ids: int32 [1024, 2], P(('dp', 'expert')), may hold values from 0 to 3, all different within a row; in each aligned block of 8 rows (0 to 7, 8 to 15, ...) at most 6 rows name the same one
- router_weight: bfloat16 [6144, 4], replicated, may hold values from -0.078125 to 0.078125
- gate_weight: bfloat16 [6144, 32768], P(None, ('expert', 'dp')), may hold values from -0.078125 to 0.078125
- up_weight: bfloat16 [6144, 32768], P(None, ('expert', 'dp')), may hold values from -0.078125 to 0.078125
- down_weight: bfloat16 [32768, 6144], P(('expert', 'dp')), may hold values from -0.0625 to 0.0625
Outputs:
- layer_out: bfloat16 [1024, 6144], P(('dp', 'expert'))
Inputs may be any that keep to these rules, and one draw needn't show every extreme that they name: `expert_ids`: each row names 2 different experts; in each aligned block of 8 rows (the rows of one output block) no expert is named more than 6 times, a bound that some block reaches. `doc_lengths`: positive lengths summing to 1024; the longest is exactly 512.
All inputs are finite; a program needn't handle non-finite values.
Results may differ from a plain program's by a relative error of at most 0.012.
Values may be sent and summed in bfloat16 or wider, within the bound.
No kernel may reach another device: no remote copies, remote signals or barrier semaphores. Data moves between devices by JAX's collectives and lax.ppermute only.
A program may use at most 128 MiB of HBM per device.

v0:
```python
import jax
import jax.numpy as jnp
from jax import lax
from jax.sharding import PartitionSpec as P

HD = 128


EPSILON = 1e-05
ROPE_BASE = 1000000.0
MASKED_SCORE = -1e30


def partner_2(block, axis, distance):
    count = lax.axis_size(axis)
    route = []
    for low in range(count):
        high = low | 1 << distance
        if high != low and high < count:
            route += [(low, high), (high, low)]
    return lax.ppermute(block, axis, route)


def rms_rows(matrix):
    matrix = matrix.astype(jnp.float32)
    return matrix * lax.rsqrt(jnp.mean(matrix * matrix, axis=-1, keepdims=True) + EPSILON)


def rotate(vectors, positions):
    half_width = vectors.shape[-1] // 2
    frequency = ROPE_BASE ** (-jnp.arange(half_width, dtype=jnp.float32) * 2.0 / vectors.shape[-1])
    angles = positions.astype(jnp.float32)[:, None] * frequency[None, :]
    cosine = jnp.cos(angles)[:, None, :]
    sine_part = jnp.sin(angles)[:, None, :]
    first_half = vectors[..., :half_width]
    second = vectors[..., half_width:]
    return jnp.concatenate(
        [first_half * cosine - second * sine_part, second * cosine + first_half * sine_part],
        axis=-1,
    )


def doc_layout(doc_lengths, positions):
    doc_ends = jnp.cumsum(doc_lengths)
    passed = (positions[:, None] >= doc_ends[None, :]).astype(jnp.int32)
    document = jnp.sum(passed, axis=1)
    doc_start = jnp.sum(passed * doc_lengths[None, :], axis=1)
    return (document, positions - doc_start)


def slot_hits(route_rows, target, capacity):
    matches = route_rows == target
    chosen = jnp.sum(matches.astype(jnp.int32), axis=-2)
    before = jnp.cumsum(chosen, axis=-2) - chosen
    slot_range = jnp.arange(capacity, dtype=jnp.int32)
    return ((before[..., None] == slot_range) & (chosen[..., None] > 0), matches)


def routing(own_normed, own_routes, router_weight, capacity):
    experts = router_weight.shape[1]
    expert_range = jnp.arange(experts, dtype=jnp.int32)
    hits, matches = slot_hits(own_routes[:, :, None], expert_range[None, None, :], capacity)
    logits = jnp.dot(own_normed, router_weight, preferred_element_type=jnp.float32)
    picked = jnp.sum(jnp.where(matches, logits[:, None, :], 0.0), axis=2)
    gates = jax.nn.softmax(picked, axis=1)
    gate_cols = jnp.sum(jnp.where(matches, gates[:, :, None], 0.0), axis=1)
    dispatch_own = jnp.transpose(hits, (1, 2, 0))
    return (dispatch_own, gate_cols)


def expert_rows(arrived, gate_weight, up_weight, down_weight):
    arrived_shape = arrived.shape
    flat_rows = arrived.reshape(-1, arrived_shape[-1])
    gate_part = jnp.dot(flat_rows, gate_weight, preferred_element_type=jnp.float32)
    up_part = jnp.dot(flat_rows, up_weight, preferred_element_type=jnp.float32)
    activated = (jax.nn.silu(gate_part) * up_part).astype(jnp.bfloat16)
    produced = jnp.dot(activated, down_weight, preferred_element_type=jnp.float32).astype(
        jnp.bfloat16
    )
    return produced.reshape(arrived_shape)


def combine_rows(returned, dispatch_own, gate_cols, slab_count):
    experts, capacity, own_count = dispatch_own.shape
    model_width = returned.shape[-1]
    summed = jnp.sum(
        returned.reshape(-1, experts, slab_count, capacity, model_width).astype(jnp.float32),
        axis=(0, 2),
    )
    weights = dispatch_own.astype(jnp.float32) * jnp.transpose(gate_cols)[:, None, :]
    return jnp.einsum("ecr,ecd->rd", weights, summed, precision=lax.Precision.HIGHEST)


def per_device(
    tokens,
    query_weight,
    key_value_weight,
    out_weight,
    doc_lengths,
    expert_ids,
    router_weight,
    gate_weight,
    up_weight,
    down_weight,
):
    tok_dev = tokens.shape[0]
    model_width = tokens.shape[1]
    head_dim = HD
    per_group = query_weight.shape[1] // head_dim
    groups = lax.axis_size("expert")
    experts = router_weight.shape[1]
    slab_count = groups // experts
    own_count = tok_dev // groups
    capacity = own_count * 3 // 4
    my_place = lax.axis_index("expert")
    my_expert = my_place // slab_count
    holds_keys = my_place % 2 == 0
    row_offset = lax.axis_index("dp") * tok_dev
    positions = row_offset + jnp.arange(tok_dev, dtype=jnp.int32)
    document, in_document = doc_layout(doc_lengths, positions)
    normed_in = rms_rows(tokens).astype(jnp.bfloat16)
    queries = jnp.dot(normed_in, query_weight, preferred_element_type=jnp.float32).reshape(
        tok_dev, per_group, head_dim
    )
    queries = rotate(queries, in_document).astype(jnp.bfloat16)
    half_part = jnp.dot(normed_in, key_value_weight, preferred_element_type=jnp.float32)
    rotated = rotate(half_part[:, None, :], in_document)[:, 0, :]
    mine = jnp.where(holds_keys, rotated, half_part).astype(jnp.bfloat16)
    partner = partner_2(mine, "expert", 0)
    key_rows = jnp.where(holds_keys, mine, partner)
    values = jnp.where(holds_keys, partner, mine)
    score_scale = head_dim ** (-0.5)
    running_max = jnp.full((tok_dev, per_group), MASKED_SCORE, jnp.float32)
    key_piece = lax.all_gather(key_rows, "dp", axis=0, tiled=True)
    value_piece = lax.all_gather(values, "dp", axis=0, tiled=True)
    piece_rows = key_piece.shape[0]
    key_places = jnp.arange(piece_rows, dtype=jnp.int32)
    key_doc, unused = doc_layout(doc_lengths, key_places)
    allowed = (document[:, None] == key_doc[None, :]) & (key_places[None, :] <= positions[:, None])
    scores = (
        jnp.einsum("tqd,jd->tqj", queries, key_piece, preferred_element_type=jnp.float32)
        * score_scale
    )
    masked = jnp.where(allowed[:, None, :], scores, MASKED_SCORE)
    new_max = jnp.maximum(running_max, jnp.max(masked, axis=2))
    expo = jnp.where(allowed[:, None, :], jnp.exp(masked - new_max[..., None]), 0.0)
    running_sum = jnp.sum(expo, axis=2)
    update = jnp.einsum(
        "tqj,jd->tqd", expo.astype(jnp.bfloat16), value_piece, preferred_element_type=jnp.float32
    )
    weighted = update
    running_max, running_sum, weighted = (new_max, running_sum, weighted)
    context = (
        (weighted / running_sum[..., None])
        .astype(jnp.bfloat16)
        .reshape(tok_dev, per_group * head_dim)
    )
    partial_value = jnp.dot(context, out_weight, preferred_element_type=jnp.float32)
    attention = lax.psum(partial_value.astype(jnp.bfloat16), "expert").astype(jnp.float32)
    hidden_state = tokens.astype(jnp.float32) + attention
    normed = rms_rows(hidden_state).astype(jnp.bfloat16)
    routes = lax.all_gather(expert_ids, "expert", axis=0, tiled=True)
    blocks = routes.reshape(groups, own_count, routes.shape[1])
    hits, unused = slot_hits(blocks[..., None], my_expert, capacity)
    selection = hits[:, :, 0, :].astype(jnp.bfloat16)
    per_block = normed.reshape(groups, own_count, model_width)
    arrived = jnp.einsum(
        "grc,grd->gcd", selection, per_block, preferred_element_type=jnp.float32
    ).astype(jnp.bfloat16)
    produced = expert_rows(
        lax.all_gather(arrived, "dp", axis=0, tiled=True), gate_weight, up_weight, down_weight
    )
    returned = lax.all_to_all(produced, ("dp", "expert"), split_axis=0, concat_axis=0, tiled=True)
    own_state = lax.dynamic_slice_in_dim(hidden_state, my_place * own_count, own_count, 0)
    own_normed = lax.dynamic_slice_in_dim(normed, my_place * own_count, own_count, 0)
    dispatch_own, gate_cols = routing(own_normed, expert_ids, router_weight, capacity)
    moe = combine_rows(returned, dispatch_own, gate_cols, slab_count)
    return (own_state + moe).astype(jnp.bfloat16)


def solution(mesh):
    placed = (
        P("dp", None),
        P(None, "expert"),
        P(None, "expert"),
        P("expert", None),
        P(),
        P(("dp", "expert"), None),
        P(),
        P(None, ("expert", "dp")),
        P(None, ("expert", "dp")),
        P(("expert", "dp"), None),
    )
    return jax.shard_map(
        per_device, mesh=mesh, in_specs=placed, out_specs=P(("dp", "expert"), None), check_vma=False
    )
```

profile of v0, /device:TPU:12, one launch (start us, length us, event | category | flops | bytes accessed | tf_op | source)
XLA Modules:
  0.0 474.7 jit_solution(1011539286811798069)
XLA Ops:
  6.5 0.0 all-reduce.2.cloned.1.call-start
  6.6 1.0 reduce-window.8
  7.6 1.9 fusion.2
  9.5 0.7 fusion.46
  10.3 2.7 fusion.13
  12.9 0.2 fusion.33
  13.1 0.6 fusion.26
  13.8 0.4 collective-permute-start
  14.2 0.1 convert_reduce_fusion.1
  14.3 1.0 multiply_cosine_fusion
  15.2 4.4 fusion.15
  19.6 0.7 fusion.53
  20.3 0.1 copy.40
  20.4 1.0 copy.39
  21.4 0.9 subtract_convert_fusion
  22.4 0.2 fusion.17
  22.6 0.0 collective-permute-done
  22.6 0.8 broadcast_select_fusion
  23.4 13.1 %all_gather.13 = bf16[1024,128]{0,1:T(8,128)(2,1)S(1)} all-gather(bf16[128,128]{0,1:T(8,128)(2,1)S(1)} %get-tuple-element.15), channel_id=1, replica_groups=mesh['dp'=8,'expert'=16] {'dp'}, dimensions={0}, use_global_device_ids=true | all-gather | bytes 294912 | tf_op jit(solution)/shard_map/all_gather | solution.py:135
  36.5 11.5 %all_gather.12 = bf16[1024,128]{0,1:T(8,128)(2,1)S(1)} all-gather(bf16[128,128]{0,1:T(8,128)(2,1)S(1)} %get-tuple-element.16), channel_id=1, replica_groups=mesh['dp'=8,'expert'=16] {'dp'}, dimensions={0}, use_global_device_ids=true | all-gather | bytes 294912 | tf_op jit(solution)/shard_map/all_gather | solution.py:134
  48.0 0.6 fusion.54
  48.5 0.5 fusion.5
  49.0 0.5 fusion.8
  49.5 0.0 copy-start.7
  49.6 4.5 convolution_convert_fusion.2
  54.1 0.0 all-reduce.2.cloned.1.call-update
  54.1 0.0 all-gather.3.cloned.1.call-start
  54.2 22.2 %all-gather = s32[16,8,2]{1,2,0:T(2,128)S(1)} all-gather(s32[1,8,2]{1,2,0:T(2,128)S(1)} %bitcast.59), channel_id=1, replica_groups=mesh['dp'=8,'expert'=16] {'expert'}, dimensions={0}, use_global_device_ids=true | all-gather | bytes 1088 | tf_op jit(solution)/shard_map/all_gather | solution.py:162
  76.4 0.2 reduce_window_sum.34
  76.6 66.0 %all-reduce.2.cloned.1.call-done = bf16[128,6144]{1,0:T(8,128)(2,1)} async-done(((bf16[128,6144]{1,0:T(8,128)(2,1)}), bf16[128,6144]{1,0:T(8,128)(2,1)}) %all-reduce.2.cloned.1.call-update) | async-done | bytes 1572880 | tf_op jit(solution)/shard_map/psum | solution.py:159
  142.6 4.2 convert_add_fusion
  146.8 0.5 multiply_convert_fusion
  147.4 1.1 copy-done.4
  148.5 0.6 convolution_convert_fusion.1
  149.1 1.7 copy.34
  150.7 0.0 all-gather.3.cloned.1.call-update
  150.8 55.8 %all-gather.3.cloned.1.call-done = bf16[128,6,6144]{2,0,1:T(8,128)(2,1)} async-done(((bf16[16,6,6144]{2,0,1:T(8,128)(2,1)}), bf16[128,6,6144]{2,0,1:T(8,128)(2,1)}) %all-gather.3.cloned.1.call-update) | async-done | bytes 9437200 | tf_op jit(solution)/shard_map/all_gather | solution.py:171
  206.6 12.8 %copy.35 = bf16[128,6,6144]{2,1,0:T(8,128)(2,1)} copy(bf16[128,6,6144]{2,0,1:T(8,128)(2,1)} %all-gather.3.cloned.1.call-done) | data formatting | bytes 18874368 | tf_op jit(solution)/shard_map/all_gather | solution.py:171
  219.4 14.3 %reshape.305 = bf16[768,6144]{1,0:T(8,128)(2,1)} reshape(bf16[128,6,6144]{2,1,0:T(8,128)(2,1)} %copy.35) | data formatting | bytes 18874368 | tf_op jit(solution)/shard_map/reshape | solution.py:73
  233.7 8.0 %fusion.55 = f32[768,256]{1,0:T(8,128)} fusion(bf16[768,6144]{1,0:T(8,128)(2,1)} %reshape.305, bf16[6144,256]{1,0:T(8,128)(2,1)} %param.17), kind=kOutput, calls=%fused_computation.95 | convolution fusion | flops 2415919104 | bytes 13369344 | tf_op jit(solution)/shard_map/dot_general | solution.py:74
  241.8 19.4 %convolution_convert_fusion = bf16[768,6144]{1,0:T(8,128)(2,1)} fusion(bf16[256,6144]{1,0:T(8,128)(2,1)S(1)} %copy-done, bf16[768,6144]{1,0:T(8,128)(2,1)} %reshape.305, bf16[6144,256]{1,0:T(8,128)(2,1)} %param.18, f32[768,256]{1,0:T(8,128)} %fusion.55), kind=kOutput, calls=%fused_computation.1 | convolution fusion | flops 4837736448 | bytes 25952256 | tf_op jit(solution)/shard_map/dot_general | solution.py:77
  261.2 14.1 %reshape.306 = bf16[128,6,6144]{2,1,0:T(8,128)(2,1)} reshape(bf16[768,6144]{1,0:T(8,128)(2,1)} %convolution_convert_fusion) | data formatting | bytes 18874368 | tf_op jit(solution)/shard_map/reshape | solution.py:80
  275.3 8.6 %all-to-all-start = ((bf16[128,6,6144]{2,1,0:T(8,128)(2,1)}), bf16[128,6,6144]{2,1,0:T(8,128)(2,1)}, u32[]{:S(2)}, u32[]{:S(2)}) async-start(bf16[128,6,6144]{2,1,0:T(8,128)(2,1)} %reshape.306), calls=%async_computation | async-start | bytes 25165824 | tf_op jit(solution)/shard_map/all_to_all | solution.py:173
  284.0 0.2 reduce_window_sum.32
  284.2 1.1 fusion.23
  285.3 171.5 %all-to-all-done = bf16[128,6,6144]{2,1,0:T(8,128)(2,1)} async-done(((bf16[128,6,6144]{2,1,0:T(8,128)(2,1)}), bf16[128,6,6144]{2,1,0:T(8,128)(2,1)}, u32[]{:S(2)}, u32[]{:S(2)}) %all-to-all-start) | async-done | bytes 9437216 | tf_op jit(solution)/shard_map/all_to_all | solution.py:173
  456.8 7.9 %convert_reduce_fusion = f32[4,6,6144]{2,1,0:T(8,128)S(1)} fusion(bf16[8,4,4,6,6144]{4,3,2,1,0:T(8,128)(2,1)} %bitcast.15), kind=kLoop, calls=%fused_computation | loop fusion | flops 9289728 | bytes 10027008 | tf_op jit(solution)/shard_map/reduce_sum | solution.py:86
  464.7 3.2 fusion.1
  (31 shorter events, 0.2 us)
Async XLA Ops:
  6.5 235.2 %copy-start = (bf16[256,6144]{1,0:T(8,128)(2,1)S(1)}, bf16[256,6144]{1,0:T(8,128)(2,1)}, u32[]{:S(2)}) copy-start(bf16[256,6144]{1,0:T(8,128)(2,1)} %param.19) | copy-start | bytes 9437188
  6.5 136.0 %all-reduce.2.cloned.1.call-start = ((), (), s32[]{:S(2)}) async-start(), calls=%async_computation.1 | async-start | bytes 3145728 | tf_op jit(solution)/shard_map/psum | solution.py:159
  7.6 7.7 %copy-start.2 = (bf16[128,6144]{1,0:T(8,128)(2,1)S(1)}, bf16[128,6144]{1,0:T(8,128)(2,1)}, u32[]{:S(2)}) copy-start(bf16[128,6144]{1,0:T(8,128)(2,1)} %param.10) | copy-start | bytes 4718596
  13.8 8.8 %collective-permute-start = (bf16[128,128]{0,1:T(8,128)(2,1)}, bf16[128,128]{0,1:T(8,128)(2,1)}, u32[]{:S(2)}, u32[]{:S(2)}) collective-permute-start(bf16[128,128]{0,1:T(8,128)(2,1)} %fusion.26), channel_id=1, source_target_pairs={{0,1},{1,0},{2,3},{3,2},{4,5},{5,4},{6,7},{7,6},{8,9},{9,8},{10,11... | collective-permute-start | bytes 98312 | tf_op jit(solution)/shard_map/ppermute | solution.py:21
  49.5 4.6 copy-start.7
  54.1 152.5 %all-gather.3.cloned.1.call-start = ((), (), s32[]{:S(2)}) async-start(), calls=%async_computation.2 | async-start | bytes 10616832 | tf_op jit(solution)/shard_map/all_gather | solution.py:171
  142.6 4.2 copy-start.3
  142.6 4.2 copy-start.5
  147.4 1.1 copy-start.4
  275.3 8.8 %copy-start.6 = (bf16[6144,4]{0,1:T(4,128)(2,1)S(1)}, bf16[6144,4]{0,1:T(4,128)(2,1)}, u32[]{:S(2)}) copy-start(bf16[6144,4]{0,1:T(4,128)(2,1)} %param.16) | copy-start | bytes 147460
  275.3 181.5 %all-to-all-start = ((bf16[128,6,6144]{2,1,0:T(8,128)(2,1)}), bf16[128,6,6144]{2,1,0:T(8,128)(2,1)}, u32[]{:S(2)}, u32[]{:S(2)}) async-start(bf16[128,6,6144]{2,1,0:T(8,128)(2,1)} %reshape.306), calls=%async_computation | async-start | bytes 25165824 | tf_op jit(solution)/shard_map/all_to_all | solution.py:173
  456.8 11.1 %copy-start.1 = (bf16[256,6144]{1,0:T(8,128)(2,1)S(1)}, bf16[256,6144]{1,0:T(8,128)(2,1)}, u32[]{:S(2)}) copy-start(bf16[256,6144]{1,0:T(8,128)(2,1)} %param.19) | copy-start | bytes 9437188
Sparse Core Ops, SparseCore 0:
  54.2 88.2 all-reduce.1
  150.9 55.6 all-gather.2
where the time goes:
time: 476 us; the launch traced here: 475 us
  waiting for transfers between devices  293 us (62%)
  blocking collectives  46.8 us (10%)
  local copies, waits for them, and re-layouts  45.9 us (10%)
  matrix products  44.9 us (9%)
  other arithmetic  21.1 us (4%)
  between operations  13.6 us (3%)
  starting transfers between devices  9.12 us (2%)
    all_to_all x1, waiting for transfers between devices, per_device(): lax.all_to_all(produced, ('dp', 'expert'), split_axis=0, concat_axis=0, t...  171 us
    psum x1, waiting for transfers between devices, per_device(): lax.psum(partial_value.astype(jnp.bfloat16), 'expert').astype(jnp.float32)  66 us
    all_gather x1, waiting for transfers between devices, per_device(): lax.all_gather(arrived, 'dp', axis=0, tiled=True)  55.8 us
    all_gather x1, blocking collectives, per_device(): routes = lax.all_gather(expert_ids, 'expert', axis=0, tiled=True)  22.2 us
    dot_general x1, matrix products, expert_rows(): jnp.dot(activated, down_weight, preferred_element_type=jnp.float32)  19.4 us
    reshape x1, local copies, waits for them, and re-layouts, expert_rows(): flat_rows = arrived.reshape(-1, arrived_shape[-1])  14.3 us
    reshape x1, local copies, waits for them, and re-layouts, expert_rows(): return produced.reshape(arrived_shape)  14.1 us
    all_gather x1, blocking collectives, per_device(): value_piece = lax.all_gather(values, 'dp', axis=0, tiled=True)  13.1 us
  transfers between devices with their start and end apart: 4, of which 3 were waited for; matrix products, arithmetic and copies ran while one was open for 2% of the time, Pallas kernels for 0%

commit v1 on v0

v1 whole, which is shorter than its diff:
```python
import jax
import jax.numpy as jnp
import numpy as np
from jax import lax
from jax.sharding import Mesh
from jax.sharding import PartitionSpec as P

HD = 128
CORES = 2

EPSILON = 1e-05
ROPE_BASE = 1000000.0
MASKED_SCORE = -1e30


def rms_rows(matrix):
    matrix = matrix.astype(jnp.float32)
    return matrix * lax.rsqrt(jnp.mean(matrix * matrix, axis=-1, keepdims=True) + EPSILON)


def rotate(vectors, positions):
    half_width = vectors.shape[-1] // 2
    frequency = ROPE_BASE ** (-jnp.arange(half_width, dtype=jnp.float32) * 2.0 / vectors.shape[-1])
    angles = positions.astype(jnp.float32)[:, None] * frequency[None, :]
    cosine = jnp.cos(angles)[:, None, :]
    sine_part = jnp.sin(angles)[:, None, :]
    first_half = vectors[..., :half_width]
    second = vectors[..., half_width:]
    return jnp.concatenate(
        [first_half * cosine - second * sine_part, second * cosine + first_half * sine_part],
        axis=-1,
    )


def doc_layout(doc_lengths, positions):
    doc_ends = jnp.cumsum(doc_lengths)
    passed = (positions[:, None] >= doc_ends[None, :]).astype(jnp.int32)
    document = jnp.sum(passed, axis=1)
    doc_start = jnp.sum(passed * doc_lengths[None, :], axis=1)
    return (document, positions - doc_start)


def per_device(
    tokens,
    query_weight,
    key_value_weight,
    out_weight,
    doc_lengths,
    expert_ids,
    router_weight,
    gate_weight,
    up_weight,
    down_weight,
):
    tok_dev, model_width = tokens.shape
    head_dim = HD
    per_group = query_weight.shape[1] // head_dim
    nx = lax.axis_size("x")
    ny = lax.axis_size("y")
    nc = lax.axis_size("c")
    xi = lax.axis_index("x")
    yi = lax.axis_index("y")
    zi = lax.axis_index("z")
    ci = lax.axis_index("c")
    shard = zi * nc + ci
    group = xi * ny + yi
    experts = router_weight.shape[1]
    own_count = tok_dev // (nx * ny)
    capacity = own_count * 3 // 4

    positions = shard * tok_dev + jnp.arange(tok_dev, dtype=jnp.int32)
    document, in_document = doc_layout(doc_lengths, positions)
    normed_in = rms_rows(tokens).astype(jnp.bfloat16)
    queries = jnp.dot(normed_in, query_weight, preferred_element_type=jnp.float32).reshape(
        tok_dev, per_group, head_dim
    )
    queries = rotate(queries, in_document).astype(jnp.bfloat16)
    half_part = jnp.dot(normed_in, key_value_weight, preferred_element_type=jnp.float32)
    rotated = rotate(half_part[:, None, :], in_document)[:, 0, :]
    holds_keys = group % 2 == 0
    mine = jnp.where(holds_keys, rotated, half_part).astype(jnp.bfloat16)
    pairs = [(i, i ^ 1) for i in range(ny)]
    partner = lax.ppermute(mine, "y", pairs)
    key_rows = jnp.where(holds_keys, mine, partner)
    values = jnp.where(holds_keys, partner, mine)
    both = jnp.stack([key_rows, values], axis=0)
    gathered = lax.all_gather(both, ("z", "c"), axis=1, tiled=True)
    key_piece = gathered[0]
    value_piece = gathered[1]
    piece_rows = key_piece.shape[0]
    key_places = jnp.arange(piece_rows, dtype=jnp.int32)
    key_doc, unused = doc_layout(doc_lengths, key_places)
    allowed = (document[:, None] == key_doc[None, :]) & (key_places[None, :] <= positions[:, None])
    scores = (
        jnp.einsum("tqd,jd->tqj", queries, key_piece, preferred_element_type=jnp.float32)
        * head_dim ** (-0.5)
    )
    masked = jnp.where(allowed[:, None, :], scores, MASKED_SCORE)
    row_max = jnp.max(masked, axis=2)
    expo = jnp.where(allowed[:, None, :], jnp.exp(masked - row_max[..., None]), 0.0)
    denom = jnp.sum(expo, axis=2)
    weighted = jnp.einsum(
        "tqj,jd->tqd", expo.astype(jnp.bfloat16), value_piece, preferred_element_type=jnp.float32
    )
    context = (
        (weighted / denom[..., None]).astype(jnp.bfloat16).reshape(tok_dev, per_group * head_dim)
    )
    partial_value = jnp.dot(context, out_weight, preferred_element_type=jnp.float32)
    attention = lax.psum_scatter(
        partial_value.astype(jnp.bfloat16), ("x", "y"), scatter_dimension=0, tiled=True
    ).astype(jnp.float32)

    own_tokens = lax.dynamic_slice_in_dim(tokens, group * own_count, own_count, 0)
    hidden_state = own_tokens.astype(jnp.float32) + attention
    normed = rms_rows(hidden_state).astype(jnp.bfloat16)
    logits = jnp.dot(normed, router_weight, preferred_element_type=jnp.float32)
    expert_range = jnp.arange(experts, dtype=jnp.int32)
    matches = expert_ids[:, :, None] == expert_range[None, None, :]
    picked = jnp.sum(jnp.where(matches, logits[:, None, :], 0.0), axis=2)
    gates = jax.nn.softmax(picked, axis=1)
    gate_cols = jnp.sum(jnp.where(matches, gates[:, :, None], 0.0), axis=1)
    names = jnp.any(matches, axis=1).astype(jnp.int32)
    slot = jnp.cumsum(names, axis=0) - names
    slot_range = jnp.arange(capacity, dtype=jnp.int32)
    hits = (slot[:, :, None] == slot_range) & (names[:, :, None] > 0)
    send = jnp.einsum(
        "rec,rd->ecd", hits.astype(jnp.bfloat16), normed, preferred_element_type=jnp.float32
    ).astype(jnp.bfloat16)

    arrived = lax.all_to_all(send, "x", split_axis=0, concat_axis=0, tiled=True)
    arrived = arrived.reshape(experts * capacity, model_width)
    rows = lax.all_gather(arrived, ("y", "z"), axis=0, tiled=True)
    rows = lax.all_gather(rows, "c", axis=0, tiled=True)

    gate_part = jnp.dot(rows, gate_weight, preferred_element_type=jnp.float32)
    up_part = jnp.dot(rows, up_weight, preferred_element_type=jnp.float32)
    activated = (jax.nn.silu(gate_part) * up_part).astype(jnp.bfloat16)
    produced = jnp.dot(activated, down_weight, preferred_element_type=jnp.float32).astype(
        jnp.bfloat16
    )

    summed = lax.psum_scatter(produced, "c", scatter_dimension=0, tiled=True)
    summed = lax.psum_scatter(summed, ("y", "z"), scatter_dimension=0, tiled=True)
    summed = summed.reshape(experts, capacity, model_width)
    returned = lax.all_to_all(summed, "x", split_axis=0, concat_axis=0, tiled=True)

    weights = jnp.where(hits, gate_cols[:, :, None], 0.0)
    moe = jnp.einsum(
        "rec,ecd->rd", weights, returned.astype(jnp.float32), precision=lax.Precision.HIGHEST
    )
    return (hidden_state + moe).astype(jnp.bfloat16)


def solution(mesh):
    dp_size = mesh.shape["dp"]

    def run(*args):
        experts = args[6].shape[1]
        ex_size = mesh.shape["expert"]
        devices = np.asarray(mesh.devices).reshape(
            dp_size // CORES, CORES, experts, ex_size // experts
        )
        fine = Mesh(devices, ("z", "c", "x", "y"))
        tok = ("z", "c")
        grp = ("x", "y")
        placed = (
            P(tok, None),
            P(None, grp),
            P(None, grp),
            P(grp, None),
            P(),
            P(tok + grp, None),
            P(),
            P(None, grp + tok),
            P(None, grp + tok),
            P(grp + tok, None),
        )
        body = jax.shard_map(
            per_device, mesh=fine, in_specs=placed, out_specs=P(tok + grp, None), check_vma=False
        )
        return body(*args)

    return run
```

time: 476 us -> 389 us (0.82)
  the two profiles are of different devices: /device:TPU:12 before, /device:TPU:112 now
where the time goes in v1:
time: 389 us; the launch traced here: 384 us
  waiting for transfers between devices  273 us (70%)
  matrix products  48.7 us (13%)
  blocking collectives  24.1 us (6%)
  between operations  14 us (4%)
  other arithmetic  11.8 us (3%)
  local copies, waits for them, and re-layouts  7.13 us (2%)
  starting transfers between devices  5.88 us (2%)
    unnamed x7, waiting for transfers between devices  167 us
    all_gather x1, waiting for transfers between devices, per_device(): rows = lax.all_gather(arrived, ('y', 'z'), axis=0, tiled=True)  51.7 us
    all_gather x1, waiting for transfers between devices, per_device(): rows = lax.all_gather(rows, 'c', axis=0, tiled=True)  27.2 us
    reduce_scatter x1, waiting for transfers between devices, per_device(): summed = lax.psum_scatter(produced, 'c', scatter_dimension=0, tiled=True)  21.5 us
    dot_general x1, matrix products, per_device(): jnp.dot(activated, down_weight, preferred_element_type=jnp.float32)  19.4 us
    all_gather x1, blocking collectives, per_device(): gathered = lax.all_gather(both, ('z', 'c'), axis=1, tiled=True)  12.9 us
    all_to_all x1, blocking collectives, per_device(): arrived = lax.all_to_all(send, 'x', split_axis=0, concat_axis=0, tiled=True)  11.2 us
    dot_general x1, matrix products, per_device(): gate_part = jnp.dot(rows, gate_weight, preferred_element_type=jnp.float32)  8.06 us
  transfers between devices with their start and end apart: 7, of which 6 were waited for; matrix products, arithmetic and copies ran while one was open for 3% of the time, Pallas kernels for 0%

profile of v1, /device:TPU:112, one launch (start us, length us, event | category | flops | bytes accessed | tf_op | source)
XLA Modules:
  0.0 384.4 jit_solution(10693237825929702553)
XLA Ops:
  6.6 1.0 reduce-window.8
  7.6 1.9 fusion.3
  9.5 0.1 fusion.33
  9.6 2.2 fusion.9
  11.9 0.2 fusion.21
  12.1 0.6 fusion.16
  12.7 1.3 collective-permute-start
  14.0 0.1 convert_reduce_fusion
  14.1 1.0 multiply_cosine_fusion
  15.0 4.4 %fusion.11 = f32[128,384]{0,1:T(8,128)S(1)} fusion(bf16[6144,384]{1,0:T(8,128)(2,1)} %param.11, bf16[128,6144]{1,0:T(8,128)(2,1)S(1)} %copy-done.1, f32[128]{0:T(128)S(1)} %add_rsqrt_fusion.1), kind=kOutput, calls=%fused_computation.20 | convolution fusion | flops 606339072 | bytes 6488576 | tf_op jit(solution)/shard_map/dot_general | solution.py:74
  19.4 0.7 fusion.46
  20.0 0.1 copy.41
  20.2 1.0 copy.40
  21.2 1.6 subtract_convert_fusion
  22.8 0.2 fusion.13
  23.0 0.8 select_bitcast_fusion.1
  23.8 12.9 %all_gather.9 = bf16[2,1024,128]{1,2,0:T(8,128)(2,1)} all-gather(bf16[2,128,128]{1,2,0:T(8,128)(2,1)S(1)} %pad_maximum_fusion.1), channel_id=1, replica_groups=mesh['z'=4,'c'=2,'x'=4,'y'=4] {'z','c'}, dimensions={1}, use_global_device_ids=true | all-gather | bytes 589824 | tf_op jit(solution)/shard_map/all_gather | solution.py:87
  36.7 2.0 fusion.47
  38.7 2.6 multiply_select_fusion
  41.3 2.5 fusion.7
  43.8 4.5 %convolution_convert_fusion.1 = bf16[128,6144]{1,0:T(8,128)(2,1)} fusion(bf16[128,384]{0,1:T(8,128)(2,1)S(1)} %bitcast.63, bf16[384,6144]{1,0:T(8,128)(2,1)} %param.13), kind=kOutput, calls=%fused_computation.2 | convolution fusion | flops 604766208 | bytes 6389760 | tf_op jit(solution)/shard_map/dot_general | solution.py:108
  48.4 0.0 all-gather.3.cloned.1.call-start
  48.4 0.6 copy-done.6
  49.0 0.2 reduce_window_sum.19
  49.2 0.6 dynamic-slice
  50.5 86.4 %all-reduce.4.cloned.1.call-done = bf16[128,6144]{1,0:T(8,128)(2,1)} async-done(((bf16[128,6144]{1,0:T(8,128)(2,1)}), bf16[128,6144]{1,0:T(8,128)(2,1)}) %all-reduce.4.cloned.1.call-update) | async-done | bytes 1572880
  136.9 1.1 multiply_reduce_fusion
  138.0 1.0 multiply_convert_fusion
  139.0 0.6 copy-done.4
  139.7 0.4 convolution_convert_fusion.2
  140.0 11.2 %all_to_all.10 = bf16[4,6,6144]{2,1,0:T(8,128)(2,1)S(1)} all-to-all(bf16[4,6,6144]{2,1,0:T(8,128)(2,1)S(1)} %convolution_convert_fusion.2), channel_id=1, replica_groups=mesh['z'=4,'c'=2,'x'=4,'y'=4] {'x'}, dimensions={0} | all-to-all | bytes 589824 | tf_op jit(solution)/shard_map/all_to_all | solution.py:130
  151.2 0.8 reshape.263
  152.1 51.7 %all-gather.3.cloned.1.call-done = bf16[384,6144]{1,0:T(8,128)(2,1)} async-done(((bf16[24,6144]{1,0:T(8,128)(2,1)}), bf16[384,6144]{1,0:T(8,128)(2,1)}) %all-gather.3.cloned.1.call-update) | async-done | bytes 4718608 | tf_op jit(solution)/shard_map/all_gather | solution.py:132
  203.8 0.2 reduce-scatter.5.cloned.1.call-start
  204.1 27.2 %all-gather.5.cloned.1.call-done = bf16[768,6144]{1,0:T(8,128)(2,1)} async-done(((bf16[384,6144]{1,0:T(8,128)(2,1)}), bf16[768,6144]{1,0:T(8,128)(2,1)}) %all-gather.5.cloned.1.call-update) | async-done | bytes 9437200 | tf_op jit(solution)/shard_map/all_gather | solution.py:133
  231.3 8.1 %fusion.49 = f32[768,256]{1,0:T(8,128)} fusion(bf16[768,6144]{1,0:T(8,128)(2,1)} %all-gather.5.cloned.1.call-done, bf16[6144,256]{1,0:T(8,128)(2,1)} %param.17), kind=kOutput, calls=%fused_computation.87 | convolution fusion | flops 2415919104 | bytes 13369344 | tf_op jit(solution)/shard_map/dot_general | solution.py:135
  239.3 19.4 %convolution_convert_fusion = bf16[768,6144]{1,0:T(8,128)(2,1)} fusion(bf16[256,6144]{1,0:T(8,128)(2,1)S(1)} %copy-done, bf16[768,6144]{1,0:T(8,128)(2,1)} %all-gather.5.cloned.1.call-done, bf16[6144,256]{1,0:T(8,128)(2,1)} %param.18, f32[768,256]{1,0:T(8,128)} %fusion.49), kind=kOutput, calls=%fused_computation.1 | convolution fusion | flops 4837736448 | bytes 25952256 | tf_op jit(solution)/shard_map/dot_general | solution.py:138
  258.8 21.5 %reduce-scatter.5.cloned.1.call-done = bf16[384,6144]{1,0:T(8,128)(2,1)} async-done(((bf16[768,6144]{1,0:T(8,128)(2,1)}), bf16[384,6144]{1,0:T(8,128)(2,1)}) %reduce-scatter.5.cloned.1.call-update) | async-done | bytes 4718608 | tf_op jit(solution)/shard_map/reduce_scatter | solution.py:142
  280.3 0.9 copy-done.5
  281.1 0.2 fusion.48
  281.4 0.5 fusion.37
  281.9 80.0 %reduce-scatter.7.cloned.1.call-done = bf16[24,6144]{1,0:T(8,128)(2,1)} async-done(((bf16[384,6144]{1,0:T(8,128)(2,1)}), bf16[24,6144]{1,0:T(8,128)(2,1)}) %reduce-scatter.7.cloned.1.call-update) | async-done | bytes 294928
  361.9 1.8 reshape.264
  363.7 4.2 %all-to-all-start.1 = ((bf16[4,6,6144]{2,1,0:T(8,128)(2,1)}), bf16[4,6,6144]{2,1,0:T(8,128)(2,1)S(1)}, u32[]{:S(2)}, u32[]{:S(2)}) async-start(bf16[4,6,6144]{2,1,0:T(8,128)(2,1)} %reshape.264), calls=%async_computation.2 | async-start | bytes 786432 | tf_op jit(solution)/shard_map/all_to_all | solution.py:145
  368.0 0.7 fusion.36
  368.6 0.7 select_reduce_fusion
  369.3 6.0 %all-to-all-done.1 = bf16[4,6,6144]{2,1,0:T(8,128)(2,1)S(1)} async-done(((bf16[4,6,6144]{2,1,0:T(8,128)(2,1)}), bf16[4,6,6144]{2,1,0:T(8,128)(2,1)S(1)}, u32[]{:S(2)}, u32[]{:S(2)}) %all-to-all-start.1) | async-done | bytes 294944 | tf_op jit(solution)/shard_map/all_to_all | solution.py:145
  375.4 2.5 fusion.2
  (37 shorter events, 0.3 us)
Async XLA Ops:
  6.5 232.8 %copy-start = (bf16[256,6144]{1,0:T(8,128)(2,1)S(1)}, bf16[256,6144]{1,0:T(8,128)(2,1)}, u32[]{:S(2)}) copy-start(bf16[256,6144]{1,0:T(8,128)(2,1)} %param.19) | copy-start | bytes 9437188
  6.5 3.0 copy-start.7
  6.5 130.3 %all-reduce.4.cloned.1.call-start = ((), (), s32[]{:S(2)}) async-start(), calls=%async_computation.7 | async-start | bytes 3145728
  7.6 2.0 copy-start.1
  12.7 10.3 %collective-permute-start = (bf16[128,128]{0,1:T(8,128)(2,1)}, bf16[128,128]{0,1:T(8,128)(2,1)}, u32[]{:S(2)}, u32[]{:S(2)}) collective-permute-start(bf16[128,128]{0,1:T(8,128)(2,1)} %fusion.16), channel_id=1, source_target_pairs={{0,1},{1,0},{2,3},{3,2},{4,5},{5,4},{6,7},{7,6},{8,9},{9,8},{10,11... | collective-permute-start | bytes 98312 | tf_op jit(solution)/shard_map/ppermute | solution.py:83
  36.7 2.0 copy-start.2
  36.7 2.0 copy-start.3
  48.3 0.7 copy-start.6
  48.3 0.9 copy-start.9
  48.4 155.4 %all-gather.3.cloned.1.call-start = ((), (), s32[]{:S(2)}) async-start(), calls=%async_computation.4 | async-start | bytes 5013504 | tf_op jit(solution)/shard_map/all_gather | solution.py:132
  139.0 0.6 copy-start.4
  152.0 79.2 %all-gather.5.cloned.1.call-start = ((), (), s32[]{:S(2)}) async-start(), calls=%async_computation.5 | async-start | bytes 14155776 | tf_op jit(solution)/shard_map/all_gather | solution.py:133
  203.8 76.4 %reduce-scatter.5.cloned.1.call-start = ((), (), s32[]{:S(2)}) async-start(), calls=%async_computation.6 | async-start | bytes 14155776 | tf_op jit(solution)/shard_map/reduce_scatter | solution.py:142
  258.7 103.2 %reduce-scatter.7.cloned.1.call-start = ((), (), s32[]{:S(2)}) async-start(), calls=%async_computation.8 | async-start | bytes 5013504
  280.2 0.9 copy-start.5
  280.3 0.9 copy-start.8
  363.7 11.6 %all-to-all-start.1 = ((bf16[4,6,6144]{2,1,0:T(8,128)(2,1)}), bf16[4,6,6144]{2,1,0:T(8,128)(2,1)S(1)}, u32[]{:S(2)}, u32[]{:S(2)}) async-start(bf16[4,6,6144]{2,1,0:T(8,128)(2,1)} %reshape.264), calls=%async_computation.2 | async-start | bytes 786432 | tf_op jit(solution)/shard_map/all_to_all | solution.py:145
Sparse Core Ops, SparseCore 0:
  48.5 88.3 all-reduce.3
  152.2 51.6 all-gather.2
  205.5 25.7 all-gather.4
  258.8 21.3 reduce-scatter.4
  283.4 78.4 reduce-scatter.6

commit v2 on v1

--- a/solution.py
+++ b/solution.py
@@ -38,6 +38,13 @@
     document = jnp.sum(passed, axis=1)
     doc_start = jnp.sum(passed * doc_lengths[None, :], axis=1)
     return (document, positions - doc_start)
+
+
+def expert_rows(rows, gate_weight, up_weight, down_weight):
+    gate_part = jnp.dot(rows, gate_weight, preferred_element_type=jnp.float32)
+    up_part = jnp.dot(rows, up_weight, preferred_element_type=jnp.float32)
+    activated = (jax.nn.silu(gate_part) * up_part).astype(jnp.bfloat16)
+    return jnp.dot(activated, down_weight, preferred_element_type=jnp.float32).astype(jnp.bfloat16)
 
 
 def per_device(
@@ -106,9 +113,13 @@
         (weighted / denom[..., None]).astype(jnp.bfloat16).reshape(tok_dev, per_group * head_dim)
     )
     partial_value = jnp.dot(context, out_weight, preferred_element_type=jnp.float32)
-    attention = lax.psum_scatter(
-        partial_value.astype(jnp.bfloat16), ("x", "y"), scatter_dimension=0, tiled=True
-    ).astype(jnp.float32)
+    blocks = partial_value.astype(jnp.bfloat16).reshape(nx * ny, own_count, model_width)
+    attention = jnp.sum(
+        lax.all_to_all(blocks, ("x", "y"), split_axis=0, concat_axis=0, tiled=True).astype(
+            jnp.float32
+        ),
+        axis=0,
+    )
 
     own_tokens = lax.dynamic_slice_in_dim(tokens, group * own_count, own_count, 0)
     hidden_state = own_tokens.astype(jnp.float32) + attention
@@ -130,23 +141,26 @@
     arrived = lax.all_to_all(send, "x", split_axis=0, concat_axis=0, tiled=True)
     arrived = arrived.reshape(experts * capacity, model_width)
     rows = lax.all_gather(arrived, ("y", "z"), axis=0, tiled=True)
-    rows = lax.all_gather(rows, "c", axis=0, tiled=True)
+    core_swap = [(i, i ^ 1) for i in range(nc)]
+    other_rows = lax.ppermute(rows, "c", core_swap)
+    own_out = expert_rows(rows, gate_weight, up_weight, down_weight)
+    other_out = expert_rows(other_rows, gate_weight, up_weight, down_weight)
+    other_back = lax.ppermute(other_out, "c", core_swap)
+    summed = (own_out.astype(jnp.float32) + other_back.astype(jnp.float32)).astype(jnp.bfloat16)
 
-    gate_part = jnp.dot(rows, gate_weight, preferred_element_type=jnp.float32)
-    up_part = jnp.dot(rows, up_weight, preferred_element_type=jnp.float32)
-    activated = (jax.nn.silu(gate_part) * up_part).astype(jnp.bfloat16)
-    produced = jnp.dot(activated, down_weight, preferred_element_type=jnp.float32).astype(
-        jnp.bfloat16
+    lines = summed.reshape(-1, experts * capacity, model_width)
+    summed = jnp.sum(
+        lax.all_to_all(lines, ("y", "z"), split_axis=0, concat_axis=0, tiled=True).astype(
+            jnp.float32
+        ),
+        axis=0,
     )
-
-    summed = lax.psum_scatter(produced, "c", scatter_dimension=0, tiled=True)
-    summed = lax.psum_scatter(summed, ("y", "z"), scatter_dimension=0, tiled=True)
     summed = summed.reshape(experts, capacity, model_width)
     returned = lax.all_to_all(summed, "x", split_axis=0, concat_axis=0, tiled=True)
 
     weights = jnp.where(hits, gate_cols[:, :, None], 0.0)
     moe = jnp.einsum(
-        "rec,ecd->rd", weights, returned.astype(jnp.float32), precision=lax.Precision.HIGHEST
+        "rec,ecd->rd", weights, returned, precision=lax.Precision.HIGHEST
     )
     return (hidden_state + moe).astype(jnp.bfloat16)
 

time: 389 us -> 309 us (0.79)
  waiting for transfers between devices: 273 us -> 172 us
  starting transfers between devices: 5.88 us -> 20.5 us
  matrix products: 48.7 us -> 54.5 us
  other arithmetic: 11.8 us -> 16.1 us
    unnamed x7 -> x1, waiting for transfers between devices: 167 us -> 0.02 us
    all_to_all x0 -> x2, waiting for transfers between devices: none -> 97.6 us  [the longest x1 76 us: per_device(): lax.all_to_all(lines, ('y', 'z'), split_axis=0, concat_axis=0, tiled=True)]
    all_gather x1 -> x0, waiting for transfers between devices: 27.2 us -> none  [per_device(): rows = lax.all_gather(rows, 'c', axis=0, tiled=True)]
    reduce_scatter x1 -> x0, waiting for transfers between devices: 21.5 us -> none  [per_device(): summed = lax.psum_scatter(produced, 'c', scatter_dimension=0, tiled=True)]
    all_to_all x0 -> x2, starting transfers between devices: none -> 14.8 us  [the longest x1 7.41 us: per_device(): lax.all_to_all(blocks, ('x', 'y'), split_axis=0, concat_axis=0, tiled=True)]
    ppermute x0 -> x2, waiting for transfers between devices: none -> 10.8 us  [the longest x1 8.12 us: per_device(): other_rows = lax.ppermute(rows, 'c', core_swap)]
    reduce_sum x0 -> x2, other arithmetic: none -> 5.62 us  [the longest x1 3.98 us: per_device(): jnp.sum(lax.all_to_all(lines, ('y', 'z'), split_axis=0, concat_axis=0, ti...]
    all_to_all x1, waiting for transfers between devices: 6.02 us -> 11.6 us  [per_device(): lax.all_to_all(summed, 'x', split_axis=0, concat_axis=0, tiled=True)]
  transfers between devices with their start and end apart: 7 -> 7, of which waited for: 6 -> 6; matrix products, arithmetic and copies ran while one was open for 3% -> 5% of each run, Pallas kernels for 0% -> 0%
where the time goes in v2:
time: 309 us; the launch traced here: 308 us
  waiting for transfers between devices  172 us (56%)
  matrix products  54.5 us (18%)
  blocking collectives  23.6 us (8%)
  starting transfers between devices  20.5 us (7%)
  other arithmetic  16.1 us (5%)
  between operations  13.6 us (4%)
  local copies, waits for them, and re-layouts  7.89 us (3%)
    all_to_all x1, waiting for transfers between devices, per_device(): lax.all_to_all(lines, ('y', 'z'), split_axis=0, concat_axis=0, tiled=True)  76 us
    all_gather x1, waiting for transfers between devices, per_device(): rows = lax.all_gather(arrived, ('y', 'z'), axis=0, tiled=True)  51.8 us
    dot_general x2, matrix products, expert_rows(): jnp.dot(activated, down_weight, preferred_element_type=jnp.float32)  22.4 us
    all_to_all x1, waiting for transfers between devices, per_device(): lax.all_to_all(blocks, ('x', 'y'), split_axis=0, concat_axis=0, tiled=True)  21.6 us
    all_gather x1, blocking collectives, per_device(): gathered = lax.all_gather(both, ('z', 'c'), axis=1, tiled=True)  12.9 us
    all_to_all x1, waiting for transfers between devices, per_device(): lax.all_to_all(summed, 'x', split_axis=0, concat_axis=0, tiled=True)  11.6 us
    all_to_all x1, blocking collectives, per_device(): arrived = lax.all_to_all(send, 'x', split_axis=0, concat_axis=0, tiled=True)  10.7 us
    dot_general x2, matrix products, expert_rows(): gate_part = jnp.dot(rows, gate_weight, preferred_element_type=jnp.float32)  9.51 us
  transfers between devices with their start and end apart: 7, of which 6 were waited for; matrix products, arithmetic and copies ran while one was open for 5% of the time, Pallas kernels for 0%

profile of v2, /device:TPU:112, one launch (start us, length us, event | category | flops | bytes accessed | tf_op | source)
XLA Modules:
  0.0 308.0 jit_solution(3163621801347355551)
XLA Ops:
  6.6 1.0 reduce-window.8
  7.6 0.9 fusion.41
  8.4 1.8 fusion.4
  10.2 2.7 fusion.10
  12.9 0.2 fusion.29
  13.1 0.6 fusion.24
  13.8 1.3 collective-permute-start
  15.0 1.0 multiply_cosine_fusion
  16.0 0.1 convert_reduce_fusion.2
  16.1 4.4 %fusion.12 = f32[128,384]{0,1:T(8,128)S(1)} fusion(bf16[6144,384]{1,0:T(8,128)(2,1)} %param.11, bf16[128,6144]{1,0:T(8,128)(2,1)S(1)} %copy-done.1, f32[128]{0:T(128)S(1)} %add_rsqrt_fusion.1), kind=kOutput, calls=%fused_computation.25 | convolution fusion | flops 606339072 | bytes 6488576 | tf_op jit(solution)/shard_map/dot_general | solution.py:81
  20.5 0.7 fusion.56
  21.1 0.1 copy.33
  21.3 1.0 copy.34
  22.3 1.6 subtract_convert_fusion
  23.9 0.2 fusion.14
  24.1 0.8 select_bitcast_fusion.1
  24.9 12.9 %all_gather.6 = bf16[2,1024,128]{1,2,0:T(8,128)(2,1)} all-gather(bf16[2,128,128]{1,2,0:T(8,128)(2,1)S(1)} %pad_maximum_fusion.1), channel_id=1, replica_groups=mesh['z'=4,'c'=2,'x'=4,'y'=4] {'z','c'}, dimensions={1}, use_global_device_ids=true | all-gather | bytes 589824 | tf_op jit(solution)/shard_map/all_gather | solution.py:94
  37.8 2.0 fusion.57
  39.8 2.6 multiply_select_fusion
  42.4 2.5 fusion.8
  44.9 4.5 %fusion.1 = bf16[16,8,6144]{2,1,0:T(8,128)(2,1)} fusion(bf16[128,384]{0,1:T(8,128)(2,1)S(1)} %bitcast.61, bf16[384,6144]{1,0:T(8,128)(2,1)} %param.13), kind=kOutput, calls=%fused_computation.6 | convolution fusion | flops 604766208 | bytes 6389760 | tf_op jit(solution)/shard_map/dot_general | solution.py:115
  49.4 7.4 %all-to-all-start = ((bf16[16,8,6144]{2,1,0:T(8,128)(2,1)}), bf16[16,8,6144]{2,1,0:T(8,128)(2,1)}, u32[]{:S(2)}, u32[]{:S(2)}) async-start(bf16[16,8,6144]{2,1,0:T(8,128)(2,1)} %fusion.1), calls=%async_computation | async-start | bytes 3145728 | tf_op jit(solution)/shard_map/all_to_all | solution.py:118
  56.8 0.0 all-gather.2.cloned.1.call-start
  56.9 0.2 reduce_window_sum.19
  57.1 21.6 %all-to-all-done = bf16[16,8,6144]{2,1,0:T(8,128)(2,1)} async-done(((bf16[16,8,6144]{2,1,0:T(8,128)(2,1)}), bf16[16,8,6144]{2,1,0:T(8,128)(2,1)}, u32[]{:S(2)}, u32[]{:S(2)}) %all-to-all-start) | async-done | bytes 1572896 | tf_op jit(solution)/shard_map/all_to_all | solution.py:118
  78.7 1.6 convert_reduce_fusion.1
  80.3 1.1 multiply_reduce_fusion
  81.4 1.0 multiply_convert_fusion.2
  82.4 0.4 convolution_convert_fusion.3
  82.8 10.7 %all_to_all.20 = bf16[4,6,6144]{2,1,0:T(8,128)(2,1)} all-to-all(bf16[4,6,6144]{2,1,0:T(8,128)(2,1)S(1)} %convolution_convert_fusion.3), channel_id=1, replica_groups=mesh['z'=4,'c'=2,'x'=4,'y'=4] {'x'}, dimensions={0} | all-to-all | bytes 589824 | tf_op jit(solution)/shard_map/all_to_all | solution.py:141
  93.5 1.8 reshape.270
  95.3 51.8 %all-gather.2.cloned.1.call-done = bf16[384,6144]{1,0:T(8,128)(2,1)} async-done(((bf16[24,6144]{1,0:T(8,128)(2,1)}), bf16[384,6144]{1,0:T(8,128)(2,1)}) %all-gather.2.cloned.1.call-update) | async-done | bytes 4718608 | tf_op jit(solution)/shard_map/all_gather | solution.py:143
  147.1 8.1 %collective-permute-done.1 = bf16[384,6144]{1,0:T(8,128)(2,1)S(1)} collective-permute-done((bf16[384,6144]{1,0:T(8,128)(2,1)}, bf16[384,6144]{1,0:T(8,128)(2,1)S(1)}, u32[]{:S(2)}, u32[]{:S(2)}) %collective-permute-start.1) | collective-permute-done | bytes 4718624 | tf_op jit(solution)/shard_map/ppermute | solution.py:145
  155.2 2.2 copy-done.2
  157.5 4.1 %fusion.62 = f32[384,256]{1,0:T(8,128)} fusion(bf16[384,6144]{1,0:T(8,128)(2,1)S(1)} %collective-permute-done.1, bf16[6144,256]{1,0:T(8,128)(2,1)} %param.17), kind=kOutput, calls=%fused_computation.104 | convolution fusion | flops 1207959552 | bytes 8257536 | tf_op jit(solution)/shard_map/dot_general | solution.py:44
  161.5 10.5 %convolution_convert_fusion = bf16[384,6144]{1,0:T(8,128)(2,1)} fusion(bf16[256,6144]{1,0:T(8,128)(2,1)S(1)} %copy-done, f32[384,256]{1,0:T(8,128)} %fusion.62, bf16[384,6144]{1,0:T(8,128)(2,1)} %copy-done.2, bf16[6144,256]{1,0:T(8,128)(2,1)} %param.18), kind=kOutput, calls=%fused_computation.3 | convolution fusion | flops 2418868224 | bytes 16121856 | tf_op jit(solution)/shard_map/dot_general | solution.py:47
  172.0 0.1 collective-permute-start.2
  172.2 5.5 %fusion.61 = f32[384,256]{1,0:T(8,128)} fusion(bf16[384,6144]{1,0:T(8,128)(2,1)} %all-gather.2.cloned.1.call-done, bf16[6144,256]{1,0:T(8,128)(2,1)} %param.17), kind=kOutput, calls=%fused_computation.103 | convolution fusion | flops 1207959552 | bytes 8257536 | tf_op jit(solution)/shard_map/dot_general | solution.py:44
  177.6 2.6 collective-permute-done.2
  180.3 11.9 %add_convert_fusion = bf16[384,6144]{1,0:T(8,128)(2,1)} fusion(bf16[384,6144]{1,0:T(8,128)(2,1)} %collective-permute-done.2, bf16[256,6144]{1,0:T(8,128)(2,1)S(1)} %copy-done, bf16[384,6144]{1,0:T(8,128)(2,1)} %all-gather.2.cloned.1.call-done, bf16[6144,256]{1,0:T(8,128)(2,1)} %param.18, f32[384,256]{1,0:T(8,128)} %fusion.61), kind=kOutput, calls=%fused_computation.2 | convolution fusion | flops 2428305408 | bytes 20840448 | tf_op jit(solution)/shard_map/dot_general | solution.py:47
  192.2 7.3 %all-to-all-start.2 = ((bf16[16,24,6144]{2,1,0:T(8,128)(2,1)}), bf16[16,24,6144]{2,1,0:T(8,128)(2,1)}, u32[]{:S(2)}, u32[]{:S(2)}) async-start(bf16[16,24,6144]{2,1,0:T(8,128)(2,1)} %bitcast.58), calls=%async_computation.2 | async-start | bytes 9437184 | tf_op jit(solution)/shard_map/all_to_all | solution.py:153
  199.6 0.2 fusion.60
  199.8 76.0 %all-to-all-done.2 = bf16[16,24,6144]{2,1,0:T(8,128)(2,1)} async-done(((bf16[16,24,6144]{2,1,0:T(8,128)(2,1)}), bf16[16,24,6144]{2,1,0:T(8,128)(2,1)}, u32[]{:S(2)}, u32[]{:S(2)}) %all-to-all-start.2) | async-done | bytes 4718624 | tf_op jit(solution)/shard_map/all_to_all | solution.py:153
  275.8 4.0 %convert_reduce_fusion = f32[24,6144]{1,0:T(8,128)} fusion(bf16[16,24,6144]{2,1,0:T(8,128)(2,1)} %all-to-all-done.2), kind=kLoop, calls=%fused_computation.1 | loop fusion | flops 4571136 | bytes 5308416 | tf_op jit(solution)/shard_map/reduce_sum | solution.py:152
  279.7 2.0 reshape.272
  281.8 4.3 %all-to-all-start.3 = ((f32[4,6,6144]{2,1,0:T(8,128)}), f32[4,6,6144]{2,1,0:T(8,128)}, u32[]{:S(2)}, u32[]{:S(2)}) async-start(f32[4,6,6144]{2,1,0:T(8,128)} %reshape.272), calls=%async_computation.3 | async-start | bytes 1572864 | tf_op jit(solution)/shard_map/all_to_all | solution.py:159
  286.1 11.6 %all-to-all-done.3 = f32[4,6,6144]{2,1,0:T(8,128)} async-done(((f32[4,6,6144]{2,1,0:T(8,128)}), f32[4,6,6144]{2,1,0:T(8,128)}, u32[]{:S(2)}, u32[]{:S(2)}) %all-to-all-start.3) | async-done | bytes 589856 | tf_op jit(solution)/shard_map/all_to_all | solution.py:159
  297.7 3.4 %fusion.3 = bf16[8,6144]{1,0:T(8,128)(2,1)} fusion(f32[4,6,6144]{2,1,0:T(8,128)} %all-to-all-done.3, f32[8,6144]{1,0:T(8,128)S(1)} %convert_reduce_fusion.1, bf16[128,6144]{1,0:T(8,128)(2,1)} %param.10, s32[]{:T(128)S(6)} %select_n.47, f32[8,4]{0,1:T(4,128)S(1)} %select_reduce_fusion, s32[8,4]{0,1:T(4,128)S(1)} %convert_subtract_fusion, ...), kind=kOutput, calls=%fused_computation.10 | convolution fusion | flops 14352960 | bytes 983332 | tf_op jit(solution)/shard_map/rec,ecd->rd/dot_general | solution.py:162
  (30 shorter events, 0.2 us)
Async XLA Ops:
  6.5 155.0 %copy-start = (bf16[256,6144]{1,0:T(8,128)(2,1)S(1)}, bf16[256,6144]{1,0:T(8,128)(2,1)}, u32[]{:S(2)}) copy-start(bf16[256,6144]{1,0:T(8,128)(2,1)} %param.19) | copy-start | bytes 9437188
  7.6 8.5 %copy-start.1 = (bf16[128,6144]{1,0:T(8,128)(2,1)S(1)}, bf16[128,6144]{1,0:T(8,128)(2,1)}, u32[]{:S(2)}) copy-start(bf16[128,6144]{1,0:T(8,128)(2,1)} %param.10) | copy-start | bytes 4718596
  13.8 10.3 %collective-permute-start = (bf16[128,128]{0,1:T(8,128)(2,1)}, bf16[128,128]{0,1:T(8,128)(2,1)}, u32[]{:S(2)}, u32[]{:S(2)}) collective-permute-start(bf16[128,128]{0,1:T(8,128)(2,1)} %fusion.24), channel_id=1, source_target_pairs={{0,1},{1,0},{2,3},{3,2},{4,5},{5,4},{6,7},{7,6},{8,9},{9,8},{10,11... | collective-permute-start | bytes 98312 | tf_op jit(solution)/shard_map/ppermute | solution.py:90
  23.9 15.9 %copy-start.3 = (bf16[128,3,64]{2,0,1:T(8,128)(2,1)S(1)}, bf16[128,3,64]{2,0,1:T(8,128)(2,1)}, u32[]{:S(2)}) copy-start(bf16[128,3,64]{2,0,1:T(8,128)(2,1)} %get-tuple-element.7) | copy-start | bytes 147460
  23.9 15.9 %copy-start.4 = (bf16[128,3,64]{2,0,1:T(8,128)(2,1)S(1)}, bf16[128,3,64]{2,0,1:T(8,128)(2,1)}, u32[]{:S(2)}) copy-start(bf16[128,3,64]{2,0,1:T(8,128)(2,1)} %get-tuple-element.8) | copy-start | bytes 147460
  49.4 7.5 %copy-start.5 = (s32[8,2]{0,1:T(2,128)S(1)}, s32[8,2]{0,1:T(2,128)}, u32[]{:S(2)}) copy-start(s32[8,2]{0,1:T(2,128)} %param.15) | copy-start | bytes 196
  49.4 29.3 %all-to-all-start = ((bf16[16,8,6144]{2,1,0:T(8,128)(2,1)}), bf16[16,8,6144]{2,1,0:T(8,128)(2,1)}, u32[]{:S(2)}, u32[]{:S(2)}) async-start(bf16[16,8,6144]{2,1,0:T(8,128)(2,1)} %fusion.1), calls=%async_computation | async-start | bytes 3145728 | tf_op jit(solution)/shard_map/all_to_all | solution.py:118
  56.8 90.3 %all-gather.2.cloned.1.call-start = ((), (), s32[]{:S(2)}) async-start(), calls=%async_computation.4 | async-start | bytes 5013504 | tf_op jit(solution)/shard_map/all_gather | solution.py:143
  147.1 8.1 %collective-permute-start.1 = (bf16[384,6144]{1,0:T(8,128)(2,1)}, bf16[384,6144]{1,0:T(8,128)(2,1)S(1)}, u32[]{:S(2)}, u32[]{:S(2)}) collective-permute-start(bf16[384,6144]{1,0:T(8,128)(2,1)} %all-gather.2.cloned.1.call-done), channel_id=1, source_target_pairs={{0,16},{16,0},{1,17},{17,1},{2,18},{18,2},{3,19},{19,3},{4,20},{20... | collective-permute-start | bytes 14155784 | tf_op jit(solution)/shard_map/ppermute | solution.py:145
  155.2 2.2 copy-start.2
  172.0 8.3 %collective-permute-start.2 = (bf16[384,6144]{1,0:T(8,128)(2,1)}, bf16[384,6144]{1,0:T(8,128)(2,1)}, u32[]{:S(2)}, u32[]{:S(2)}) collective-permute-start(bf16[384,6144]{1,0:T(8,128)(2,1)} %convolution_convert_fusion), channel_id=1, source_target_pairs={{0,16},{16,0},{1,17},{17,1},{2,18},{18,2},{3,19},{19,3},{4,20},{20... | collective-permute-start | bytes 14155784 | tf_op jit(solution)/shard_map/ppermute | solution.py:148
  192.2 7.4 %copy-start.6 = (bf16[6144,4]{0,1:T(4,128)(2,1)S(1)}, bf16[6144,4]{0,1:T(4,128)(2,1)}, u32[]{:S(2)}) copy-start(bf16[6144,4]{0,1:T(4,128)(2,1)} %param.16) | copy-start | bytes 147460
  192.2 83.5 %all-to-all-start.2 = ((bf16[16,24,6144]{2,1,0:T(8,128)(2,1)}), bf16[16,24,6144]{2,1,0:T(8,128)(2,1)}, u32[]{:S(2)}, u32[]{:S(2)}) async-start(bf16[16,24,6144]{2,1,0:T(8,128)(2,1)} %bitcast.58), calls=%async_computation.2 | async-start | bytes 9437184 | tf_op jit(solution)/shard_map/all_to_all | solution.py:153
  281.8 16.0 %all-to-all-start.3 = ((f32[4,6,6144]{2,1,0:T(8,128)}), f32[4,6,6144]{2,1,0:T(8,128)}, u32[]{:S(2)}, u32[]{:S(2)}) async-start(f32[4,6,6144]{2,1,0:T(8,128)} %reshape.272), calls=%async_computation.3 | async-start | bytes 1572864 | tf_op jit(solution)/shard_map/all_to_all | solution.py:159
Sparse Core Ops, SparseCore 0:
  95.4 51.6 all-gather.1

commit v3 on v2

--- a/solution.py
+++ b/solution.py
@@ -5,8 +5,10 @@
 from jax.sharding import Mesh
 from jax.sharding import PartitionSpec as P
 
+
 HD = 128
 CORES = 2
+CHUNKS = 2
 
 EPSILON = 1e-05
 ROPE_BASE = 1000000.0
@@ -96,7 +98,7 @@
     value_piece = gathered[1]
     piece_rows = key_piece.shape[0]
     key_places = jnp.arange(piece_rows, dtype=jnp.int32)
-    key_doc, unused = doc_layout(doc_lengths, key_places)
+    key_doc, _ = doc_layout(doc_lengths, key_places)
     allowed = (document[:, None] == key_doc[None, :]) & (key_places[None, :] <= positions[:, None])
     scores = (
         jnp.einsum("tqd,jd->tqj", queries, key_piece, preferred_element_type=jnp.float32)
@@ -140,21 +142,21 @@
 
     arrived = lax.all_to_all(send, "x", split_axis=0, concat_axis=0, tiled=True)
     arrived = arrived.reshape(experts * capacity, model_width)
-    rows = lax.all_gather(arrived, ("y", "z"), axis=0, tiled=True)
     core_swap = [(i, i ^ 1) for i in range(nc)]
-    other_rows = lax.ppermute(rows, "c", core_swap)
-    own_out = expert_rows(rows, gate_weight, up_weight, down_weight)
-    other_out = expert_rows(other_rows, gate_weight, up_weight, down_weight)
-    other_back = lax.ppermute(other_out, "c", core_swap)
-    summed = (own_out.astype(jnp.float32) + other_back.astype(jnp.float32)).astype(jnp.bfloat16)
-
-    lines = summed.reshape(-1, experts * capacity, model_width)
-    summed = jnp.sum(
-        lax.all_to_all(lines, ("y", "z"), split_axis=0, concat_axis=0, tiled=True).astype(
-            jnp.float32
-        ),
-        axis=0,
-    )
+    chunk_rows = experts * capacity // CHUNKS
+    results = []
+    for part in range(CHUNKS):
+        piece = arrived[part * chunk_rows:(part + 1) * chunk_rows]
+        rows = lax.all_gather(piece, ("y", "z"), axis=0, tiled=True)
+        other_rows = lax.ppermute(rows, "c", core_swap)
+        own_out = expert_rows(rows, gate_weight, up_weight, down_weight)
+        other_out = expert_rows(other_rows, gate_weight, up_weight, down_weight)
+        other_back = lax.ppermute(other_out, "c", core_swap)
+        summed = (own_out.astype(jnp.float32) + other_back.astype(jnp.float32)).astype(jnp.bfloat16)
+        lines = summed.reshape(-1, chunk_rows, model_width)
+        spread = lax.all_to_all(lines, ("y", "z"), split_axis=0, concat_axis=0, tiled=True)
+        results.append(jnp.sum(spread.astype(jnp.float32), axis=0))
+    summed = jnp.concatenate(results, axis=0)
     summed = summed.reshape(experts, capacity, model_width)
     returned = lax.all_to_all(summed, "x", split_axis=0, concat_axis=0, tiled=True)
 

time: 309 us -> 366 us (1.18)
  waiting for transfers between devices: 172 us -> 191 us
  local copies, waits for them, and re-layouts: 7.89 us -> 24.4 us
  matrix products: 54.5 us -> 64 us
  starting transfers between devices: 20.5 us -> 28.9 us
    all_gather x1 -> x2, waiting for transfers between devices: 51.8 us -> 88.8 us  [per_device(): rows = lax.all_gather(piece, ('y', 'z'), axis=0, tiled=True)]
    unnamed x16 -> x24, local copies, waits for them, and re-layouts: 3.41 us -> 12.4 us
    ppermute x1 -> x2, waiting for transfers between devices: 8.12 us -> 0.01 us  [per_device(): other_rows = lax.ppermute(rows, 'c', core_swap)]
    all_to_all x1 -> x2, starting transfers between devices: 7.35 us -> 15.4 us  [per_device(): lax.all_to_all(lines, ('y', 'z'), split_axis=0, concat_axis=0, tiled=True)]
    reshape x1 -> x2, local copies, waits for them, and re-layouts: 1.81 us -> 8.58 us  [per_device(): lines = summed.reshape(-1, chunk_rows, model_width)]
    all_to_all x1 -> x2, waiting for transfers between devices: 76 us -> 69.7 us  [per_device(): lax.all_to_all(lines, ('y', 'z'), split_axis=0, concat_axis=0, tiled=True)]
    dot_general x2 -> x4, matrix products: 22.4 us -> 28 us  [expert_rows(): jnp.dot(activated, down_weight, preferred_element_type=jnp.float32)]
    dot_general x2 -> x4, matrix products: 9.51 us -> 13.5 us  [expert_rows(): gate_part = jnp.dot(rows, gate_weight, preferred_element_type=jnp.float32)]
  transfers between devices with their start and end apart: 7 -> 11, of which waited for: 6 -> 6; matrix products, arithmetic and copies ran while one was open for 5% -> 20% of each run, Pallas kernels for 0% -> 0%
where the time goes in v3:
time: 366 us; the launch traced here: 365 us
  waiting for transfers between devices  191 us (52%)
  matrix products  64 us (17%)
  starting transfers between devices  28.9 us (8%)
  local copies, waits for them, and re-layouts  24.4 us (7%)
  blocking collectives  23.6 us (6%)
  other arithmetic  18.7 us (5%)
  between operations  13.7 us (4%)
    all_gather x2, waiting for transfers between devices, per_device(): rows = lax.all_gather(piece, ('y', 'z'), axis=0, tiled=True)  88.8 us
    all_to_all x2, waiting for transfers between devices, per_device(): lax.all_to_all(lines, ('y', 'z'), split_axis=0, concat_axis=0, tiled=True)  69.7 us
    dot_general x4, matrix products, expert_rows(): jnp.dot(activated, down_weight, preferred_element_type=jnp.float32)  28 us
    all_to_all x1, waiting for transfers between devices, per_device(): lax.all_to_all(blocks, ('x', 'y'), split_axis=0, concat_axis=0, tiled=True)  21.6 us
    all_to_all x2, starting transfers between devices, per_device(): lax.all_to_all(lines, ('y', 'z'), split_axis=0, concat_axis=0, tiled=True)  15.4 us
    dot_general x4, matrix products, expert_rows(): gate_part = jnp.dot(rows, gate_weight, preferred_element_type=jnp.float32)  13.5 us
    all_gather x1, blocking collectives, per_device(): gathered = lax.all_gather(both, ('z', 'c'), axis=1, tiled=True)  13 us
    unnamed x24, local copies, waits for them, and re-layouts  12.4 us
  transfers between devices with their start and end apart: 11, of which 6 were waited for; matrix products, arithmetic and copies ran while one was open for 20% of the time, Pallas kernels for 0%

profile of v3, /device:TPU:112, one launch (start us, length us, event | category | flops | bytes accessed | tf_op | source)
XLA Modules:
  0.0 364.5 jit_solution(13842777046743662879)
XLA Ops:
  6.6 1.0 reduce-window.8
  7.6 0.7 fusion.51
  8.3 1.9 fusion.6
  10.2 2.7 fusion.13
  13.8 1.3 collective-permute-start
  15.0 1.0 multiply_cosine_fusion
  16.1 4.4 %fusion.15 = f32[128,384]{0,1:T(8,128)S(1)} fusion(bf16[6144,384]{1,0:T(8,128)(2,1)} %param.11, bf16[128,6144]{1,0:T(8,128)(2,1)S(1)} %copy-done.1, f32[128]{0:T(128)S(1)} %add_rsqrt_fusion.1), kind=kOutput, calls=%fused_computation.33 | convolution fusion | flops 606339072 | bytes 6488576 | tf_op jit(solution)/shard_map/dot_general | solution.py:83
  21.3 1.0 copy.41
  22.3 1.6 subtract_convert_fusion
  24.1 0.8 select_bitcast_fusion.1
  24.9 13.0 %all_gather.9 = bf16[2,1024,128]{1,2,0:T(8,128)(2,1)} all-gather(bf16[2,128,128]{1,2,0:T(8,128)(2,1)S(1)} %pad_maximum_fusion.2), channel_id=1, replica_groups=mesh['z'=4,'c'=2,'x'=4,'y'=4] {'z','c'}, dimensions={1}, use_global_device_ids=true | all-gather | bytes 589824 | tf_op jit(solution)/shard_map/all_gather | solution.py:96
  37.9 2.0 fusion.70
  39.9 2.6 multiply_select_fusion
  42.5 2.5 fusion.9
  45.0 4.5 %fusion.3 = bf16[16,8,6144]{2,1,0:T(8,128)(2,1)} fusion(bf16[128,384]{0,1:T(8,128)(2,1)S(1)} %bitcast.69, bf16[384,6144]{1,0:T(8,128)(2,1)} %param.13), kind=kOutput, calls=%fused_computation.8 | convolution fusion | flops 604766208 | bytes 6389760 | tf_op jit(solution)/shard_map/dot_general | solution.py:117
  49.5 7.4 %all-to-all-start = ((bf16[16,8,6144]{2,1,0:T(8,128)(2,1)}), bf16[16,8,6144]{2,1,0:T(8,128)(2,1)}, u32[]{:S(2)}, u32[]{:S(2)}) async-start(bf16[16,8,6144]{2,1,0:T(8,128)(2,1)} %fusion.3), calls=%async_computation | async-start | bytes 3145728 | tf_op jit(solution)/shard_map/all_to_all | solution.py:120
  57.2 21.6 %all-to-all-done = bf16[16,8,6144]{2,1,0:T(8,128)(2,1)} async-done(((bf16[16,8,6144]{2,1,0:T(8,128)(2,1)}), bf16[16,8,6144]{2,1,0:T(8,128)(2,1)}, u32[]{:S(2)}, u32[]{:S(2)}) %all-to-all-start) | async-done | bytes 1572896 | tf_op jit(solution)/shard_map/all_to_all | solution.py:120
  78.8 1.6 convert_reduce_fusion.2
  80.5 1.1 multiply_reduce_fusion
  81.6 1.0 multiply_convert_fusion.2
  83.2 10.6 %all_to_all.25 = bf16[4,6,6144]{2,1,0:T(8,128)(2,1)S(1)} all-to-all(bf16[4,6,6144]{2,1,0:T(8,128)(2,1)S(1)} %convolution_convert_fusion.5), channel_id=1, replica_groups=mesh['z'=4,'c'=2,'x'=4,'y'=4] {'x'}, dimensions={0} | all-to-all | bytes 589824 | tf_op jit(solution)/shard_map/all_to_all | solution.py:143
  94.5 1.6 reshape.276
  96.2 0.7 reshape.278
  96.9 44.4 %all-gather.5.cloned.1.call-done = bf16[16,12,6144]{2,1,0:T(8,128)(2,1)} async-done(((bf16[1,12,6144]{2,1,0:T(8,128)(2,1)}), bf16[16,12,6144]{2,1,0:T(8,128)(2,1)}) %all-gather.5.cloned.1.call-update) | async-done | bytes 2359312 | tf_op jit(solution)/shard_map/all_gather | solution.py:150
  141.3 4.3 %reshape.277 = bf16[192,6144]{1,0:T(8,128)(2,1)} reshape(bf16[16,12,6144]{2,1,0:T(8,128)(2,1)} %all-gather.5.cloned.1.call-done) | data formatting | bytes 4718592
  145.6 44.5 %all-gather.7.cloned.1.call-done = bf16[16,12,6144]{2,1,0:T(8,128)(2,1)} async-done(((bf16[1,12,6144]{2,1,0:T(8,128)(2,1)}), bf16[16,12,6144]{2,1,0:T(8,128)(2,1)}) %all-gather.7.cloned.1.call-update) | async-done | bytes 2359312 | tf_op jit(solution)/shard_map/all_gather | solution.py:150
  190.1 4.3 %reshape.279 = bf16[192,6144]{1,0:T(8,128)(2,1)} reshape(bf16[16,12,6144]{2,1,0:T(8,128)(2,1)} %all-gather.7.cloned.1.call-done) | data formatting | bytes 4718592
  194.4 3.4 fusion.77
  197.8 6.6 %convolution_convert_fusion.2 = bf16[192,6144]{1,0:T(8,128)(2,1)} fusion(bf16[256,6144]{1,0:T(8,128)(2,1)S(1)} %copy-done, f32[192,256]{1,0:T(8,128)S(1)} %fusion.77, bf16[192,6144]{1,0:T(8,128)(2,1)} %collective-permute-done.1, bf16[6144,256]{1,0:T(8,128)(2,1)} %param.18), kind=kOutput, calls=%fused_computation.3 | convolution fusion | flops 1209434112 | bytes 11206656 | tf_op jit(solution)/shard_map/dot_general | solution.py:49
  204.9 3.4 fusion.79
  208.3 6.6 %convolution_convert_fusion = bf16[192,6144]{1,0:T(8,128)(2,1)} fusion(bf16[256,6144]{1,0:T(8,128)(2,1)S(1)} %copy-done, f32[192,256]{1,0:T(8,128)S(1)} %fusion.79, bf16[192,6144]{1,0:T(8,128)(2,1)} %collective-permute-done.3, bf16[6144,256]{1,0:T(8,128)(2,1)} %param.18), kind=kOutput, calls=%fused_computation.1 | convolution fusion | flops 1209434112 | bytes 11206656 | tf_op jit(solution)/shard_map/dot_general | solution.py:49
  215.0 3.4 fusion.76
  218.4 7.4 %add_convert_fusion.1 = bf16[192,6144]{1,0:T(8,128)(2,1)} fusion(bf16[192,6144]{1,0:T(8,128)(2,1)} %collective-permute-done.2, bf16[256,6144]{1,0:T(8,128)(2,1)S(1)} %copy-done, bf16[192,6144]{1,0:T(8,128)(2,1)} %reshape.277, bf16[6144,256]{1,0:T(8,128)(2,1)} %param.18, f32[192,256]{1,0:T(8,128)S(1)} %fusion.76), kind=kOutput, calls=%fused_computation.16 | convolution fusion | flops 1214152704 | bytes 13565952 | tf_op jit(solution)/shard_map/dot_general | solution.py:49
  225.7 4.3 %reshape.273 = bf16[16,12,6144]{2,1,0:T(8,128)(2,1)} reshape(bf16[192,6144]{1,0:T(8,128)(2,1)} %add_convert_fusion.1) | data formatting | bytes 4718592 | tf_op jit(solution)/shard_map/reshape | solution.py:156
  230.0 7.0 %all-to-all-start.2 = ((bf16[16,12,6144]{2,1,0:T(8,128)(2,1)}), bf16[16,12,6144]{2,1,0:T(8,128)(2,1)}, u32[]{:S(2)}, u32[]{:S(2)}) async-start(bf16[16,12,6144]{2,1,0:T(8,128)(2,1)} %reshape.273), calls=%async_computation.2 | async-start | bytes 6291456 | tf_op jit(solution)/shard_map/all_to_all | solution.py:157
  237.0 3.4 fusion.78
  240.4 7.4 %add_convert_fusion = bf16[192,6144]{1,0:T(8,128)(2,1)} fusion(bf16[192,6144]{1,0:T(8,128)(2,1)} %collective-permute-done.4, bf16[256,6144]{1,0:T(8,128)(2,1)S(1)} %copy-done, bf16[192,6144]{1,0:T(8,128)(2,1)} %reshape.279, bf16[6144,256]{1,0:T(8,128)(2,1)} %param.18, f32[192,256]{1,0:T(8,128)S(1)} %fusion.78), kind=kOutput, calls=%fused_computation.15 | convolution fusion | flops 1214152704 | bytes 13565952 | tf_op jit(solution)/shard_map/dot_general | solution.py:49
  247.7 4.3 %reshape.274 = bf16[16,12,6144]{2,1,0:T(8,128)(2,1)} reshape(bf16[192,6144]{1,0:T(8,128)(2,1)} %add_convert_fusion) | data formatting | bytes 4718592 | tf_op jit(solution)/shard_map/reshape | solution.py:156
  252.0 30.8 %all-to-all-done.2 = bf16[16,12,6144]{2,1,0:T(8,128)(2,1)} async-done(((bf16[16,12,6144]{2,1,0:T(8,128)(2,1)}), bf16[16,12,6144]{2,1,0:T(8,128)(2,1)}, u32[]{:S(2)}, u32[]{:S(2)}) %all-to-all-start.2) | async-done | bytes 2359328 | tf_op jit(solution)/shard_map/all_to_all | solution.py:157
  282.9 8.4 %all-to-all-start.3 = ((bf16[16,12,6144]{2,1,0:T(8,128)(2,1)}), bf16[16,12,6144]{2,1,0:T(8,128)(2,1)}, u32[]{:S(2)}, u32[]{:S(2)}) async-start(bf16[16,12,6144]{2,1,0:T(8,128)(2,1)} %reshape.274), calls=%async_computation.3 | async-start | bytes 6291456 | tf_op jit(solution)/shard_map/all_to_all | solution.py:157
  291.5 3.2 convert_reduce_fusion.1
  294.7 38.9 %all-to-all-done.3 = bf16[16,12,6144]{2,1,0:T(8,128)(2,1)} async-done(((bf16[16,12,6144]{2,1,0:T(8,128)(2,1)}), bf16[16,12,6144]{2,1,0:T(8,128)(2,1)}, u32[]{:S(2)}, u32[]{:S(2)}) %all-to-all-start.3) | async-done | bytes 2359328 | tf_op jit(solution)/shard_map/all_to_all | solution.py:157
  333.6 2.5 convert_reduce_fusion
  336.2 0.9 pad_maximum_fusion
  337.0 2.0 reshape.275
  339.0 4.2 %all-to-all-start.4 = ((f32[4,6,6144]{2,1,0:T(8,128)}), f32[4,6,6144]{2,1,0:T(8,128)}, u32[]{:S(2)}, u32[]{:S(2)}) async-start(f32[4,6,6144]{2,1,0:T(8,128)} %reshape.275), calls=%async_computation.4 | async-start | bytes 1572864 | tf_op jit(solution)/shard_map/all_to_all | solution.py:161
  343.3 11.0 %all-to-all-done.4 = f32[4,6,6144]{2,1,0:T(8,128)} async-done(((f32[4,6,6144]{2,1,0:T(8,128)}), f32[4,6,6144]{2,1,0:T(8,128)}, u32[]{:S(2)}, u32[]{:S(2)}) %all-to-all-start.4) | async-done | bytes 589856 | tf_op jit(solution)/shard_map/all_to_all | solution.py:161
  354.3 3.4 fusion.5
  (55 shorter events, 4.4 us)
Async XLA Ops:
  6.5 191.2 %copy-start = (bf16[256,6144]{1,0:T(8,128)(2,1)S(1)}, bf16[256,6144]{1,0:T(8,128)(2,1)}, u32[]{:S(2)}) copy-start(bf16[256,6144]{1,0:T(8,128)(2,1)} %param.19) | copy-start | bytes 9437188
  8.3 7.8 %copy-start.1 = (bf16[128,6144]{1,0:T(8,128)(2,1)S(1)}, bf16[128,6144]{1,0:T(8,128)(2,1)}, u32[]{:S(2)}) copy-start(bf16[128,6144]{1,0:T(8,128)(2,1)} %param.10) | copy-start | bytes 4718596
  13.8 10.3 %collective-permute-start = (bf16[128,128]{0,1:T(8,128)(2,1)}, bf16[128,128]{0,1:T(8,128)(2,1)}, u32[]{:S(2)}, u32[]{:S(2)}) collective-permute-start(bf16[128,128]{0,1:T(8,128)(2,1)} %fusion.34), channel_id=1, source_target_pairs={{0,1},{1,0},{2,3},{3,2},{4,5},{5,4},{6,7},{7,6},{8,9},{9,8},{10,11... | collective-permute-start | bytes 98312 | tf_op jit(solution)/shard_map/ppermute | solution.py:92
  24.9 15.0 %copy-start.3 = (bf16[128,3,64]{2,0,1:T(8,128)(2,1)S(1)}, bf16[128,3,64]{2,0,1:T(8,128)(2,1)}, u32[]{:S(2)}) copy-start(bf16[128,3,64]{2,0,1:T(8,128)(2,1)} %get-tuple-element.7) | copy-start | bytes 147460
  24.9 15.0 %copy-start.4 = (bf16[128,3,64]{2,0,1:T(8,128)(2,1)S(1)}, bf16[128,3,64]{2,0,1:T(8,128)(2,1)}, u32[]{:S(2)}) copy-start(bf16[128,3,64]{2,0,1:T(8,128)(2,1)} %get-tuple-element.8) | copy-start | bytes 147460
  49.5 7.5 %copy-start.7 = (s32[8,2]{0,1:T(2,128)S(1)}, s32[8,2]{0,1:T(2,128)}, u32[]{:S(2)}) copy-start(s32[8,2]{0,1:T(2,128)} %param.15) | copy-start | bytes 196
  49.5 29.3 %all-to-all-start = ((bf16[16,8,6144]{2,1,0:T(8,128)(2,1)}), bf16[16,8,6144]{2,1,0:T(8,128)(2,1)}, u32[]{:S(2)}, u32[]{:S(2)}) async-start(bf16[16,8,6144]{2,1,0:T(8,128)(2,1)} %fusion.3), calls=%async_computation | async-start | bytes 3145728 | tf_op jit(solution)/shard_map/all_to_all | solution.py:120
  56.9 84.3 %all-gather.5.cloned.1.call-start = ((), (), s32[]{:S(2)}) async-start(), calls=%async_computation.5 | async-start | bytes 3342336 | tf_op jit(solution)/shard_map/all_gather | solution.py:150
  82.5 0.6 copy-start.5
  96.1 94.0 %all-gather.7.cloned.1.call-start = ((), (), s32[]{:S(2)}) async-start(), calls=%async_computation.6 | async-start | bytes 3342336 | tf_op jit(solution)/shard_map/all_gather | solution.py:150
  145.6 48.8 %collective-permute-start.1 = (bf16[192,6144]{1,0:T(8,128)(2,1)}, bf16[192,6144]{1,0:T(8,128)(2,1)}, u32[]{:S(2)}, u32[]{:S(2)}) collective-permute-start(bf16[192,6144]{1,0:T(8,128)(2,1)} %reshape.277), channel_id=1, source_target_pairs={{0,16},{16,0},{1,17},{17,1},{2,18},{18,2},{3,19},{19,3},{4,20},{20... | collective-permute-start | bytes 7077896 | tf_op jit(solution)/shard_map/ppermute | solution.py:151
  194.4 10.6 %collective-permute-start.3 = (bf16[192,6144]{1,0:T(8,128)(2,1)}, bf16[192,6144]{1,0:T(8,128)(2,1)}, u32[]{:S(2)}, u32[]{:S(2)}) collective-permute-start(bf16[192,6144]{1,0:T(8,128)(2,1)} %reshape.279), channel_id=1, source_target_pairs={{0,16},{16,0},{1,17},{17,1},{2,18},{18,2},{3,19},{19,3},{4,20},{20... | collective-permute-start | bytes 7077896 | tf_op jit(solution)/shard_map/ppermute | solution.py:151
  204.4 13.9 %collective-permute-start.2 = (bf16[192,6144]{1,0:T(8,128)(2,1)}, bf16[192,6144]{1,0:T(8,128)(2,1)}, u32[]{:S(2)}, u32[]{:S(2)}) collective-permute-start(bf16[192,6144]{1,0:T(8,128)(2,1)} %convolution_convert_fusion.2), channel_id=1, source_target_pairs={{0,16},{16,0},{1,17},{17,1},{2,18},{18,2},{3,19},{19,3},{4,20},{20... | collective-permute-start | bytes 7077896 | tf_op jit(solution)/shard_map/ppermute | solution.py:154
  215.0 25.4 %collective-permute-start.4 = (bf16[192,6144]{1,0:T(8,128)(2,1)}, bf16[192,6144]{1,0:T(8,128)(2,1)}, u32[]{:S(2)}, u32[]{:S(2)}) collective-permute-start(bf16[192,6144]{1,0:T(8,128)(2,1)} %convolution_convert_fusion), channel_id=1, source_target_pairs={{0,16},{16,0},{1,17},{17,1},{2,18},{18,2},{3,19},{19,3},{4,20},{20... | collective-permute-start | bytes 7077896 | tf_op jit(solution)/shard_map/ppermute | solution.py:154
  230.0 52.9 %all-to-all-start.2 = ((bf16[16,12,6144]{2,1,0:T(8,128)(2,1)}), bf16[16,12,6144]{2,1,0:T(8,128)(2,1)}, u32[]{:S(2)}, u32[]{:S(2)}) async-start(bf16[16,12,6144]{2,1,0:T(8,128)(2,1)} %reshape.273), calls=%async_computation.2 | async-start | bytes 6291456 | tf_op jit(solution)/shard_map/all_to_all | solution.py:157
  252.0 39.2 %copy-start.6 = (bf16[8,6144]{1,0:T(8,128)(2,1)S(1)}, bf16[8,6144]{1,0:T(8,128)(2,1)}, u32[]{:S(2)}) copy-start(bf16[8,6144]{1,0:T(8,128)(2,1)} %copy-done.5) | copy-start | bytes 294916
  252.0 39.3 %copy-start.8 = (bf16[6144,4]{0,1:T(4,128)(2,1)S(1)}, bf16[6144,4]{0,1:T(4,128)(2,1)}, u32[]{:S(2)}) copy-start(bf16[6144,4]{0,1:T(4,128)(2,1)} %param.16) | copy-start | bytes 147460
  282.9 50.7 %all-to-all-start.3 = ((bf16[16,12,6144]{2,1,0:T(8,128)(2,1)}), bf16[16,12,6144]{2,1,0:T(8,128)(2,1)}, u32[]{:S(2)}, u32[]{:S(2)}) async-start(bf16[16,12,6144]{2,1,0:T(8,128)(2,1)} %reshape.274), calls=%async_computation.3 | async-start | bytes 6291456 | tf_op jit(solution)/shard_map/all_to_all | solution.py:157
  333.6 2.5 copy-start.2
  339.0 15.2 %all-to-all-start.4 = ((f32[4,6,6144]{2,1,0:T(8,128)}), f32[4,6,6144]{2,1,0:T(8,128)}, u32[]{:S(2)}, u32[]{:S(2)}) async-start(f32[4,6,6144]{2,1,0:T(8,128)} %reshape.275), calls=%async_computation.4 | async-start | bytes 1572864 | tf_op jit(solution)/shard_map/all_to_all | solution.py:161
Sparse Core Ops, SparseCore 0:
  96.2 44.9 all-gather.4
  143.5 46.5 all-gather.6

commit v4 on v2

--- a/solution.py
+++ b/solution.py
@@ -140,12 +140,14 @@
 
     arrived = lax.all_to_all(send, "x", split_axis=0, concat_axis=0, tiled=True)
     arrived = arrived.reshape(experts * capacity, model_width)
-    rows = lax.all_gather(arrived, ("y", "z"), axis=0, tiled=True)
+    rows = lax.all_gather(arrived, ("c", "y", "z"), axis=0, tiled=True)
+    line_rows = rows.shape[0] // nc
+    other_rows = lax.dynamic_slice_in_dim(rows, (1 - ci) * line_rows, line_rows, 0)
+    own_rows = lax.dynamic_slice_in_dim(rows, ci * line_rows, line_rows, 0)
     core_swap = [(i, i ^ 1) for i in range(nc)]
-    other_rows = lax.ppermute(rows, "c", core_swap)
-    own_out = expert_rows(rows, gate_weight, up_weight, down_weight)
     other_out = expert_rows(other_rows, gate_weight, up_weight, down_weight)
     other_back = lax.ppermute(other_out, "c", core_swap)
+    own_out = expert_rows(own_rows, gate_weight, up_weight, down_weight)
     summed = (own_out.astype(jnp.float32) + other_back.astype(jnp.float32)).astype(jnp.bfloat16)
 
     lines = summed.reshape(-1, experts * capacity, model_width)

time: 309 us -> 297 us (0.961)
  waiting for transfers between devices: 172 us -> 161 us
    ppermute x1 -> x0, waiting for transfers between devices: 8.12 us -> none  [per_device(): other_rows = lax.ppermute(rows, 'c', core_swap)]
    all_to_all x1, waiting for transfers between devices: 76 us -> 72.2 us  [per_device(): lax.all_to_all(lines, ('y', 'z'), split_axis=0, concat_axis=0, tiled=True)]
  transfers between devices with their start and end apart: 7 -> 6, of which waited for: 6 -> 5; matrix products, arithmetic and copies ran while one was open for 5% -> 5% of each run, Pallas kernels for 0% -> 0%
where the time goes in v4:
time: 297 us
  waiting for transfers between devices  161 us (54%)
  matrix products  55.9 us (19%)
  blocking collectives  23.6 us (8%)
  starting transfers between devices  20.9 us (7%)
  other arithmetic  16.1 us (5%)
  between operations  13.6 us (5%)
  local copies, waits for them, and re-layouts  5.66 us (2%)
    all_to_all x1, waiting for transfers between devices, per_device(): lax.all_to_all(lines, ('y', 'z'), split_axis=0, concat_axis=0, tiled=True)  72.2 us
    all_gather x1, waiting for transfers between devices, per_device(): rows = lax.all_gather(arrived, ('c', 'y', 'z'), axis=0, tiled=True)  52.9 us
    dot_general x2, matrix products, expert_rows(): jnp.dot(activated, down_weight, preferred_element_type=jnp.float32)  22.5 us
    all_to_all x1, waiting for transfers between devices, per_device(): lax.all_to_all(blocks, ('x', 'y'), split_axis=0, concat_axis=0, tiled=True)  21.6 us
    all_gather x1, blocking collectives, per_device(): gathered = lax.all_gather(both, ('z', 'c'), axis=1, tiled=True)  12.9 us
    all_to_all x1, waiting for transfers between devices, per_device(): lax.all_to_all(summed, 'x', split_axis=0, concat_axis=0, tiled=True)  11.6 us
    dot_general x2, matrix products, expert_rows(): gate_part = jnp.dot(rows, gate_weight, preferred_element_type=jnp.float32)  10.9 us
    all_to_all x1, blocking collectives, per_device(): arrived = lax.all_to_all(send, 'x', split_axis=0, concat_axis=0, tiled=True)  10.7 us
  transfers between devices with their start and end apart: 6, of which 5 were waited for; matrix products, arithmetic and copies ran while one was open for 5% of the time, Pallas kernels for 0%

profile of v4, /device:TPU:112, one launch (start us, length us, event | category | flops | bytes accessed | tf_op | source)
XLA Modules:
  0.0 296.6 jit_solution(7345001094900425947)
XLA Ops:
  6.6 1.0 reduce-window.8
  7.6 1.9 fusion.12
  9.5 0.7 fusion.69
  10.3 2.7 fusion.31
  12.9 0.2 fusion.57
  13.1 0.6 fusion.52
  13.8 1.3 collective-permute-start
  15.0 0.1 convert_reduce_fusion.2
  15.1 1.0 multiply_cosine_fusion
  16.1 4.4 %fusion.33 = f32[128,384]{0,1:T(8,128)S(1)} fusion(bf16[6144,384]{1,0:T(8,128)(2,1)} %param.11, bf16[128,6144]{1,0:T(8,128)(2,1)S(1)} %copy-done.1, f32[128]{0:T(128)S(1)} %add_rsqrt_fusion.1), kind=kOutput, calls=%fused_computation.35 | convolution fusion | flops 606339072 | bytes 6488576 | tf_op jit(solution)/shard_map/dot_general | solution.py:81
  20.5 0.7 fusion.90
  21.1 0.1 copy.34
  21.2 1.0 copy.33
  22.3 1.6 subtract_convert_fusion
  23.9 0.2 fusion.37
  24.1 0.0 collective-permute-done
  24.1 0.8 select_bitcast_fusion.1
  24.9 12.9 %all_gather.6 = bf16[2,1024,128]{1,2,0:T(8,128)(2,1)} all-gather(bf16[2,128,128]{1,2,0:T(8,128)(2,1)S(1)} %pad_maximum_fusion.1), channel_id=1, replica_groups=mesh['z'=4,'c'=2,'x'=4,'y'=4] {'z','c'}, dimensions={1}, use_global_device_ids=true | all-gather | bytes 589824 | tf_op jit(solution)/shard_map/all_gather | solution.py:94
  37.8 2.0 fusion.91
  39.8 2.6 multiply_select_fusion
  42.3 2.5 fusion.29
  44.9 4.5 %fusion.1 = bf16[16,8,6144]{2,1,0:T(8,128)(2,1)} fusion(bf16[128,384]{0,1:T(8,128)(2,1)S(1)} %bitcast.57, bf16[384,6144]{1,0:T(8,128)(2,1)} %param.13), kind=kOutput, calls=%fused_computation.6 | convolution fusion | flops 604766208 | bytes 6389760 | tf_op jit(solution)/shard_map/dot_general | solution.py:115
  49.4 7.4 %all-to-all-start = ((bf16[16,8,6144]{2,1,0:T(8,128)(2,1)}), bf16[16,8,6144]{2,1,0:T(8,128)(2,1)}, u32[]{:S(2)}, u32[]{:S(2)}) async-start(bf16[16,8,6144]{2,1,0:T(8,128)(2,1)} %fusion.1), calls=%async_computation | async-start | bytes 3145728 | tf_op jit(solution)/shard_map/all_to_all | solution.py:118
  56.8 0.0 all-gather.2.cloned.1.call-start
  56.9 0.2 reduce_window_sum.19
  57.1 21.6 %all-to-all-done = bf16[16,8,6144]{2,1,0:T(8,128)(2,1)} async-done(((bf16[16,8,6144]{2,1,0:T(8,128)(2,1)}), bf16[16,8,6144]{2,1,0:T(8,128)(2,1)}, u32[]{:S(2)}, u32[]{:S(2)}) %all-to-all-start) | async-done | bytes 1572896 | tf_op jit(solution)/shard_map/all_to_all | solution.py:118
  78.7 1.6 convert_reduce_fusion.1
  80.3 1.1 multiply_reduce_fusion
  81.4 1.0 multiply_convert_fusion
  82.4 0.4 convolution_convert_fusion.3
  82.7 10.7 %all_to_all.20 = bf16[4,6,6144]{2,1,0:T(8,128)(2,1)} all-to-all(bf16[4,6,6144]{2,1,0:T(8,128)(2,1)S(1)} %convolution_convert_fusion.3), channel_id=1, replica_groups=mesh['z'=4,'c'=2,'x'=4,'y'=4] {'x'}, dimensions={0} | all-to-all | bytes 589824 | tf_op jit(solution)/shard_map/all_to_all | solution.py:141
  93.4 1.8 reshape.270
  95.3 0.0 all-gather.2.cloned.1.call-update
  95.3 52.9 %all-gather.2.cloned.1.call-done = bf16[768,6144]{1,0:T(8,128)(2,1)} async-done(((bf16[24,6144]{1,0:T(8,128)(2,1)}), bf16[768,6144]{1,0:T(8,128)(2,1)}) %all-gather.2.cloned.1.call-update) | async-done | bytes 9437200 | tf_op jit(solution)/shard_map/all_gather | solution.py:143
  148.2 5.5 %fusion.6 = f32[384,256]{1,0:T(8,128)} fusion(bf16[6144,256]{1,0:T(8,128)(2,1)} %param.17, bf16[768,6144]{1,0:T(8,128)(2,1)} %all-gather.2.cloned.1.call-done, s32[]{:T(128)S(6)} %select_n.65), kind=kOutput, calls=%fused_computation.13 | convolution fusion | flops 1207959552 | bytes 8257540 | tf_op jit(solution)/shard_map/dot_general | solution.py:44
  153.7 10.5 %convolution_convert_fusion = bf16[384,6144]{1,0:T(8,128)(2,1)} fusion(bf16[256,6144]{1,0:T(8,128)(2,1)S(1)} %copy-done, bf16[6144,256]{1,0:T(8,128)(2,1)} %param.18, bf16[768,6144]{1,0:T(8,128)(2,1)} %all-gather.2.cloned.1.call-done, s32[]{:T(128)S(6)} %select_n.65, f32[384,256]{1,0:T(8,128)} %fusion.6), kind=kOutput, calls=%fused_computation.3 | convolution fusion | flops 2418868224 | bytes 16121860 | tf_op jit(solution)/shard_map/dot_general | solution.py:47
  164.2 0.2 collective-permute-start.1
  164.4 5.5 %fusion.10 = f32[384,256]{1,0:T(8,128)} fusion(bf16[6144,256]{1,0:T(8,128)(2,1)} %param.17, bf16[768,6144]{1,0:T(8,128)(2,1)} %all-gather.2.cloned.1.call-done, s32[]{:T(128)S(6)} %select_n.64), kind=kOutput, calls=%fused_computation.17 | convolution fusion | flops 1207959552 | bytes 8257540 | tf_op jit(solution)/shard_map/dot_general | solution.py:44
  169.9 2.6 collective-permute-done.1
  172.4 12.0 %add_convert_fusion = bf16[384,6144]{1,0:T(8,128)(2,1)} fusion(bf16[384,6144]{1,0:T(8,128)(2,1)} %collective-permute-done.1, bf16[256,6144]{1,0:T(8,128)(2,1)S(1)} %copy-done, bf16[6144,256]{1,0:T(8,128)(2,1)} %param.18, bf16[768,6144]{1,0:T(8,128)(2,1)} %all-gather.2.cloned.1.call-done, s32[]{:T(128)S(6)} %select_n.64, f32[384,256]{1,0:T(8,128)} %fusion.10), kind=kOutput, calls=%fused_computation.2 | convolution fusion | flops 2428305408 | bytes 20840452 | tf_op jit(solution)/shard_map/dot_general | solution.py:47
  184.4 7.5 %all-to-all-start.2 = ((bf16[16,24,6144]{2,1,0:T(8,128)(2,1)}), bf16[16,24,6144]{2,1,0:T(8,128)(2,1)}, u32[]{:S(2)}, u32[]{:S(2)}) async-start(bf16[16,24,6144]{2,1,0:T(8,128)(2,1)} %bitcast.54), calls=%async_computation.2 | async-start | bytes 9437184 | tf_op jit(solution)/shard_map/all_to_all | solution.py:155
  191.9 0.2 fusion.92
  192.1 72.2 %all-to-all-done.2 = bf16[16,24,6144]{2,1,0:T(8,128)(2,1)} async-done(((bf16[16,24,6144]{2,1,0:T(8,128)(2,1)}), bf16[16,24,6144]{2,1,0:T(8,128)(2,1)}, u32[]{:S(2)}, u32[]{:S(2)}) %all-to-all-start.2) | async-done | bytes 4718624 | tf_op jit(solution)/shard_map/all_to_all | solution.py:155
  264.3 4.0 %convert_reduce_fusion = f32[24,6144]{1,0:T(8,128)} fusion(bf16[16,24,6144]{2,1,0:T(8,128)(2,1)} %all-to-all-done.2), kind=kLoop, calls=%fused_computation.1 | loop fusion | flops 4571136 | bytes 5308416 | tf_op jit(solution)/shard_map/reduce_sum | solution.py:154
  268.3 2.0 reshape.272
  270.3 4.4 %all-to-all-start.3 = ((f32[4,6,6144]{2,1,0:T(8,128)}), f32[4,6,6144]{2,1,0:T(8,128)}, u32[]{:S(2)}, u32[]{:S(2)}) async-start(f32[4,6,6144]{2,1,0:T(8,128)} %reshape.272), calls=%async_computation.3 | async-start | bytes 1572864 | tf_op jit(solution)/shard_map/all_to_all | solution.py:161
  274.8 11.6 %all-to-all-done.3 = f32[4,6,6144]{2,1,0:T(8,128)} async-done(((f32[4,6,6144]{2,1,0:T(8,128)}), f32[4,6,6144]{2,1,0:T(8,128)}, u32[]{:S(2)}, u32[]{:S(2)}) %all-to-all-start.3) | async-done | bytes 589856 | tf_op jit(solution)/shard_map/all_to_all | solution.py:161
  286.4 3.4 %fusion.3 = bf16[8,6144]{1,0:T(8,128)(2,1)} fusion(f32[4,6,6144]{2,1,0:T(8,128)} %all-to-all-done.3, f32[8,6144]{1,0:T(8,128)S(1)} %convert_reduce_fusion.1, bf16[128,6144]{1,0:T(8,128)(2,1)} %param.10, s32[]{:T(128)S(6)} %select_n.53, f32[8,4]{0,1:T(4,128)S(1)} %select_reduce_fusion, s32[8,4]{0,1:T(4,128)S(1)} %convert_subtract_fusion, ...), kind=kOutput, calls=%fused_computation.10 | convolution fusion | flops 14352960 | bytes 983332 | tf_op jit(solution)/shard_map/rec,ecd->rd/dot_general | solution.py:164
  (26 shorter events, 0.2 us)
Async XLA Ops:
  6.5 147.2 %copy-start = (bf16[256,6144]{1,0:T(8,128)(2,1)S(1)}, bf16[256,6144]{1,0:T(8,128)(2,1)}, u32[]{:S(2)}) copy-start(bf16[256,6144]{1,0:T(8,128)(2,1)} %param.19) | copy-start | bytes 9437188
  7.6 8.5 %copy-start.1 = (bf16[128,6144]{1,0:T(8,128)(2,1)S(1)}, bf16[128,6144]{1,0:T(8,128)(2,1)}, u32[]{:S(2)}) copy-start(bf16[128,6144]{1,0:T(8,128)(2,1)} %param.10) | copy-start | bytes 4718596
  13.8 10.3 %collective-permute-start = (bf16[128,128]{0,1:T(8,128)(2,1)}, bf16[128,128]{0,1:T(8,128)(2,1)}, u32[]{:S(2)}, u32[]{:S(2)}) collective-permute-start(bf16[128,128]{0,1:T(8,128)(2,1)} %fusion.52), channel_id=1, source_target_pairs={{0,1},{1,0},{2,3},{3,2},{4,5},{5,4},{6,7},{7,6},{8,9},{9,8},{10,11... | collective-permute-start | bytes 98312 | tf_op jit(solution)/shard_map/ppermute | solution.py:90
  23.9 15.9 %copy-start.2 = (bf16[128,3,64]{2,0,1:T(8,128)(2,1)S(1)}, bf16[128,3,64]{2,0,1:T(8,128)(2,1)}, u32[]{:S(2)}) copy-start(bf16[128,3,64]{2,0,1:T(8,128)(2,1)} %get-tuple-element.7) | copy-start | bytes 147460
  23.9 15.9 %copy-start.3 = (bf16[128,3,64]{2,0,1:T(8,128)(2,1)S(1)}, bf16[128,3,64]{2,0,1:T(8,128)(2,1)}, u32[]{:S(2)}) copy-start(bf16[128,3,64]{2,0,1:T(8,128)(2,1)} %get-tuple-element.8) | copy-start | bytes 147460
  49.4 7.5 %copy-start.4 = (s32[8,2]{0,1:T(2,128)S(1)}, s32[8,2]{0,1:T(2,128)}, u32[]{:S(2)}) copy-start(s32[8,2]{0,1:T(2,128)} %param.15) | copy-start | bytes 196
  49.4 29.3 %all-to-all-start = ((bf16[16,8,6144]{2,1,0:T(8,128)(2,1)}), bf16[16,8,6144]{2,1,0:T(8,128)(2,1)}, u32[]{:S(2)}, u32[]{:S(2)}) async-start(bf16[16,8,6144]{2,1,0:T(8,128)(2,1)} %fusion.1), calls=%async_computation | async-start | bytes 3145728 | tf_op jit(solution)/shard_map/all_to_all | solution.py:118
  56.8 91.5 %all-gather.2.cloned.1.call-start = ((), (), s32[]{:S(2)}) async-start(), calls=%async_computation.4 | async-start | bytes 9732096 | tf_op jit(solution)/shard_map/all_gather | solution.py:143
  164.2 8.3 %collective-permute-start.1 = (bf16[384,6144]{1,0:T(8,128)(2,1)}, bf16[384,6144]{1,0:T(8,128)(2,1)}, u32[]{:S(2)}, u32[]{:S(2)}) collective-permute-start(bf16[384,6144]{1,0:T(8,128)(2,1)} %convolution_convert_fusion), channel_id=1, source_target_pairs={{0,16},{16,0},{1,17},{17,1},{2,18},{18,2},{3,19},{19,3},{4,20},{20... | collective-permute-start | bytes 14155784 | tf_op jit(solution)/shard_map/ppermute | solution.py:149
  184.4 7.5 %copy-start.5 = (bf16[6144,4]{0,1:T(4,128)(2,1)S(1)}, bf16[6144,4]{0,1:T(4,128)(2,1)}, u32[]{:S(2)}) copy-start(bf16[6144,4]{0,1:T(4,128)(2,1)} %param.16) | copy-start | bytes 147460
  184.4 79.9 %all-to-all-start.2 = ((bf16[16,24,6144]{2,1,0:T(8,128)(2,1)}), bf16[16,24,6144]{2,1,0:T(8,128)(2,1)}, u32[]{:S(2)}, u32[]{:S(2)}) async-start(bf16[16,24,6144]{2,1,0:T(8,128)(2,1)} %bitcast.54), calls=%async_computation.2 | async-start | bytes 9437184 | tf_op jit(solution)/shard_map/all_to_all | solution.py:155
  270.3 16.0 %all-to-all-start.3 = ((f32[4,6,6144]{2,1,0:T(8,128)}), f32[4,6,6144]{2,1,0:T(8,128)}, u32[]{:S(2)}, u32[]{:S(2)}) async-start(f32[4,6,6144]{2,1,0:T(8,128)} %reshape.272), calls=%async_computation.3 | async-start | bytes 1572864 | tf_op jit(solution)/shard_map/all_to_all | solution.py:161
Sparse Core Ops, SparseCore 0:
  95.4 52.7 all-gather.1

commit v5 on v4

--- a/solution.py
+++ b/solution.py
@@ -43,7 +43,7 @@
 def expert_rows(rows, gate_weight, up_weight, down_weight):
     gate_part = jnp.dot(rows, gate_weight, preferred_element_type=jnp.float32)
     up_part = jnp.dot(rows, up_weight, preferred_element_type=jnp.float32)
-    activated = (jax.nn.silu(gate_part) * up_part).astype(jnp.bfloat16)
+    activated = lax.optimization_barrier((jax.nn.silu(gate_part) * up_part).astype(jnp.bfloat16))
     return jnp.dot(activated, down_weight, preferred_element_type=jnp.float32).astype(jnp.bfloat16)
 
 
@@ -157,12 +157,12 @@
         ),
         axis=0,
     )
-    summed = summed.reshape(experts, capacity, model_width)
+    summed = summed.reshape(experts, capacity, model_width).astype(jnp.bfloat16)
     returned = lax.all_to_all(summed, "x", split_axis=0, concat_axis=0, tiled=True)
 
     weights = jnp.where(hits, gate_cols[:, :, None], 0.0)
     moe = jnp.einsum(
-        "rec,ecd->rd", weights, returned, precision=lax.Precision.HIGHEST
+        "rec,ecd->rd", weights, returned.astype(jnp.float32), precision=lax.Precision.HIGHEST
     )
     return (hidden_state + moe).astype(jnp.bfloat16)
 

time: 297 us -> 283 us (0.953)
  matrix products: 55.9 us -> 48.4 us
  waiting for transfers between devices: 161 us -> 154 us
    dot_general x2, matrix products: 22.5 us -> 9.53 us  [expert_rows(): jnp.dot(activated, down_weight, preferred_element_type=jnp.float32)]
    dot_general x1 -> x3, matrix products: 3.39 us -> 10.1 us  [the longest x2 7.52 us: expert_rows(): up_part = jnp.dot(rows, up_weight, preferred_element_type=jnp.float32)]
    all_to_all x1, waiting for transfers between devices: 11.6 us -> 7.51 us  [per_device(): lax.all_to_all(summed, 'x', split_axis=0, concat_axis=0, tiled=True)]
  transfers between devices with their start and end apart: 6 -> 6, of which waited for: 5 -> 4; matrix products, arithmetic and copies ran while one was open for 5% -> 6% of each run, Pallas kernels for 0% -> 0%
where the time goes in v5:
time: 283 us; the launch traced here: 282 us
  waiting for transfers between devices  154 us (54%)
  matrix products  48.4 us (17%)
  blocking collectives  23.6 us (8%)
  starting transfers between devices  20.7 us (7%)
  other arithmetic  16 us (6%)
  between operations  13.6 us (5%)
  local copies, waits for them, and re-layouts  5.46 us (2%)
    all_to_all x1, waiting for transfers between devices, per_device(): lax.all_to_all(lines, ('y', 'z'), split_axis=0, concat_axis=0, tiled=True)  72 us
    all_gather x1, waiting for transfers between devices, per_device(): rows = lax.all_gather(arrived, ('c', 'y', 'z'), axis=0, tiled=True)  52.9 us
    all_to_all x1, waiting for transfers between devices, per_device(): lax.all_to_all(blocks, ('x', 'y'), split_axis=0, concat_axis=0, tiled=True)  21.6 us
    all_gather x1, blocking collectives, per_device(): gathered = lax.all_gather(both, ('z', 'c'), axis=1, tiled=True)  12.9 us
    all_to_all x1, blocking collectives, per_device(): arrived = lax.all_to_all(send, 'x', split_axis=0, concat_axis=0, tiled=True)  10.7 us
    dot_general x2, matrix products, expert_rows(): gate_part = jnp.dot(rows, gate_weight, preferred_element_type=jnp.float32)  9.68 us
    dot_general x2, matrix products, expert_rows(): jnp.dot(activated, down_weight, preferred_element_type=jnp.float32)  9.53 us
    dot_general x2, matrix products, expert_rows(): up_part = jnp.dot(rows, up_weight, preferred_element_type=jnp.float32)  7.52 us
  transfers between devices with their start and end apart: 6, of which 4 were waited for; matrix products, arithmetic and copies ran while one was open for 6% of the time, Pallas kernels for 0%

profile of v5, /device:TPU:112, one launch (start us, length us, event | category | flops | bytes accessed | tf_op | source)
XLA Modules:
  0.0 281.9 jit_solution(9201397432409863038)
XLA Ops:
  6.6 1.0 reduce-window.8
  7.6 1.9 fusion.12
  9.5 0.7 fusion.53
  10.3 2.7 fusion.29
  12.9 0.2 fusion.41
  13.1 0.6 fusion.36
  13.8 1.3 collective-permute-start
  15.0 0.1 convert_reduce_fusion.1
  15.1 1.0 multiply_cosine_fusion
  16.1 4.4 %fusion.31 = f32[128,384]{0,1:T(8,128)S(1)} fusion(bf16[6144,384]{1,0:T(8,128)(2,1)} %param.11, bf16[128,6144]{1,0:T(8,128)(2,1)S(1)} %copy-done.1, f32[128]{0:T(128)S(1)} %add_rsqrt_fusion.1), kind=kOutput, calls=%fused_computation.34 | convolution fusion | flops 606339072 | bytes 6488576 | tf_op jit(solution)/shard_map/dot_general | solution.py:81
  20.5 0.7 fusion.70
  21.1 0.1 copy.34
  21.2 1.0 copy.33
  22.3 1.6 subtract_convert_fusion
  23.9 0.2 fusion.33
  24.1 0.8 select_bitcast_fusion.1
  24.9 12.9 %all_gather.6 = bf16[2,1024,128]{1,2,0:T(8,128)(2,1)} all-gather(bf16[2,128,128]{1,2,0:T(8,128)(2,1)S(1)} %pad_maximum_fusion.1), channel_id=1, replica_groups=mesh['z'=4,'c'=2,'x'=4,'y'=4] {'z','c'}, dimensions={1}, use_global_device_ids=true | all-gather | bytes 589824 | tf_op jit(solution)/shard_map/all_gather | solution.py:94
  37.8 2.0 fusion.71
  39.8 2.6 multiply_select_fusion
  42.3 2.5 fusion.27
  44.9 4.5 %fusion.1 = bf16[16,8,6144]{2,1,0:T(8,128)(2,1)} fusion(bf16[128,384]{0,1:T(8,128)(2,1)S(1)} %bitcast.59, bf16[384,6144]{1,0:T(8,128)(2,1)} %param.13), kind=kOutput, calls=%fused_computation.5 | convolution fusion | flops 604766208 | bytes 6389760 | tf_op jit(solution)/shard_map/dot_general | solution.py:115
  49.4 7.4 %all-to-all-start = ((bf16[16,8,6144]{2,1,0:T(8,128)(2,1)}), bf16[16,8,6144]{2,1,0:T(8,128)(2,1)}, u32[]{:S(2)}, u32[]{:S(2)}) async-start(bf16[16,8,6144]{2,1,0:T(8,128)(2,1)} %fusion.1), calls=%async_computation | async-start | bytes 3145728 | tf_op jit(solution)/shard_map/all_to_all | solution.py:118
  56.8 0.0 all-gather.2.cloned.1.call-start
  56.9 0.2 reduce_window_sum.19
  57.1 21.6 %all-to-all-done = bf16[16,8,6144]{2,1,0:T(8,128)(2,1)} async-done(((bf16[16,8,6144]{2,1,0:T(8,128)(2,1)}), bf16[16,8,6144]{2,1,0:T(8,128)(2,1)}, u32[]{:S(2)}, u32[]{:S(2)}) %all-to-all-start) | async-done | bytes 1572896 | tf_op jit(solution)/shard_map/all_to_all | solution.py:118
  78.7 1.6 convert_reduce_fusion
  80.3 1.1 multiply_reduce_fusion
  81.4 1.0 multiply_convert_fusion
  82.4 0.4 convolution_convert_fusion.3
  82.7 10.7 %all_to_all.20 = bf16[4,6,6144]{2,1,0:T(8,128)(2,1)} all-to-all(bf16[4,6,6144]{2,1,0:T(8,128)(2,1)S(1)} %convolution_convert_fusion.3), channel_id=1, replica_groups=mesh['z'=4,'c'=2,'x'=4,'y'=4] {'x'}, dimensions={0} | all-to-all | bytes 589824 | tf_op jit(solution)/shard_map/all_to_all | solution.py:141
  93.4 1.8 reshape.269
  95.3 0.0 all-gather.2.cloned.1.call-update
  95.3 52.9 %all-gather.2.cloned.1.call-done = bf16[768,6144]{1,0:T(8,128)(2,1)} async-done(((bf16[24,6144]{1,0:T(8,128)(2,1)}), bf16[768,6144]{1,0:T(8,128)(2,1)}) %all-gather.2.cloned.1.call-update) | async-done | bytes 9437200 | tf_op jit(solution)/shard_map/all_gather | solution.py:143
  148.2 4.8 %fusion.6 = f32[384,256]{1,0:T(8,128)S(1)} fusion(bf16[6144,256]{1,0:T(8,128)(2,1)} %param.17, bf16[768,6144]{1,0:T(8,128)(2,1)} %all-gather.2.cloned.1.call-done, s32[]{:T(128)S(6)} %select_n.65), kind=kOutput, calls=%fused_computation.12 | convolution fusion | flops 1207959552 | bytes 8257540 | tf_op jit(solution)/shard_map/dot_general | solution.py:44
  153.1 3.8 %fusion.21 = bf16[384,256]{1,0:T(8,128)(2,1)S(1)} fusion(bf16[6144,256]{1,0:T(8,128)(2,1)S(1)} %copy-done.5, bf16[768,6144]{1,0:T(8,128)(2,1)} %all-gather.2.cloned.1.call-done, s32[]{:T(128)S(6)} %select_n.65, f32[384,256]{1,0:T(8,128)S(1)} %fusion.6), kind=kOutput, calls=%fused_computation.28 | convolution fusion | flops 1208549376 | bytes 8454148 | tf_op jit(solution)/shard_map/dot_general | solution.py:45
  156.9 3.5 %convolution_convert_fusion = bf16[384,6144]{1,0:T(8,128)(2,1)} fusion(bf16[384,256]{1,0:T(8,128)(2,1)S(1)} %fusion.21, bf16[256,6144]{1,0:T(8,128)(2,1)S(1)} %copy-done), kind=kOutput, calls=%fused_computation.2 | convolution fusion | flops 1210318848 | bytes 8060928 | tf_op jit(solution)/shard_map/dot_general | solution.py:47
  160.4 0.2 collective-permute-start.1
  160.6 4.8 %fusion.10 = f32[384,256]{1,0:T(8,128)S(1)} fusion(bf16[6144,256]{1,0:T(8,128)(2,1)} %param.17, bf16[768,6144]{1,0:T(8,128)(2,1)} %all-gather.2.cloned.1.call-done, s32[]{:T(128)S(6)} %select_n.64), kind=kOutput, calls=%fused_computation.16 | convolution fusion | flops 1207959552 | bytes 8257540 | tf_op jit(solution)/shard_map/dot_general | solution.py:44
  165.5 3.8 %fusion.24 = bf16[384,256]{1,0:T(8,128)(2,1)S(1)} fusion(bf16[6144,256]{1,0:T(8,128)(2,1)S(1)} %copy-done.6, bf16[768,6144]{1,0:T(8,128)(2,1)} %all-gather.2.cloned.1.call-done, s32[]{:T(128)S(6)} %select_n.64, f32[384,256]{1,0:T(8,128)S(1)} %fusion.10), kind=kOutput, calls=%fused_computation.29 | convolution fusion | flops 1208549376 | bytes 8454148 | tf_op jit(solution)/shard_map/dot_general | solution.py:45
  169.3 6.0 %add_convert_fusion = bf16[384,6144]{1,0:T(8,128)(2,1)} fusion(bf16[384,6144]{1,0:T(8,128)(2,1)} %collective-permute-done.1, bf16[384,256]{1,0:T(8,128)(2,1)S(1)} %fusion.24, bf16[256,6144]{1,0:T(8,128)(2,1)S(1)} %copy-done), kind=kOutput, calls=%fused_computation.1 | convolution fusion | flops 1219756032 | bytes 12779520 | tf_op jit(solution)/shard_map/dot_general | solution.py:47
  175.3 7.5 %all-to-all-start.2 = ((bf16[16,24,6144]{2,1,0:T(8,128)(2,1)}), bf16[16,24,6144]{2,1,0:T(8,128)(2,1)}, u32[]{:S(2)}, u32[]{:S(2)}) async-start(bf16[16,24,6144]{2,1,0:T(8,128)(2,1)} %bitcast.56), calls=%async_computation.2 | async-start | bytes 9437184 | tf_op jit(solution)/shard_map/all_to_all | solution.py:155
  182.8 0.2 fusion.72
  183.1 72.0 %all-to-all-done.2 = bf16[16,24,6144]{2,1,0:T(8,128)(2,1)} async-done(((bf16[16,24,6144]{2,1,0:T(8,128)(2,1)}), bf16[16,24,6144]{2,1,0:T(8,128)(2,1)}, u32[]{:S(2)}, u32[]{:S(2)}) %all-to-all-start.2) | async-done | bytes 4718624 | tf_op jit(solution)/shard_map/all_to_all | solution.py:155
  255.0 3.9 %reduce_sum.112 = bf16[24,6144]{1,0:T(8,128)(2,1)} reduce(bf16[16,24,6144]{2,1,0:T(8,128)(2,1)} %all-to-all-done.2, bf16[]{:T(256)} %constant.82.clone.1), dimensions={0}, to_apply=%region_15.16 | reduce | flops 2211840 | bytes 5013506 | tf_op jit(solution)/shard_map/reduce_sum | solution.py:154
  258.9 1.8 convert_element_type.111
  260.7 4.2 %all-to-all-start.3 = ((bf16[4,6,6144]{2,1,0:T(8,128)(2,1)}), bf16[4,6,6144]{2,1,0:T(8,128)(2,1)}, u32[]{:S(2)}, u32[]{:S(2)}) async-start(bf16[4,6,6144]{2,1,0:T(8,128)(2,1)} %convert_element_type.111), calls=%async_computation.3 | async-start | bytes 786432 | tf_op jit(solution)/shard_map/all_to_all | solution.py:161
  265.0 7.5 %all-to-all-done.3 = bf16[4,6,6144]{2,1,0:T(8,128)(2,1)} async-done(((bf16[4,6,6144]{2,1,0:T(8,128)(2,1)}), bf16[4,6,6144]{2,1,0:T(8,128)(2,1)}, u32[]{:S(2)}, u32[]{:S(2)}) %all-to-all-start.3) | async-done | bytes 294944 | tf_op jit(solution)/shard_map/all_to_all | solution.py:161
  272.5 2.6 fusion.3
  (32 shorter events, 0.2 us)
Async XLA Ops:
  6.5 150.3 %copy-start = (bf16[256,6144]{1,0:T(8,128)(2,1)S(1)}, bf16[256,6144]{1,0:T(8,128)(2,1)}, u32[]{:S(2)}) copy-start(bf16[256,6144]{1,0:T(8,128)(2,1)} %param.19) | copy-start | bytes 9437188
  7.6 8.5 %copy-start.1 = (bf16[128,6144]{1,0:T(8,128)(2,1)S(1)}, bf16[128,6144]{1,0:T(8,128)(2,1)}, u32[]{:S(2)}) copy-start(bf16[128,6144]{1,0:T(8,128)(2,1)} %param.10) | copy-start | bytes 4718596
  13.8 10.3 %collective-permute-start = (bf16[128,128]{0,1:T(8,128)(2,1)}, bf16[128,128]{0,1:T(8,128)(2,1)}, u32[]{:S(2)}, u32[]{:S(2)}) collective-permute-start(bf16[128,128]{0,1:T(8,128)(2,1)} %fusion.36), channel_id=1, source_target_pairs={{0,1},{1,0},{2,3},{3,2},{4,5},{5,4},{6,7},{7,6},{8,9},{9,8},{10,11... | collective-permute-start | bytes 98312 | tf_op jit(solution)/shard_map/ppermute | solution.py:90
  23.9 15.9 %copy-start.2 = (bf16[128,3,64]{2,0,1:T(8,128)(2,1)S(1)}, bf16[128,3,64]{2,0,1:T(8,128)(2,1)}, u32[]{:S(2)}) copy-start(bf16[128,3,64]{2,0,1:T(8,128)(2,1)} %get-tuple-element.7) | copy-start | bytes 147460
  23.9 15.9 %copy-start.3 = (bf16[128,3,64]{2,0,1:T(8,128)(2,1)S(1)}, bf16[128,3,64]{2,0,1:T(8,128)(2,1)}, u32[]{:S(2)}) copy-start(bf16[128,3,64]{2,0,1:T(8,128)(2,1)} %get-tuple-element.8) | copy-start | bytes 147460
  49.4 7.5 %copy-start.4 = (s32[8,2]{0,1:T(2,128)S(1)}, s32[8,2]{0,1:T(2,128)}, u32[]{:S(2)}) copy-start(s32[8,2]{0,1:T(2,128)} %param.15) | copy-start | bytes 196
  49.4 29.3 %all-to-all-start = ((bf16[16,8,6144]{2,1,0:T(8,128)(2,1)}), bf16[16,8,6144]{2,1,0:T(8,128)(2,1)}, u32[]{:S(2)}, u32[]{:S(2)}) async-start(bf16[16,8,6144]{2,1,0:T(8,128)(2,1)} %fusion.1), calls=%async_computation | async-start | bytes 3145728 | tf_op jit(solution)/shard_map/all_to_all | solution.py:118
  56.8 91.5 %all-gather.2.cloned.1.call-start = ((), (), s32[]{:S(2)}) async-start(), calls=%async_computation.4 | async-start | bytes 9732096 | tf_op jit(solution)/shard_map/all_gather | solution.py:143
  148.2 4.9 %copy-start.5 = (bf16[6144,256]{1,0:T(8,128)(2,1)S(1)}, bf16[6144,256]{1,0:T(8,128)(2,1)}, u32[]{:S(2)}) copy-start(bf16[6144,256]{1,0:T(8,128)(2,1)} %param.18) | copy-start | bytes 9437188
  160.4 8.9 %collective-permute-start.1 = (bf16[384,6144]{1,0:T(8,128)(2,1)}, bf16[384,6144]{1,0:T(8,128)(2,1)}, u32[]{:S(2)}, u32[]{:S(2)}) collective-permute-start(bf16[384,6144]{1,0:T(8,128)(2,1)} %convolution_convert_fusion), channel_id=1, source_target_pairs={{0,16},{16,0},{1,17},{17,1},{2,18},{18,2},{3,19},{19,3},{4,20},{20... | collective-permute-start | bytes 14155784 | tf_op jit(solution)/shard_map/ppermute | solution.py:149
  160.6 4.9 %copy-start.6 = (bf16[6144,256]{1,0:T(8,128)(2,1)S(1)}, bf16[6144,256]{1,0:T(8,128)(2,1)}, u32[]{:S(2)}) copy-start(bf16[6144,256]{1,0:T(8,128)(2,1)} %param.18) | copy-start | bytes 9437188
  175.3 7.5 %copy-start.7 = (bf16[6144,4]{0,1:T(4,128)(2,1)S(1)}, bf16[6144,4]{0,1:T(4,128)(2,1)}, u32[]{:S(2)}) copy-start(bf16[6144,4]{0,1:T(4,128)(2,1)} %param.16) | copy-start | bytes 147460
  175.3 79.7 %all-to-all-start.2 = ((bf16[16,24,6144]{2,1,0:T(8,128)(2,1)}), bf16[16,24,6144]{2,1,0:T(8,128)(2,1)}, u32[]{:S(2)}, u32[]{:S(2)}) async-start(bf16[16,24,6144]{2,1,0:T(8,128)(2,1)} %bitcast.56), calls=%async_computation.2 | async-start | bytes 9437184 | tf_op jit(solution)/shard_map/all_to_all | solution.py:155
  260.7 11.8 %all-to-all-start.3 = ((bf16[4,6,6144]{2,1,0:T(8,128)(2,1)}), bf16[4,6,6144]{2,1,0:T(8,128)(2,1)}, u32[]{:S(2)}, u32[]{:S(2)}) async-start(bf16[4,6,6144]{2,1,0:T(8,128)(2,1)} %convert_element_type.111), calls=%async_computation.3 | async-start | bytes 786432 | tf_op jit(solution)/shard_map/all_to_all | solution.py:161
Sparse Core Ops, SparseCore 0:
  95.4 52.7 all-gather.1

commit v6 on v5

--- a/solution.py
+++ b/solution.py
@@ -91,11 +91,21 @@
     key_rows = jnp.where(holds_keys, mine, partner)
     values = jnp.where(holds_keys, partner, mine)
     both = jnp.stack([key_rows, values], axis=0)
-    gathered = lax.all_gather(both, ("z", "c"), axis=1, tiled=True)
+    nz = lax.axis_size("z")
+    core_swap = [(i, i ^ 1) for i in range(nc)]
+    other_core = lax.ppermute(both, "c", core_swap)
+    pair = jnp.where(ci == 0, jnp.stack([both, other_core]), jnp.stack([other_core, both]))
+    ring = [pair] + [
+        lax.ppermute(pair, "z", [(i, (i - k) % nz) for i in range(nz)]) for k in range(1, nz)
+    ]
+    gathered = jnp.stack(ring).transpose(2, 0, 1, 3, 4).reshape(2, -1, head_dim)
     key_piece = gathered[0]
     value_piece = gathered[1]
-    piece_rows = key_piece.shape[0]
-    key_places = jnp.arange(piece_rows, dtype=jnp.int32)
+    ring_range = jnp.arange(nz, dtype=jnp.int32)
+    shard_of = ((zi + ring_range) % nz)[:, None] * nc + jnp.arange(nc, dtype=jnp.int32)[None, :]
+    key_places = (
+        shard_of[:, :, None] * tok_dev + jnp.arange(tok_dev, dtype=jnp.int32)[None, None, :]
+    ).reshape(-1)
     key_doc, unused = doc_layout(doc_lengths, key_places)
     allowed = (document[:, None] == key_doc[None, :]) & (key_places[None, :] <= positions[:, None])
     scores = (
@@ -134,17 +144,21 @@
     slot = jnp.cumsum(names, axis=0) - names
     slot_range = jnp.arange(capacity, dtype=jnp.int32)
     hits = (slot[:, :, None] == slot_range) & (names[:, :, None] > 0)
+    shift = (xi + jnp.arange(nx, dtype=jnp.int32)) % nx
+    hits = jnp.take(hits, shift, axis=1)
+    gate_cols = jnp.take(gate_cols, shift, axis=1)
     send = jnp.einsum(
         "rec,rd->ecd", hits.astype(jnp.bfloat16), normed, preferred_element_type=jnp.float32
     ).astype(jnp.bfloat16)
 
-    arrived = lax.all_to_all(send, "x", split_axis=0, concat_axis=0, tiled=True)
-    arrived = arrived.reshape(experts * capacity, model_width)
+    arrived = [send[0]] + [
+        lax.ppermute(send[k], "x", [(i, (i + k) % nx) for i in range(nx)]) for k in range(1, nx)
+    ]
+    arrived = jnp.concatenate(arrived, axis=0)
     rows = lax.all_gather(arrived, ("c", "y", "z"), axis=0, tiled=True)
     line_rows = rows.shape[0] // nc
     other_rows = lax.dynamic_slice_in_dim(rows, (1 - ci) * line_rows, line_rows, 0)
     own_rows = lax.dynamic_slice_in_dim(rows, ci * line_rows, line_rows, 0)
-    core_swap = [(i, i ^ 1) for i in range(nc)]
     other_out = expert_rows(other_rows, gate_weight, up_weight, down_weight)
     other_back = lax.ppermute(other_out, "c", core_swap)
     own_out = expert_rows(own_rows, gate_weight, up_weight, down_weight)
@@ -158,7 +172,13 @@
         axis=0,
     )
     summed = summed.reshape(experts, capacity, model_width).astype(jnp.bfloat16)
-    returned = lax.all_to_all(summed, "x", split_axis=0, concat_axis=0, tiled=True)
+    returned = jnp.stack(
+        [summed[0]]
+        + [
+            lax.ppermute(summed[k], "x", [(i, (i - k) % nx) for i in range(nx)])
+            for k in range(1, nx)
+        ]
+    )
 
     weights = jnp.where(hits, gate_cols[:, :, None], 0.0)
     moe = jnp.einsum(

time: 283 us -> 274 us (0.968)
  blocking collectives: 23.6 us -> 0 us
  starting transfers between devices: 20.7 us -> 28.8 us
  waiting for transfers between devices: 154 us -> 160 us
    ppermute x0 -> x10, waiting for transfers between devices: none -> 16.6 us  [the longest x3 7.29 us: per_device(): lax.ppermute(pair, 'z', [(i, (i - k) % nz) for i in range(nz)])]
    all_gather x1 -> x0, blocking collectives: 12.9 us -> none  [per_device(): gathered = lax.all_gather(both, ('z', 'c'), axis=1, tiled=True)]
    ppermute x0 -> x10, starting transfers between devices: none -> 12.3 us  [the longest x3 5.68 us: per_device(): lax.ppermute(summed[k], 'x', [(i, (i - k) % nx) for i in range(nx)])]
    all_to_all x1 -> x0, blocking collectives: 10.7 us -> none  [per_device(): arrived = lax.all_to_all(send, 'x', split_axis=0, concat_axis=0, tiled=True)]
    all_to_all x1 -> x0, waiting for transfers between devices: 7.51 us -> none  [per_device(): lax.all_to_all(summed, 'x', split_axis=0, concat_axis=0, tiled=True)]
    all_to_all x1 -> x0, starting transfers between devices: 4.25 us -> none  [per_device(): lax.all_to_all(summed, 'x', split_axis=0, concat_axis=0, tiled=True)]
  transfers between devices with their start and end apart: 6 -> 15, of which waited for: 4 -> 13; matrix products, arithmetic and copies ran while one was open for 6% -> 7% of each run, Pallas kernels for 0% -> 0%
where the time goes in v6:
time: 274 us; the launch traced here: 273 us
  waiting for transfers between devices  160 us (58%)
  matrix products  48.1 us (18%)
  starting transfers between devices  28.8 us (11%)
  other arithmetic  17.4 us (6%)
  between operations  13.7 us (5%)
  local copies, waits for them, and re-layouts  4.93 us (2%)
    all_to_all x1, waiting for transfers between devices, per_device(): lax.all_to_all(lines, ('y', 'z'), split_axis=0, concat_axis=0, tiled=True)  71.1 us
    all_gather x1, waiting for transfers between devices, per_device(): rows = lax.all_gather(arrived, ('c', 'y', 'z'), axis=0, tiled=True)  52.9 us
    all_to_all x1, waiting for transfers between devices, per_device(): lax.all_to_all(blocks, ('x', 'y'), split_axis=0, concat_axis=0, tiled=True)  19.7 us
    dot_general x2, matrix products, expert_rows(): gate_part = jnp.dot(rows, gate_weight, preferred_element_type=jnp.float32)  9.68 us
    dot_general x2, matrix products, expert_rows(): jnp.dot(activated, down_weight, preferred_element_type=jnp.float32)  9.53 us
    all_to_all x1, starting transfers between devices, per_device(): lax.all_to_all(lines, ('y', 'z'), split_axis=0, concat_axis=0, tiled=True)  7.53 us
    dot_general x2, matrix products, expert_rows(): up_part = jnp.dot(rows, up_weight, preferred_element_type=jnp.float32)  7.53 us
    all_to_all x1, starting transfers between devices, per_device(): lax.all_to_all(blocks, ('x', 'y'), split_axis=0, concat_axis=0, tiled=True)  7.41 us
  transfers between devices with their start and end apart: 15, of which 13 were waited for; matrix products, arithmetic and copies ran while one was open for 7% of the time, Pallas kernels for 0%

profile of v6, /device:TPU:112, one launch (start us, length us, event | category | flops | bytes accessed | tf_op | source)
XLA Modules:
  0.0 273.2 jit_solution(13259992120934677464)
XLA Ops:
  6.6 1.0 reduce-window.8
  7.6 1.9 fusion.12
  9.5 0.7 fusion.49
  10.3 2.5 fusion.17
  13.8 1.3 collective-permute-start
  15.1 0.9 multiply_cosine_fusion.1
  16.1 4.4 %fusion.19 = f32[128,384]{0,1:T(8,128)S(1)} fusion(bf16[6144,384]{1,0:T(8,128)(2,1)} %param.11, bf16[128,6144]{1,0:T(8,128)(2,1)S(1)} %copy-done.1, f32[128]{0:T(128)S(1)} %add_rsqrt_fusion.1), kind=kOutput, calls=%fused_computation.32 | convolution fusion | flops 606339072 | bytes 6488576 | tf_op jit(solution)/shard_map/dot_general | solution.py:81
  21.2 1.0 copy.33
  22.3 1.6 subtract_convert_fusion
  23.9 0.8 select_bitcast_fusion.1
  24.9 1.2 collective-permute-done.1
  26.2 2.5 collective-permute-start.3
  28.8 3.7 %collective-permute-done.4 = bf16[2,2,128,128]{3,2,1,0:T(8,128)(2,1)S(1)} collective-permute-done((bf16[2,2,128,128]{3,2,1,0:T(8,128)(2,1)S(1)}, bf16[2,2,128,128]{3,2,1,0:T(8,128)(2,1)S(1)}, u32[]{:S(2)}, u32[]{:S(2)}) %collective-permute-start.4) | collective-permute-done | bytes 131104 | tf_op jit(solution)/shard_map/ppermute | solution.py:99
  32.5 1.6 collective-permute-done.3
  34.1 2.0 collective-permute-done.2
  36.2 0.7 fusion.80
  36.9 1.9 fusion.82
  38.8 2.6 multiply_select_fusion
  41.4 2.5 fusion.15
  43.9 4.5 %fusion.1 = bf16[16,8,6144]{2,1,0:T(8,128)(2,1)} fusion(bf16[128,384]{0,1:T(8,128)(2,1)S(1)} %bitcast.95, bf16[384,6144]{1,0:T(8,128)(2,1)} %param.13), kind=kOutput, calls=%fused_computation.7 | convolution fusion | flops 604766208 | bytes 6389760 | tf_op jit(solution)/shard_map/dot_general | solution.py:125
  48.4 7.4 %all-to-all-start = ((bf16[16,8,6144]{2,1,0:T(8,128)(2,1)}), bf16[16,8,6144]{2,1,0:T(8,128)(2,1)}, u32[]{:S(2)}, u32[]{:S(2)}) async-start(bf16[16,8,6144]{2,1,0:T(8,128)(2,1)} %fusion.1), calls=%async_computation | async-start | bytes 3145728 | tf_op jit(solution)/shard_map/all_to_all | solution.py:128
  56.8 19.7 %all-to-all-done = bf16[16,8,6144]{2,1,0:T(8,128)(2,1)} async-done(((bf16[16,8,6144]{2,1,0:T(8,128)(2,1)}), bf16[16,8,6144]{2,1,0:T(8,128)(2,1)}, u32[]{:S(2)}, u32[]{:S(2)}) %all-to-all-start) | async-done | bytes 1572896 | tf_op jit(solution)/shard_map/all_to_all | solution.py:128
  76.5 1.6 convert_reduce_fusion
  78.2 1.1 multiply_reduce_fusion
  79.2 1.0 multiply_convert_fusion.2
  80.6 1.4 collective-permute-start.7
  82.1 1.7 collective-permute-start.6
  83.7 0.9 collective-permute-start.5
  85.3 2.9 %collective-permute-done.6 = bf16[6,6144]{1,0:T(8,128)(2,1)S(1)} collective-permute-done((bf16[6,6144]{1,0:T(8,128)(2,1)S(1)}, bf16[6,6144]{1,0:T(8,128)(2,1)S(1)}, u32[]{:S(2)}, u32[]{:S(2)}) %collective-permute-start.6) | collective-permute-done | bytes 73760 | tf_op jit(solution)/shard_map/ppermute | solution.py:155
  88.2 1.4 collective-permute-done.5
  89.5 0.9 pad_maximum_fusion
  90.4 52.9 %all-gather.2.cloned.1.call-done = bf16[768,6144]{1,0:T(8,128)(2,1)} async-done(((bf16[24,6144]{1,0:T(8,128)(2,1)}), bf16[768,6144]{1,0:T(8,128)(2,1)}) %all-gather.2.cloned.1.call-update) | async-done | bytes 9437200 | tf_op jit(solution)/shard_map/all_gather | solution.py:158
  143.3 4.8 %fusion.6 = f32[384,256]{1,0:T(8,128)S(1)} fusion(bf16[6144,256]{1,0:T(8,128)(2,1)} %param.17, bf16[768,6144]{1,0:T(8,128)(2,1)} %all-gather.2.cloned.1.call-done, s32[]{:T(128)S(6)} %select_n.150), kind=kOutput, calls=%fused_computation.14 | convolution fusion | flops 1207959552 | bytes 8257540 | tf_op jit(solution)/shard_map/dot_general | solution.py:44
  148.2 3.8 %multiply_convert_fusion = bf16[384,256]{1,0:T(8,128)(2,1)S(1)} fusion(f32[384,256]{1,0:T(8,128)S(1)} %fusion.6, bf16[6144,256]{1,0:T(8,128)(2,1)S(1)} %copy-done.3, bf16[768,6144]{1,0:T(8,128)(2,1)} %all-gather.2.cloned.1.call-done, s32[]{:T(128)S(6)} %select_n.150), kind=kOutput, calls=%fused_computation.42 | convolution fusion | flops 1208549376 | bytes 8454148 | tf_op jit(solution)/shard_map/dot_general | solution.py:45
  152.0 3.5 %convolution_convert_fusion = bf16[384,6144]{1,0:T(8,128)(2,1)} fusion(bf16[384,256]{1,0:T(8,128)(2,1)S(1)} %multiply_convert_fusion, bf16[256,6144]{1,0:T(8,128)(2,1)S(1)} %copy-done), kind=kOutput, calls=%fused_computation.4 | convolution fusion | flops 1210318848 | bytes 8060928 | tf_op jit(solution)/shard_map/dot_general | solution.py:47
  155.7 4.8 %fusion.10 = f32[384,256]{1,0:T(8,128)S(1)} fusion(bf16[6144,256]{1,0:T(8,128)(2,1)} %param.17, bf16[768,6144]{1,0:T(8,128)(2,1)} %all-gather.2.cloned.1.call-done, s32[]{:T(128)S(6)} %select_n.149), kind=kOutput, calls=%fused_computation.18 | convolution fusion | flops 1207959552 | bytes 8257540 | tf_op jit(solution)/shard_map/dot_general | solution.py:44
  160.6 3.8 %multiply_convert_fusion.1 = bf16[384,256]{1,0:T(8,128)(2,1)S(1)} fusion(f32[384,256]{1,0:T(8,128)S(1)} %fusion.10, bf16[6144,256]{1,0:T(8,128)(2,1)S(1)} %copy-done.4, bf16[768,6144]{1,0:T(8,128)(2,1)} %all-gather.2.cloned.1.call-done, s32[]{:T(128)S(6)} %select_n.149), kind=kOutput, calls=%fused_computation.43 | convolution fusion | flops 1208549376 | bytes 8454148 | tf_op jit(solution)/shard_map/dot_general | solution.py:45
  164.4 6.0 %add_convert_fusion = bf16[384,6144]{1,0:T(8,128)(2,1)} fusion(bf16[384,6144]{1,0:T(8,128)(2,1)} %collective-permute-done.8, bf16[384,256]{1,0:T(8,128)(2,1)S(1)} %multiply_convert_fusion.1, bf16[256,6144]{1,0:T(8,128)(2,1)S(1)} %copy-done), kind=kOutput, calls=%fused_computation.3 | convolution fusion | flops 1219756032 | bytes 12779520 | tf_op jit(solution)/shard_map/dot_general | solution.py:47
  170.4 7.5 %all-to-all-start.1 = ((bf16[16,24,6144]{2,1,0:T(8,128)(2,1)}), bf16[16,24,6144]{2,1,0:T(8,128)(2,1)}, u32[]{:S(2)}, u32[]{:S(2)}) async-start(bf16[16,24,6144]{2,1,0:T(8,128)(2,1)} %bitcast.87), calls=%async_computation.1 | async-start | bytes 9437184 | tf_op jit(solution)/shard_map/all_to_all | solution.py:169
  178.7 71.1 %all-to-all-done.1 = bf16[16,24,6144]{2,1,0:T(8,128)(2,1)} async-done(((bf16[16,24,6144]{2,1,0:T(8,128)(2,1)}), bf16[16,24,6144]{2,1,0:T(8,128)(2,1)}, u32[]{:S(2)}, u32[]{:S(2)}) %all-to-all-start.1) | async-done | bytes 4718624 | tf_op jit(solution)/shard_map/all_to_all | solution.py:169
  249.8 3.9 %reduce_sum.112 = bf16[24,6144]{1,0:T(8,128)(2,1)} reduce(bf16[16,24,6144]{2,1,0:T(8,128)(2,1)} %all-to-all-done.1, bf16[]{:T(256)} %constant.129.clone.1), dimensions={0}, to_apply=%region_15.16 | reduce | flops 2211840 | bytes 5013506 | tf_op jit(solution)/shard_map/reduce_sum | solution.py:168
  253.7 1.2 slice_bitcast_fusion
  254.9 1.8 collective-permute-start.11
  256.7 2.5 collective-permute-start.10
  259.2 1.3 collective-permute-start.9
  260.6 1.2 collective-permute-done.11
  261.8 1.3 collective-permute-done.10
  263.9 2.5 fusion.3
  (59 shorter events, 6.4 us)
Async XLA Ops:
  6.5 145.4 %copy-start = (bf16[256,6144]{1,0:T(8,128)(2,1)S(1)}, bf16[256,6144]{1,0:T(8,128)(2,1)}, u32[]{:S(2)}) copy-start(bf16[256,6144]{1,0:T(8,128)(2,1)} %param.19) | copy-start | bytes 9437188
  7.6 8.5 %copy-start.1 = (bf16[128,6144]{1,0:T(8,128)(2,1)S(1)}, bf16[128,6144]{1,0:T(8,128)(2,1)}, u32[]{:S(2)}) copy-start(bf16[128,6144]{1,0:T(8,128)(2,1)} %param.10) | copy-start | bytes 4718596
  13.8 10.2 %collective-permute-start = (bf16[128,128]{1,0:T(8,128)(2,1)}, bf16[128,128]{1,0:T(8,128)(2,1)}, u32[]{:S(2)}, u32[]{:S(2)}) collective-permute-start(bf16[128,128]{1,0:T(8,128)(2,1)} %fusion.36), channel_id=1, source_target_pairs={{0,1},{1,0},{2,3},{3,2},{4,5},{5,4},{6,7},{7,6},{8,9},{9,8},{10,11... | collective-permute-start | bytes 98312 | tf_op jit(solution)/shard_map/ppermute | solution.py:90
  24.7 1.3 collective-permute-start.1
  26.1 6.4 %collective-permute-start.4 = (bf16[2,2,128,128]{3,2,1,0:T(8,128)(2,1)S(1)}, bf16[2,2,128,128]{3,2,1,0:T(8,128)(2,1)S(1)}, u32[]{:S(2)}, u32[]{:S(2)}) collective-permute-start(bf16[2,2,128,128]{3,2,1,0:T(8,128)(2,1)S(1)} %maximum_select_fusion.1), channel_id=1, source_target_pairs={{0,32},{32,64},{64,96},{96,0},{1,33},{33,65},{65,97},{97,1},{2,34}... | collective-permute-start | bytes 393224 | tf_op jit(solution)/shard_map/ppermute | solution.py:99
  26.2 8.0 %collective-permute-start.3 = (bf16[2,2,128,128]{3,2,1,0:T(8,128)(2,1)S(1)}, bf16[2,2,128,128]{3,2,1,0:T(8,128)(2,1)S(1)}, u32[]{:S(2)}, u32[]{:S(2)}) collective-permute-start(bf16[2,2,128,128]{3,2,1,0:T(8,128)(2,1)S(1)} %maximum_select_fusion.1), channel_id=1, source_target_pairs={{0,64},{32,96},{64,0},{96,32},{1,65},{33,97},{65,1},{97,33},{2,66}... | collective-permute-start | bytes 393224 | tf_op jit(solution)/shard_map/ppermute | solution.py:99
  28.6 7.5 %collective-permute-start.2 = (bf16[2,2,128,128]{3,2,1,0:T(8,128)(2,1)S(1)}, bf16[2,2,128,128]{3,2,1,0:T(8,128)(2,1)S(1)}, u32[]{:S(2)}, u32[]{:S(2)}) collective-permute-start(bf16[2,2,128,128]{3,2,1,0:T(8,128)(2,1)S(1)} %maximum_select_fusion.1), channel_id=1, source_target_pairs={{0,96},{32,0},{64,32},{96,64},{1,97},{33,1},{65,33},{97,65},{2,98}... | collective-permute-start | bytes 393224 | tf_op jit(solution)/shard_map/ppermute | solution.py:99
  48.4 7.5 %copy-start.2 = (s32[8,2]{0,1:T(2,128)S(1)}, s32[8,2]{0,1:T(2,128)}, u32[]{:S(2)}) copy-start(s32[8,2]{0,1:T(2,128)} %param.15) | copy-start | bytes 196
  48.4 28.1 %all-to-all-start = ((bf16[16,8,6144]{2,1,0:T(8,128)(2,1)}), bf16[16,8,6144]{2,1,0:T(8,128)(2,1)}, u32[]{:S(2)}, u32[]{:S(2)}) async-start(bf16[16,8,6144]{2,1,0:T(8,128)(2,1)} %fusion.1), calls=%async_computation | async-start | bytes 3145728 | tf_op jit(solution)/shard_map/all_to_all | solution.py:128
  55.8 87.5 %all-gather.2.cloned.1.call-start = ((), (), s32[]{:S(2)}) async-start(), calls=%async_computation.2 | async-start | bytes 9732096 | tf_op jit(solution)/shard_map/all_gather | solution.py:158
  80.6 4.7 %collective-permute-start.7 = (bf16[6,6144]{1,0:T(8,128)(2,1)S(1)}, bf16[6,6144]{1,0:T(8,128)(2,1)S(1)}, u32[]{:S(2)}, u32[]{:S(2)}) collective-permute-start(bf16[6,6144]{1,0:T(8,128)(2,1)S(1)} %get-tuple-element.12), channel_id=1, source_target_pairs={{0,12},{4,0},{8,4},{12,8},{1,13},{5,1},{9,5},{13,9},{2,14},{6,2},{... | collective-permute-start | bytes 221192 | tf_op jit(solution)/shard_map/ppermute | solution.py:155
  82.1 6.1 %collective-permute-start.6 = (bf16[6,6144]{1,0:T(8,128)(2,1)S(1)}, bf16[6,6144]{1,0:T(8,128)(2,1)S(1)}, u32[]{:S(2)}, u32[]{:S(2)}) collective-permute-start(bf16[6,6144]{1,0:T(8,128)(2,1)S(1)} %get-tuple-element.13), channel_id=1, source_target_pairs={{0,8},{4,12},{8,0},{12,4},{1,9},{5,13},{9,1},{13,5},{2,10},{6,14},... | collective-permute-start | bytes 221192 | tf_op jit(solution)/shard_map/ppermute | solution.py:155
  83.7 5.8 %collective-permute-start.5 = (bf16[6,6144]{1,0:T(8,128)(2,1)S(1)}, bf16[6,6144]{1,0:T(8,128)(2,1)S(1)}, u32[]{:S(2)}, u32[]{:S(2)}) collective-permute-start(bf16[6,6144]{1,0:T(8,128)(2,1)S(1)} %get-tuple-element.14), channel_id=1, source_target_pairs={{0,4},{4,8},{8,12},{12,0},{1,5},{5,9},{9,13},{13,1},{2,6},{6,10},{... | collective-permute-start | bytes 221192 | tf_op jit(solution)/shard_map/ppermute | solution.py:155
  143.3 4.9 %copy-start.3 = (bf16[6144,256]{1,0:T(8,128)(2,1)S(1)}, bf16[6144,256]{1,0:T(8,128)(2,1)}, u32[]{:S(2)}) copy-start(bf16[6144,256]{1,0:T(8,128)(2,1)} %param.18) | copy-start | bytes 9437188
  155.5 8.9 %collective-permute-start.8 = (bf16[384,6144]{1,0:T(8,128)(2,1)}, bf16[384,6144]{1,0:T(8,128)(2,1)}, u32[]{:S(2)}, u32[]{:S(2)}) collective-permute-start(bf16[384,6144]{1,0:T(8,128)(2,1)} %convolution_convert_fusion), channel_id=1, source_target_pairs={{0,16},{16,0},{1,17},{17,1},{2,18},{18,2},{3,19},{19,3},{4,20},{20... | collective-permute-start | bytes 14155784 | tf_op jit(solution)/shard_map/ppermute | solution.py:163
  155.7 4.9 %copy-start.4 = (bf16[6144,256]{1,0:T(8,128)(2,1)S(1)}, bf16[6144,256]{1,0:T(8,128)(2,1)}, u32[]{:S(2)}) copy-start(bf16[6144,256]{1,0:T(8,128)(2,1)} %param.18) | copy-start | bytes 9437188
  170.4 7.5 %copy-start.5 = (bf16[6144,4]{0,1:T(4,128)(2,1)S(1)}, bf16[6144,4]{0,1:T(4,128)(2,1)}, u32[]{:S(2)}) copy-start(bf16[6144,4]{0,1:T(4,128)(2,1)} %param.16) | copy-start | bytes 147460
  170.4 79.5 %all-to-all-start.1 = ((bf16[16,24,6144]{2,1,0:T(8,128)(2,1)}), bf16[16,24,6144]{2,1,0:T(8,128)(2,1)}, u32[]{:S(2)}, u32[]{:S(2)}) async-start(bf16[16,24,6144]{2,1,0:T(8,128)(2,1)} %bitcast.87), calls=%async_computation.1 | async-start | bytes 9437184 | tf_op jit(solution)/shard_map/all_to_all | solution.py:169
  254.9 6.9 %collective-permute-start.11 = (bf16[6,6144]{1,0:T(8,128)(2,1)S(1)}, bf16[6,6144]{1,0:T(8,128)(2,1)S(1)}, u32[]{:S(2)}, u32[]{:S(2)}) collective-permute-start(bf16[6,6144]{1,0:T(8,128)(2,1)S(1)} %get-tuple-element.16), channel_id=1, source_target_pairs={{0,4},{4,8},{8,12},{12,0},{1,5},{5,9},{9,13},{13,1},{2,6},{6,10},{... | collective-permute-start | bytes 221192 | tf_op jit(solution)/shard_map/ppermute | solution.py:178
  256.7 6.4 %collective-permute-start.10 = (bf16[6,6144]{1,0:T(8,128)(2,1)S(1)}, bf16[6,6144]{1,0:T(8,128)(2,1)S(1)}, u32[]{:S(2)}, u32[]{:S(2)}) collective-permute-start(bf16[6,6144]{1,0:T(8,128)(2,1)S(1)} %get-tuple-element.17), channel_id=1, source_target_pairs={{0,8},{4,12},{8,0},{12,4},{1,9},{5,13},{9,1},{13,5},{2,10},{6,14},... | collective-permute-start | bytes 221192 | tf_op jit(solution)/shard_map/ppermute | solution.py:178
  259.2 4.6 %collective-permute-start.9 = (bf16[6,6144]{1,0:T(8,128)(2,1)S(1)}, bf16[6,6144]{1,0:T(8,128)(2,1)S(1)}, u32[]{:S(2)}, u32[]{:S(2)}) collective-permute-start(bf16[6,6144]{1,0:T(8,128)(2,1)S(1)} %get-tuple-element.18), channel_id=1, source_target_pairs={{0,12},{4,0},{8,4},{12,8},{1,13},{5,1},{9,5},{13,9},{2,14},{6,2},{... | collective-permute-start | bytes 221192 | tf_op jit(solution)/shard_map/ppermute | solution.py:178
Sparse Core Ops, SparseCore 0:
  90.5 52.7 all-gather.1

commit v7 on v6

--- a/solution.py
+++ b/solution.py
@@ -164,12 +164,12 @@
     own_out = expert_rows(own_rows, gate_weight, up_weight, down_weight)
     summed = (own_out.astype(jnp.float32) + other_back.astype(jnp.float32)).astype(jnp.bfloat16)
 
-    lines = summed.reshape(-1, experts * capacity, model_width)
-    summed = jnp.sum(
-        lax.all_to_all(lines, ("y", "z"), split_axis=0, concat_axis=0, tiled=True).astype(
-            jnp.float32
-        ),
-        axis=0,
+    split = model_width * 2 // 3 // 128 * 128
+    lines = summed[:, :split].reshape(-1, experts * capacity, split)
+    spread = lax.all_to_all(lines, ("y", "z"), split_axis=0, concat_axis=0, tiled=True)
+    scattered = lax.psum_scatter(summed[:, split:], ("y", "z"), scatter_dimension=0, tiled=True)
+    summed = jnp.concatenate(
+        [jnp.sum(spread.astype(jnp.float32), axis=0), scattered.astype(jnp.float32)], axis=1
     )
     summed = summed.reshape(experts, capacity, model_width).astype(jnp.bfloat16)
     returned = jnp.stack(

time: 274 us -> 300 us (1.095); the launches traced: 273 us -> 295 us
  waiting for transfers between devices: 160 us -> 179 us
  local copies, waits for them, and re-layouts: 4.93 us -> 11.1 us
    unnamed x1 -> x3, waiting for transfers between devices: 0.02 us -> 43 us
    all_to_all x1, waiting for transfers between devices: 71.1 us -> 45.9 us  [per_device(): lax.all_to_all(lines, ('y', 'z'), split_axis=0, concat_axis=0, tiled=True)]
    slice x1 -> x2, local copies, waits for them, and re-layouts: 1.2 us -> 5.24 us  [the longest x1 3.91 us: per_device(): lines = summed[:, :split].reshape(-1, experts * capacity, split)]
  transfers between devices with their start and end apart: 15 -> 16, of which waited for: 13 -> 13; matrix products, arithmetic and copies ran while one was open for 7% -> 9% of each run, Pallas kernels for 0% -> 0%
where the time goes in v7:
time: 300 us; the launch traced here: 295 us
  waiting for transfers between devices  179 us (60%)
  matrix products  46 us (15%)
  starting transfers between devices  28.4 us (9%)
  other arithmetic  17 us (6%)
  between operations  13.7 us (5%)
  local copies, waits for them, and re-layouts  11.1 us (4%)
    all_gather x1, waiting for transfers between devices, per_device(): rows = lax.all_gather(arrived, ('c', 'y', 'z'), axis=0, tiled=True)  52.7 us
    all_to_all x1, waiting for transfers between devices, per_device(): lax.all_to_all(lines, ('y', 'z'), split_axis=0, concat_axis=0, tiled=True)  45.9 us
    unnamed x3, waiting for transfers between devices  43 us
    all_to_all x1, waiting for transfers between devices, per_device(): lax.all_to_all(blocks, ('x', 'y'), split_axis=0, concat_axis=0, tiled=True)  19.7 us
    dot_general x2, matrix products, expert_rows(): gate_part = jnp.dot(rows, gate_weight, preferred_element_type=jnp.float32)  9.68 us
    all_to_all x1, starting transfers between devices, per_device(): lax.all_to_all(lines, ('y', 'z'), split_axis=0, concat_axis=0, tiled=True)  7.53 us
    dot_general x2, matrix products, expert_rows(): up_part = jnp.dot(rows, up_weight, preferred_element_type=jnp.float32)  7.52 us
    dot_general x2, matrix products, expert_rows(): jnp.dot(activated, down_weight, preferred_element_type=jnp.float32)  7.46 us
  transfers between devices with their start and end apart: 16, of which 13 were waited for; matrix products, arithmetic and copies ran while one was open for 9% of the time, Pallas kernels for 0%

profile of v7, /device:TPU:112, one launch (start us, length us, event | category | flops | bytes accessed | tf_op | source)
XLA Modules:
  0.0 295.4 jit_solution(993328351735875066)
XLA Ops:
  6.6 1.0 reduce-window.8
  7.6 1.9 fusion.12
  10.3 2.5 fusion.17
  13.8 1.3 collective-permute-start
  15.1 0.9 multiply_cosine_fusion.1
  16.1 4.4 %fusion.19 = f32[128,384]{0,1:T(8,128)S(1)} fusion(bf16[6144,384]{1,0:T(8,128)(2,1)} %param.11, bf16[128,6144]{1,0:T(8,128)(2,1)S(1)} %copy-done.2, f32[128]{0:T(128)S(1)} %add_rsqrt_fusion.1), kind=kOutput, calls=%fused_computation.32 | convolution fusion | flops 606339072 | bytes 6488576 | tf_op jit(solution)/shard_map/dot_general | solution.py:81
  21.2 1.0 copy.40
  22.3 1.6 subtract_convert_fusion
  24.9 1.2 collective-permute-done.1
  26.2 2.5 collective-permute-start.3
  28.8 3.7 %collective-permute-done.4 = bf16[2,2,128,128]{3,2,1,0:T(8,128)(2,1)S(1)} collective-permute-done((bf16[2,2,128,128]{3,2,1,0:T(8,128)(2,1)S(1)}, bf16[2,2,128,128]{3,2,1,0:T(8,128)(2,1)S(1)}, u32[]{:S(2)}, u32[]{:S(2)}) %collective-permute-start.4) | collective-permute-done | bytes 131104 | tf_op jit(solution)/shard_map/ppermute | solution.py:99
  32.5 1.6 collective-permute-done.3
  34.1 2.0 collective-permute-done.2
  36.9 1.9 fusion.86
  38.8 2.6 multiply_select_fusion
  41.4 2.5 fusion.15
  43.9 4.5 %fusion.1 = bf16[16,8,6144]{2,1,0:T(8,128)(2,1)} fusion(bf16[128,384]{0,1:T(8,128)(2,1)S(1)} %bitcast.96, bf16[384,6144]{1,0:T(8,128)(2,1)} %param.13), kind=kOutput, calls=%fused_computation.7 | convolution fusion | flops 604766208 | bytes 6389760 | tf_op jit(solution)/shard_map/dot_general | solution.py:125
  48.4 7.4 %all-to-all-start = ((bf16[16,8,6144]{2,1,0:T(8,128)(2,1)}), bf16[16,8,6144]{2,1,0:T(8,128)(2,1)}, u32[]{:S(2)}, u32[]{:S(2)}) async-start(bf16[16,8,6144]{2,1,0:T(8,128)(2,1)} %fusion.1), calls=%async_computation | async-start | bytes 3145728 | tf_op jit(solution)/shard_map/all_to_all | solution.py:128
  56.8 19.7 %all-to-all-done = bf16[16,8,6144]{2,1,0:T(8,128)(2,1)} async-done(((bf16[16,8,6144]{2,1,0:T(8,128)(2,1)}), bf16[16,8,6144]{2,1,0:T(8,128)(2,1)}, u32[]{:S(2)}, u32[]{:S(2)}) %all-to-all-start) | async-done | bytes 1572896 | tf_op jit(solution)/shard_map/all_to_all | solution.py:128
  76.5 1.6 convert_reduce_fusion
  78.2 1.1 multiply_reduce_fusion
  79.2 1.0 multiply_convert_fusion.2
  80.6 1.4 collective-permute-start.7
  82.1 1.7 collective-permute-start.6
  83.7 0.9 collective-permute-start.5
  85.3 2.9 collective-permute-done.6
  88.2 1.4 collective-permute-done.5
  89.6 0.9 pad_maximum_fusion
  90.7 52.7 %all-gather.2.cloned.1.call-done = bf16[768,6144]{1,0:T(8,128)(2,1)} async-done(((bf16[24,6144]{1,0:T(8,128)(2,1)}), bf16[768,6144]{1,0:T(8,128)(2,1)}) %all-gather.2.cloned.1.call-update) | async-done | bytes 9437200 | tf_op jit(solution)/shard_map/all_gather | solution.py:158
  143.3 4.8 %fusion.6 = f32[384,256]{1,0:T(8,128)S(1)} fusion(bf16[6144,256]{1,0:T(8,128)(2,1)} %param.17, bf16[768,6144]{1,0:T(8,128)(2,1)} %all-gather.2.cloned.1.call-done, s32[]{:T(128)S(6)} %select_n.150), kind=kOutput, calls=%fused_computation.14 | convolution fusion | flops 1207959552 | bytes 8257540 | tf_op jit(solution)/shard_map/dot_general | solution.py:44
  148.2 3.8 %multiply_convert_fusion = bf16[384,256]{1,0:T(8,128)(2,1)S(1)} fusion(f32[384,256]{1,0:T(8,128)S(1)} %fusion.6, bf16[6144,256]{1,0:T(8,128)(2,1)S(1)} %copy-done.4, bf16[768,6144]{1,0:T(8,128)(2,1)} %all-gather.2.cloned.1.call-done, s32[]{:T(128)S(6)} %select_n.150), kind=kOutput, calls=%fused_computation.45 | convolution fusion | flops 1208549376 | bytes 8454148 | tf_op jit(solution)/shard_map/dot_general | solution.py:45
  152.0 3.6 %convolution_convert_fusion = bf16[384,6144]{1,0:T(8,128)(2,1)} fusion(bf16[384,256]{1,0:T(8,128)(2,1)S(1)} %multiply_convert_fusion, bf16[256,6144]{1,0:T(8,128)(2,1)S(1)} %copy-done), kind=kOutput, calls=%fused_computation.4 | convolution fusion | flops 1210318848 | bytes 8060928 | tf_op jit(solution)/shard_map/dot_general | solution.py:47
  155.8 4.8 %fusion.10 = f32[384,256]{1,0:T(8,128)S(1)} fusion(bf16[6144,256]{1,0:T(8,128)(2,1)} %param.17, bf16[768,6144]{1,0:T(8,128)(2,1)} %all-gather.2.cloned.1.call-done, s32[]{:T(128)S(6)} %select_n.149), kind=kOutput, calls=%fused_computation.18 | convolution fusion | flops 1207959552 | bytes 8257540 | tf_op jit(solution)/shard_map/dot_general | solution.py:44
  160.7 3.8 %multiply_convert_fusion.1 = bf16[384,256]{1,0:T(8,128)(2,1)S(1)} fusion(f32[384,256]{1,0:T(8,128)S(1)} %fusion.10, bf16[6144,256]{1,0:T(8,128)(2,1)S(1)} %copy-done.5, bf16[768,6144]{1,0:T(8,128)(2,1)} %all-gather.2.cloned.1.call-done, s32[]{:T(128)S(6)} %select_n.149), kind=kOutput, calls=%fused_computation.46 | convolution fusion | flops 1208549376 | bytes 8454148 | tf_op jit(solution)/shard_map/dot_general | solution.py:45
  164.5 3.8 %add_convert_fusion = bf16[384,6144]{1,0:T(8,128)(2,1)S(1)} fusion(bf16[384,6144]{1,0:T(8,128)(2,1)} %collective-permute-done.8, bf16[384,256]{1,0:T(8,128)(2,1)S(1)} %multiply_convert_fusion.1, bf16[256,6144]{1,0:T(8,128)(2,1)S(1)} %copy-done), kind=kOutput, calls=%fused_computation.3 | convolution fusion | flops 1219756032 | bytes 12779520 | tf_op jit(solution)/shard_map/dot_general | solution.py:47
  168.3 2.1 copy-done.1
  170.4 1.3 slice.88
  171.8 3.9 %slice.87 = bf16[384,4096]{1,0:T(8,128)(2,1)} slice(bf16[384,6144]{1,0:T(8,128)(2,1)} %copy-done.1), slice={[0:384], [0:4096]} | slice | bytes 6291456 | tf_op jit(solution)/shard_map/slice | solution.py:168
  175.7 7.5 %all-to-all-start.1 = ((bf16[16,24,4096]{2,1,0:T(8,128)(2,1)}), bf16[16,24,4096]{2,1,0:T(8,128)(2,1)}, u32[]{:S(2)}, u32[]{:S(2)}) async-start(bf16[16,24,4096]{2,1,0:T(8,128)(2,1)} %bitcast.88), calls=%async_computation.1 | async-start | bytes 6291456 | tf_op jit(solution)/shard_map/all_to_all | solution.py:169
  184.1 45.9 %all-to-all-done.1 = bf16[16,24,4096]{2,1,0:T(8,128)(2,1)} async-done(((bf16[16,24,4096]{2,1,0:T(8,128)(2,1)}), bf16[16,24,4096]{2,1,0:T(8,128)(2,1)}, u32[]{:S(2)}, u32[]{:S(2)}) %all-to-all-start.1) | async-done | bytes 3145760 | tf_op jit(solution)/shard_map/all_to_all | solution.py:169
  230.0 2.5 reduce
  232.5 43.0 %reduce-scatter.4.cloned.1.call-done = bf16[24,2048]{1,0:T(8,128)(2,1)} async-done(((bf16[384,2048]{1,0:T(8,128)(2,1)}), bf16[24,2048]{1,0:T(8,128)(2,1)}) %reduce-scatter.4.cloned.1.call-update) | async-done | bytes 98320
  275.5 1.0 fusion.30
  276.5 2.8 collective-permute-start.9
  279.3 2.3 collective-permute-start.10
  281.6 0.8 collective-permute-done.9
  282.5 3.7 %collective-permute-done.11 = bf16[6,6144]{1,0:T(8,128)(2,1)S(1)} collective-permute-done((bf16[6,6144]{1,0:T(8,128)(2,1)S(1)}, bf16[6,6144]{1,0:T(8,128)(2,1)S(1)}, u32[]{:S(2)}, u32[]{:S(2)}) %collective-permute-start.11) | collective-permute-done | bytes 73760 | tf_op jit(solution)/shard_map/ppermute | solution.py:178
  286.1 2.5 fusion.3
  (66 shorter events, 8.2 us)
Async XLA Ops:
  6.5 145.4 %copy-start = (bf16[256,6144]{1,0:T(8,128)(2,1)S(1)}, bf16[256,6144]{1,0:T(8,128)(2,1)}, u32[]{:S(2)}) copy-start(bf16[256,6144]{1,0:T(8,128)(2,1)} %param.19) | copy-start | bytes 9437188
  7.6 8.5 %copy-start.2 = (bf16[128,6144]{1,0:T(8,128)(2,1)S(1)}, bf16[128,6144]{1,0:T(8,128)(2,1)}, u32[]{:S(2)}) copy-start(bf16[128,6144]{1,0:T(8,128)(2,1)} %param.10) | copy-start | bytes 4718596
  13.8 10.2 %collective-permute-start = (bf16[128,128]{1,0:T(8,128)(2,1)}, bf16[128,128]{1,0:T(8,128)(2,1)}, u32[]{:S(2)}, u32[]{:S(2)}) collective-permute-start(bf16[128,128]{1,0:T(8,128)(2,1)} %fusion.40), channel_id=1, source_target_pairs={{0,1},{1,0},{2,3},{3,2},{4,5},{5,4},{6,7},{7,6},{8,9},{9,8},{10,11... | collective-permute-start | bytes 98312 | tf_op jit(solution)/shard_map/ppermute | solution.py:90
  24.7 1.3 collective-permute-start.1
  26.1 6.4 %collective-permute-start.4 = (bf16[2,2,128,128]{3,2,1,0:T(8,128)(2,1)S(1)}, bf16[2,2,128,128]{3,2,1,0:T(8,128)(2,1)S(1)}, u32[]{:S(2)}, u32[]{:S(2)}) collective-permute-start(bf16[2,2,128,128]{3,2,1,0:T(8,128)(2,1)S(1)} %maximum_select_fusion.1), channel_id=1, source_target_pairs={{0,32},{32,64},{64,96},{96,0},{1,33},{33,65},{65,97},{97,1},{2,34}... | collective-permute-start | bytes 393224 | tf_op jit(solution)/shard_map/ppermute | solution.py:99
  26.2 8.0 %collective-permute-start.3 = (bf16[2,2,128,128]{3,2,1,0:T(8,128)(2,1)S(1)}, bf16[2,2,128,128]{3,2,1,0:T(8,128)(2,1)S(1)}, u32[]{:S(2)}, u32[]{:S(2)}) collective-permute-start(bf16[2,2,128,128]{3,2,1,0:T(8,128)(2,1)S(1)} %maximum_select_fusion.1), channel_id=1, source_target_pairs={{0,64},{32,96},{64,0},{96,32},{1,65},{33,97},{65,1},{97,33},{2,66}... | collective-permute-start | bytes 393224 | tf_op jit(solution)/shard_map/ppermute | solution.py:99
  28.6 7.5 %collective-permute-start.2 = (bf16[2,2,128,128]{3,2,1,0:T(8,128)(2,1)S(1)}, bf16[2,2,128,128]{3,2,1,0:T(8,128)(2,1)S(1)}, u32[]{:S(2)}, u32[]{:S(2)}) collective-permute-start(bf16[2,2,128,128]{3,2,1,0:T(8,128)(2,1)S(1)} %maximum_select_fusion.1), channel_id=1, source_target_pairs={{0,96},{32,0},{64,32},{96,64},{1,97},{33,1},{65,33},{97,65},{2,98}... | collective-permute-start | bytes 393224 | tf_op jit(solution)/shard_map/ppermute | solution.py:99
  48.4 7.5 %copy-start.3 = (s32[8,2]{0,1:T(2,128)S(1)}, s32[8,2]{0,1:T(2,128)}, u32[]{:S(2)}) copy-start(s32[8,2]{0,1:T(2,128)} %param.15) | copy-start | bytes 196
  48.4 28.1 %all-to-all-start = ((bf16[16,8,6144]{2,1,0:T(8,128)(2,1)}), bf16[16,8,6144]{2,1,0:T(8,128)(2,1)}, u32[]{:S(2)}, u32[]{:S(2)}) async-start(bf16[16,8,6144]{2,1,0:T(8,128)(2,1)} %fusion.1), calls=%async_computation | async-start | bytes 3145728 | tf_op jit(solution)/shard_map/all_to_all | solution.py:128
  55.8 87.5 %all-gather.2.cloned.1.call-start = ((), (), s32[]{:S(2)}) async-start(), calls=%async_computation.3 | async-start | bytes 9732096 | tf_op jit(solution)/shard_map/all_gather | solution.py:158
  80.6 4.7 %collective-permute-start.7 = (bf16[6,6144]{1,0:T(8,128)(2,1)S(1)}, bf16[6,6144]{1,0:T(8,128)(2,1)S(1)}, u32[]{:S(2)}, u32[]{:S(2)}) collective-permute-start(bf16[6,6144]{1,0:T(8,128)(2,1)S(1)} %get-tuple-element.12), channel_id=1, source_target_pairs={{0,12},{4,0},{8,4},{12,8},{1,13},{5,1},{9,5},{13,9},{2,14},{6,2},{... | collective-permute-start | bytes 221192 | tf_op jit(solution)/shard_map/ppermute | solution.py:155
  82.1 6.1 %collective-permute-start.6 = (bf16[6,6144]{1,0:T(8,128)(2,1)S(1)}, bf16[6,6144]{1,0:T(8,128)(2,1)S(1)}, u32[]{:S(2)}, u32[]{:S(2)}) collective-permute-start(bf16[6,6144]{1,0:T(8,128)(2,1)S(1)} %get-tuple-element.13), channel_id=1, source_target_pairs={{0,8},{4,12},{8,0},{12,4},{1,9},{5,13},{9,1},{13,5},{2,10},{6,14},... | collective-permute-start | bytes 221192 | tf_op jit(solution)/shard_map/ppermute | solution.py:155
  83.7 5.8 %collective-permute-start.5 = (bf16[6,6144]{1,0:T(8,128)(2,1)S(1)}, bf16[6,6144]{1,0:T(8,128)(2,1)S(1)}, u32[]{:S(2)}, u32[]{:S(2)}) collective-permute-start(bf16[6,6144]{1,0:T(8,128)(2,1)S(1)} %get-tuple-element.14), channel_id=1, source_target_pairs={{0,4},{4,8},{8,12},{12,0},{1,5},{5,9},{9,13},{13,1},{2,6},{6,10},{... | collective-permute-start | bytes 221192 | tf_op jit(solution)/shard_map/ppermute | solution.py:155
  90.4 185.1 %reduce-scatter.4.cloned.1.call-start = ((), (), s32[]{:S(2)}) async-start(), calls=%async_computation.4 | async-start | bytes 1671168
  143.3 4.9 %copy-start.4 = (bf16[6144,256]{1,0:T(8,128)(2,1)S(1)}, bf16[6144,256]{1,0:T(8,128)(2,1)}, u32[]{:S(2)}) copy-start(bf16[6144,256]{1,0:T(8,128)(2,1)} %param.18) | copy-start | bytes 9437188
  155.6 8.9 %collective-permute-start.8 = (bf16[384,6144]{1,0:T(8,128)(2,1)}, bf16[384,6144]{1,0:T(8,128)(2,1)}, u32[]{:S(2)}, u32[]{:S(2)}) collective-permute-start(bf16[384,6144]{1,0:T(8,128)(2,1)} %convolution_convert_fusion), channel_id=1, source_target_pairs={{0,16},{16,0},{1,17},{17,1},{2,18},{18,2},{3,19},{19,3},{4,20},{20... | collective-permute-start | bytes 14155784 | tf_op jit(solution)/shard_map/ppermute | solution.py:163
  155.8 4.9 %copy-start.5 = (bf16[6144,256]{1,0:T(8,128)(2,1)S(1)}, bf16[6144,256]{1,0:T(8,128)(2,1)}, u32[]{:S(2)}) copy-start(bf16[6144,256]{1,0:T(8,128)(2,1)} %param.18) | copy-start | bytes 9437188
  168.3 2.1 copy-start.1
  175.7 7.5 %copy-start.6 = (bf16[6144,4]{0,1:T(4,128)(2,1)S(1)}, bf16[6144,4]{0,1:T(4,128)(2,1)}, u32[]{:S(2)}) copy-start(bf16[6144,4]{0,1:T(4,128)(2,1)} %param.16) | copy-start | bytes 147460
  175.7 54.3 %all-to-all-start.1 = ((bf16[16,24,4096]{2,1,0:T(8,128)(2,1)}), bf16[16,24,4096]{2,1,0:T(8,128)(2,1)}, u32[]{:S(2)}, u32[]{:S(2)}) async-start(bf16[16,24,4096]{2,1,0:T(8,128)(2,1)} %bitcast.88), calls=%async_computation.1 | async-start | bytes 6291456 | tf_op jit(solution)/shard_map/all_to_all | solution.py:169
  276.5 6.0 %collective-permute-start.9 = (bf16[6,6144]{1,0:T(8,128)(2,1)S(1)}, bf16[6,6144]{1,0:T(8,128)(2,1)S(1)}, u32[]{:S(2)}, u32[]{:S(2)}) collective-permute-start(bf16[6,6144]{1,0:T(8,128)(2,1)S(1)} %get-tuple-element.16), channel_id=1, source_target_pairs={{0,12},{4,0},{8,4},{12,8},{1,13},{5,1},{9,5},{13,9},{2,14},{6,2},{... | collective-permute-start | bytes 221192 | tf_op jit(solution)/shard_map/ppermute | solution.py:178
  279.2 6.9 %collective-permute-start.11 = (bf16[6,6144]{1,0:T(8,128)(2,1)S(1)}, bf16[6,6144]{1,0:T(8,128)(2,1)S(1)}, u32[]{:S(2)}, u32[]{:S(2)}) collective-permute-start(bf16[6,6144]{1,0:T(8,128)(2,1)S(1)} %get-tuple-element.17), channel_id=1, source_target_pairs={{0,4},{4,8},{8,12},{12,0},{1,5},{5,9},{9,13},{13,1},{2,6},{6,10},{... | collective-permute-start | bytes 221192 | tf_op jit(solution)/shard_map/ppermute | solution.py:178
  279.3 6.9 %collective-permute-start.10 = (bf16[6,6144]{1,0:T(8,128)(2,1)S(1)}, bf16[6,6144]{1,0:T(8,128)(2,1)S(1)}, u32[]{:S(2)}, u32[]{:S(2)}) collective-permute-start(bf16[6,6144]{1,0:T(8,128)(2,1)S(1)} %get-tuple-element.18), channel_id=1, source_target_pairs={{0,8},{4,12},{8,0},{12,4},{1,9},{5,13},{9,1},{13,5},{2,10},{6,14},... | collective-permute-start | bytes 221192 | tf_op jit(solution)/shard_map/ppermute | solution.py:178
Sparse Core Ops, SparseCore 0:
  90.6 52.7 all-gather.1
  171.9 103.5 reduce-scatter.3

commit v8 on v6

--- a/solution.py
+++ b/solution.py
@@ -40,9 +40,11 @@
     return (document, positions - doc_start)
 
 
-def expert_rows(rows, gate_weight, up_weight, down_weight):
-    gate_part = jnp.dot(rows, gate_weight, preferred_element_type=jnp.float32)
-    up_part = jnp.dot(rows, up_weight, preferred_element_type=jnp.float32)
+def expert_rows(rows, gate_up_weight, down_weight):
+    hidden = down_weight.shape[0]
+    both = jnp.dot(rows, gate_up_weight, preferred_element_type=jnp.float32)
+    gate_part = both[:, :hidden]
+    up_part = both[:, hidden:]
     activated = lax.optimization_barrier((jax.nn.silu(gate_part) * up_part).astype(jnp.bfloat16))
     return jnp.dot(activated, down_weight, preferred_element_type=jnp.float32).astype(jnp.bfloat16)
 
@@ -156,12 +158,13 @@
     ]
     arrived = jnp.concatenate(arrived, axis=0)
     rows = lax.all_gather(arrived, ("c", "y", "z"), axis=0, tiled=True)
+    gate_up_weight = jnp.concatenate([gate_weight, up_weight], axis=1)
     line_rows = rows.shape[0] // nc
     other_rows = lax.dynamic_slice_in_dim(rows, (1 - ci) * line_rows, line_rows, 0)
     own_rows = lax.dynamic_slice_in_dim(rows, ci * line_rows, line_rows, 0)
-    other_out = expert_rows(other_rows, gate_weight, up_weight, down_weight)
+    other_out = expert_rows(other_rows, gate_up_weight, down_weight)
     other_back = lax.ppermute(other_out, "c", core_swap)
-    own_out = expert_rows(own_rows, gate_weight, up_weight, down_weight)
+    own_out = expert_rows(own_rows, gate_up_weight, down_weight)
     summed = (own_out.astype(jnp.float32) + other_back.astype(jnp.float32)).astype(jnp.bfloat16)
 
     lines = summed.reshape(-1, experts * capacity, model_width)

time: 274 us -> 271 us (0.989)
  local copies, waits for them, and re-layouts: 4.93 us -> 10.9 us
  matrix products: 48.1 us -> 43.1 us
  waiting for transfers between devices: 160 us -> 156 us
    all_gather x1, waiting for transfers between devices: 52.9 us -> 46.9 us  [per_device(): rows = lax.all_gather(arrived, ('c', 'y', 'z'), axis=0, tiled=True)]
    dot_general x4 -> x2, matrix products: 17.2 us -> 12.3 us  [expert_rows(): both = jnp.dot(rows, gate_up_weight, preferred_element_type=jnp.float32)]
    unnamed x14 -> x13, local copies, waits for them, and re-layouts: 1.17 us -> 5.19 us
  transfers between devices with their start and end apart: 15 -> 15, of which waited for: 13 -> 14; matrix products, arithmetic and copies ran while one was open for 7% -> 9% of each run, Pallas kernels for 0% -> 0%
where the time goes in v8:
time: 271 us; the launch traced here: 270 us
  waiting for transfers between devices  156 us (58%)
  matrix products  43.1 us (16%)
  starting transfers between devices  28.7 us (11%)
  other arithmetic  17.7 us (7%)
  between operations  13.7 us (5%)
  local copies, waits for them, and re-layouts  10.9 us (4%)
    all_to_all x1, waiting for transfers between devices, per_device(): lax.all_to_all(lines, ('y', 'z'), split_axis=0, concat_axis=0, tiled=True)  70.9 us
    all_gather x1, waiting for transfers between devices, per_device(): rows = lax.all_gather(arrived, ('c', 'y', 'z'), axis=0, tiled=True)  46.9 us
    all_to_all x1, waiting for transfers between devices, per_device(): lax.all_to_all(blocks, ('x', 'y'), split_axis=0, concat_axis=0, tiled=True)  19.7 us
    dot_general x2, matrix products, expert_rows(): both = jnp.dot(rows, gate_up_weight, preferred_element_type=jnp.float32)  12.3 us
    dot_general x2, matrix products, expert_rows(): jnp.dot(activated, down_weight, preferred_element_type=jnp.float32)  9.52 us
    all_to_all x1, starting transfers between devices, per_device(): lax.all_to_all(lines, ('y', 'z'), split_axis=0, concat_axis=0, tiled=True)  7.51 us
    all_to_all x1, starting transfers between devices, per_device(): lax.all_to_all(blocks, ('x', 'y'), split_axis=0, concat_axis=0, tiled=True)  7.41 us
    ppermute x3, waiting for transfers between devices, per_device(): lax.ppermute(pair, 'z', [(i, (i - k) % nz) for i in range(nz)])  7.29 us
  transfers between devices with their start and end apart: 15, of which 14 were waited for; matrix products, arithmetic and copies ran while one was open for 9% of the time, Pallas kernels for 0%

profile of v8, /device:TPU:112, one launch (start us, length us, event | category | flops | bytes accessed | tf_op | source)
XLA Modules:
  0.0 269.8 jit_solution(7301786045554480277)
XLA Ops:
  6.6 1.0 reduce-window.8
  7.6 1.9 fusion.8
  9.5 0.7 fusion.47
  10.3 2.5 fusion.13
  13.8 1.3 collective-permute-start
  15.1 0.9 multiply_cosine_fusion.1
  16.1 4.4 %fusion.15 = f32[128,384]{0,1:T(8,128)S(1)} fusion(bf16[6144,384]{1,0:T(8,128)(2,1)} %param.11, bf16[128,6144]{1,0:T(8,128)(2,1)S(1)} %copy-done.1, f32[128]{0:T(128)S(1)} %add_rsqrt_fusion.1), kind=kOutput, calls=%fused_computation.28 | convolution fusion | flops 606339072 | bytes 6488576 | tf_op jit(solution)/shard_map/dot_general | solution.py:83
  21.2 1.0 copy.33
  22.3 1.6 subtract_convert_fusion
  23.9 0.8 select_bitcast_fusion.1
  24.9 1.2 collective-permute-done.1
  26.2 2.5 collective-permute-start.3
  28.8 3.7 %collective-permute-done.4 = bf16[2,2,128,128]{3,2,1,0:T(8,128)(2,1)S(1)} collective-permute-done((bf16[2,2,128,128]{3,2,1,0:T(8,128)(2,1)S(1)}, bf16[2,2,128,128]{3,2,1,0:T(8,128)(2,1)S(1)}, u32[]{:S(2)}, u32[]{:S(2)}) %collective-permute-start.4) | collective-permute-done | bytes 131104 | tf_op jit(solution)/shard_map/ppermute | solution.py:101
  32.5 1.6 collective-permute-done.3
  34.1 2.0 collective-permute-done.2
  36.9 1.9 fusion.74
  38.8 2.6 multiply_select_fusion
  41.4 2.5 fusion.11
  43.9 4.5 %fusion.1 = bf16[16,8,6144]{2,1,0:T(8,128)(2,1)} fusion(bf16[128,384]{0,1:T(8,128)(2,1)S(1)} %bitcast.93, bf16[384,6144]{1,0:T(8,128)(2,1)} %param.13), kind=kOutput, calls=%fused_computation.7 | convolution fusion | flops 604766208 | bytes 6389760 | tf_op jit(solution)/shard_map/dot_general | solution.py:127
  48.4 7.4 %all-to-all-start = ((bf16[16,8,6144]{2,1,0:T(8,128)(2,1)}), bf16[16,8,6144]{2,1,0:T(8,128)(2,1)}, u32[]{:S(2)}, u32[]{:S(2)}) async-start(bf16[16,8,6144]{2,1,0:T(8,128)(2,1)} %fusion.1), calls=%async_computation | async-start | bytes 3145728 | tf_op jit(solution)/shard_map/all_to_all | solution.py:130
  56.8 19.7 %all-to-all-done = bf16[16,8,6144]{2,1,0:T(8,128)(2,1)} async-done(((bf16[16,8,6144]{2,1,0:T(8,128)(2,1)}), bf16[16,8,6144]{2,1,0:T(8,128)(2,1)}, u32[]{:S(2)}, u32[]{:S(2)}) %all-to-all-start) | async-done | bytes 1572896 | tf_op jit(solution)/shard_map/all_to_all | solution.py:130
  76.5 1.6 convert_reduce_fusion
  78.2 1.1 multiply_reduce_fusion
  79.2 1.0 multiply_convert_fusion
  80.6 1.4 collective-permute-start.7
  82.1 1.7 collective-permute-start.6
  83.7 0.9 collective-permute-start.5
  85.3 2.9 %collective-permute-done.6 = bf16[6,6144]{1,0:T(8,128)(2,1)S(1)} collective-permute-done((bf16[6,6144]{1,0:T(8,128)(2,1)S(1)}, bf16[6,6144]{1,0:T(8,128)(2,1)S(1)}, u32[]{:S(2)}, u32[]{:S(2)}) %collective-permute-start.6) | collective-permute-done | bytes 73760 | tf_op jit(solution)/shard_map/ppermute | solution.py:157
  88.2 1.4 collective-permute-done.5
  89.5 0.9 pad_maximum_fusion
  90.5 4.0 %constant_dynamic-update-slice_fusion.1 = bf16[6144,512]{1,0:T(8,128)(2,1)} fusion(bf16[6144,256]{1,0:T(8,128)(2,1)} %param.17), kind=kLoop, calls=%fused_computation.93 | loop fusion | bytes 6291456
  94.5 2.0 constant_dynamic-update-slice_fusion
  96.4 46.9 %all-gather.2.cloned.1.call-done = bf16[768,6144]{1,0:T(8,128)(2,1)} async-done(((bf16[24,6144]{1,0:T(8,128)(2,1)}), bf16[768,6144]{1,0:T(8,128)(2,1)}) %all-gather.2.cloned.1.call-update) | async-done | bytes 9437200 | tf_op jit(solution)/shard_map/all_gather | solution.py:160
  143.3 6.2 %fusion.4 = f32[384,512]{1,0:T(8,128)S(1)} fusion(bf16[6144,512]{1,0:T(8,128)(2,1)} %constant_dynamic-update-slice_fusion, bf16[768,6144]{1,0:T(8,128)(2,1)} %all-gather.2.cloned.1.call-done, s32[]{:T(128)S(6)} %select_n.150), kind=kOutput, calls=%fused_computation.12 | convolution fusion | flops 2415919104 | bytes 11796484 | tf_op jit(solution)/shard_map/dot_general | solution.py:45
  149.6 3.5 %convolution_convert_fusion = bf16[384,6144]{1,0:T(8,128)(2,1)} fusion(bf16[384,256]{1,0:T(8,128)(2,1)S(1)} %fusion.17, bf16[256,6144]{1,0:T(8,128)(2,1)S(1)} %copy-done), kind=kOutput, calls=%fused_computation.4 | convolution fusion | flops 1210318848 | bytes 8060928 | tf_op jit(solution)/shard_map/dot_general | solution.py:49
  153.4 6.2 %fusion.6 = f32[384,512]{1,0:T(8,128)S(1)} fusion(bf16[6144,512]{1,0:T(8,128)(2,1)} %constant_dynamic-update-slice_fusion, bf16[768,6144]{1,0:T(8,128)(2,1)} %all-gather.2.cloned.1.call-done, s32[]{:T(128)S(6)} %select_n.149), kind=kOutput, calls=%fused_computation.14 | convolution fusion | flops 2415919104 | bytes 11796484 | tf_op jit(solution)/shard_map/dot_general | solution.py:45
  159.7 1.7 collective-permute-done.8
  161.4 6.0 %add_convert_fusion = bf16[384,6144]{1,0:T(8,128)(2,1)} fusion(bf16[384,6144]{1,0:T(8,128)(2,1)} %collective-permute-done.8, bf16[384,256]{1,0:T(8,128)(2,1)S(1)} %fusion.18, bf16[256,6144]{1,0:T(8,128)(2,1)S(1)} %copy-done), kind=kOutput, calls=%fused_computation.3 | convolution fusion | flops 1219756032 | bytes 12779520 | tf_op jit(solution)/shard_map/dot_general | solution.py:49
  167.4 7.5 %all-to-all-start.1 = ((bf16[16,24,6144]{2,1,0:T(8,128)(2,1)}), bf16[16,24,6144]{2,1,0:T(8,128)(2,1)}, u32[]{:S(2)}, u32[]{:S(2)}) async-start(bf16[16,24,6144]{2,1,0:T(8,128)(2,1)} %bitcast.85), calls=%async_computation.1 | async-start | bytes 9437184 | tf_op jit(solution)/shard_map/all_to_all | solution.py:172
  175.8 70.9 %all-to-all-done.1 = bf16[16,24,6144]{2,1,0:T(8,128)(2,1)} async-done(((bf16[16,24,6144]{2,1,0:T(8,128)(2,1)}), bf16[16,24,6144]{2,1,0:T(8,128)(2,1)}, u32[]{:S(2)}, u32[]{:S(2)}) %all-to-all-start.1) | async-done | bytes 4718624 | tf_op jit(solution)/shard_map/all_to_all | solution.py:172
  246.7 3.9 %reduce_sum.112 = bf16[24,6144]{1,0:T(8,128)(2,1)} reduce(bf16[16,24,6144]{2,1,0:T(8,128)(2,1)} %all-to-all-done.1, bf16[]{:T(256)} %constant.129.clone.1), dimensions={0}, to_apply=%region_15.16 | reduce | flops 2211840 | bytes 5013506 | tf_op jit(solution)/shard_map/reduce_sum | solution.py:171
  250.6 1.2 slice_bitcast_fusion
  251.8 1.5 collective-permute-start.11
  253.2 2.7 collective-permute-start.10
  255.9 1.5 collective-permute-start.9
  257.4 1.3 collective-permute-done.11
  258.7 1.1 collective-permute-done.10
  260.5 2.5 fusion.3
  (59 shorter events, 7.4 us)
Async XLA Ops:
  6.5 143.1 %copy-start = (bf16[256,6144]{1,0:T(8,128)(2,1)S(1)}, bf16[256,6144]{1,0:T(8,128)(2,1)}, u32[]{:S(2)}) copy-start(bf16[256,6144]{1,0:T(8,128)(2,1)} %param.19) | copy-start | bytes 9437188
  7.6 8.5 %copy-start.1 = (bf16[128,6144]{1,0:T(8,128)(2,1)S(1)}, bf16[128,6144]{1,0:T(8,128)(2,1)}, u32[]{:S(2)}) copy-start(bf16[128,6144]{1,0:T(8,128)(2,1)} %param.10) | copy-start | bytes 4718596
  13.8 10.2 %collective-permute-start = (bf16[128,128]{1,0:T(8,128)(2,1)}, bf16[128,128]{1,0:T(8,128)(2,1)}, u32[]{:S(2)}, u32[]{:S(2)}) collective-permute-start(bf16[128,128]{1,0:T(8,128)(2,1)} %fusion.34), channel_id=1, source_target_pairs={{0,1},{1,0},{2,3},{3,2},{4,5},{5,4},{6,7},{7,6},{8,9},{9,8},{10,11... | collective-permute-start | bytes 98312 | tf_op jit(solution)/shard_map/ppermute | solution.py:92
  24.7 1.3 collective-permute-start.1
  26.1 6.4 %collective-permute-start.4 = (bf16[2,2,128,128]{3,2,1,0:T(8,128)(2,1)S(1)}, bf16[2,2,128,128]{3,2,1,0:T(8,128)(2,1)S(1)}, u32[]{:S(2)}, u32[]{:S(2)}) collective-permute-start(bf16[2,2,128,128]{3,2,1,0:T(8,128)(2,1)S(1)} %maximum_select_fusion.1), channel_id=1, source_target_pairs={{0,32},{32,64},{64,96},{96,0},{1,33},{33,65},{65,97},{97,1},{2,34}... | collective-permute-start | bytes 393224 | tf_op jit(solution)/shard_map/ppermute | solution.py:101
  26.2 8.0 %collective-permute-start.3 = (bf16[2,2,128,128]{3,2,1,0:T(8,128)(2,1)S(1)}, bf16[2,2,128,128]{3,2,1,0:T(8,128)(2,1)S(1)}, u32[]{:S(2)}, u32[]{:S(2)}) collective-permute-start(bf16[2,2,128,128]{3,2,1,0:T(8,128)(2,1)S(1)} %maximum_select_fusion.1), channel_id=1, source_target_pairs={{0,64},{32,96},{64,0},{96,32},{1,65},{33,97},{65,1},{97,33},{2,66}... | collective-permute-start | bytes 393224 | tf_op jit(solution)/shard_map/ppermute | solution.py:101
  28.6 7.5 %collective-permute-start.2 = (bf16[2,2,128,128]{3,2,1,0:T(8,128)(2,1)S(1)}, bf16[2,2,128,128]{3,2,1,0:T(8,128)(2,1)S(1)}, u32[]{:S(2)}, u32[]{:S(2)}) collective-permute-start(bf16[2,2,128,128]{3,2,1,0:T(8,128)(2,1)S(1)} %maximum_select_fusion.1), channel_id=1, source_target_pairs={{0,96},{32,0},{64,32},{96,64},{1,97},{33,1},{65,33},{97,65},{2,98}... | collective-permute-start | bytes 393224 | tf_op jit(solution)/shard_map/ppermute | solution.py:101
  48.4 7.5 %copy-start.3 = (s32[8,2]{0,1:T(2,128)S(1)}, s32[8,2]{0,1:T(2,128)}, u32[]{:S(2)}) copy-start(s32[8,2]{0,1:T(2,128)} %param.15) | copy-start | bytes 196
  48.4 28.1 %all-to-all-start = ((bf16[16,8,6144]{2,1,0:T(8,128)(2,1)}), bf16[16,8,6144]{2,1,0:T(8,128)(2,1)}, u32[]{:S(2)}, u32[]{:S(2)}) async-start(bf16[16,8,6144]{2,1,0:T(8,128)(2,1)} %fusion.1), calls=%async_computation | async-start | bytes 3145728 | tf_op jit(solution)/shard_map/all_to_all | solution.py:130
  55.8 87.5 %all-gather.2.cloned.1.call-start = ((), (), s32[]{:S(2)}) async-start(), calls=%async_computation.2 | async-start | bytes 9732096 | tf_op jit(solution)/shard_map/all_gather | solution.py:160
  80.6 4.7 %collective-permute-start.7 = (bf16[6,6144]{1,0:T(8,128)(2,1)S(1)}, bf16[6,6144]{1,0:T(8,128)(2,1)S(1)}, u32[]{:S(2)}, u32[]{:S(2)}) collective-permute-start(bf16[6,6144]{1,0:T(8,128)(2,1)S(1)} %get-tuple-element.12), channel_id=1, source_target_pairs={{0,12},{4,0},{8,4},{12,8},{1,13},{5,1},{9,5},{13,9},{2,14},{6,2},{... | collective-permute-start | bytes 221192 | tf_op jit(solution)/shard_map/ppermute | solution.py:157
  82.1 6.1 %collective-permute-start.6 = (bf16[6,6144]{1,0:T(8,128)(2,1)S(1)}, bf16[6,6144]{1,0:T(8,128)(2,1)S(1)}, u32[]{:S(2)}, u32[]{:S(2)}) collective-permute-start(bf16[6,6144]{1,0:T(8,128)(2,1)S(1)} %get-tuple-element.13), channel_id=1, source_target_pairs={{0,8},{4,12},{8,0},{12,4},{1,9},{5,13},{9,1},{13,5},{2,10},{6,14},... | collective-permute-start | bytes 221192 | tf_op jit(solution)/shard_map/ppermute | solution.py:157
  83.7 5.8 %collective-permute-start.5 = (bf16[6,6144]{1,0:T(8,128)(2,1)S(1)}, bf16[6,6144]{1,0:T(8,128)(2,1)S(1)}, u32[]{:S(2)}, u32[]{:S(2)}) collective-permute-start(bf16[6,6144]{1,0:T(8,128)(2,1)S(1)} %get-tuple-element.14), channel_id=1, source_target_pairs={{0,4},{4,8},{8,12},{12,0},{1,5},{5,9},{9,13},{13,1},{2,6},{6,10},{... | collective-permute-start | bytes 221192 | tf_op jit(solution)/shard_map/ppermute | solution.py:157
  90.4 4.0 %copy-start.2 = (bf16[6144,256]{1,0:T(8,128)(2,1)S(1)}, bf16[6144,256]{1,0:T(8,128)(2,1)}, u32[]{:S(2)}) copy-start(bf16[6144,256]{1,0:T(8,128)(2,1)} %param.18) | copy-start | bytes 9437188
  153.2 8.3 %collective-permute-start.8 = (bf16[384,6144]{1,0:T(8,128)(2,1)}, bf16[384,6144]{1,0:T(8,128)(2,1)}, u32[]{:S(2)}, u32[]{:S(2)}) collective-permute-start(bf16[384,6144]{1,0:T(8,128)(2,1)} %convolution_convert_fusion), channel_id=1, source_target_pairs={{0,16},{16,0},{1,17},{17,1},{2,18},{18,2},{3,19},{19,3},{4,20},{20... | collective-permute-start | bytes 14155784 | tf_op jit(solution)/shard_map/ppermute | solution.py:166
  167.4 7.5 %copy-start.4 = (bf16[6144,4]{0,1:T(4,128)(2,1)S(1)}, bf16[6144,4]{0,1:T(4,128)(2,1)}, u32[]{:S(2)}) copy-start(bf16[6144,4]{0,1:T(4,128)(2,1)} %param.16) | copy-start | bytes 147460
  167.4 79.3 %all-to-all-start.1 = ((bf16[16,24,6144]{2,1,0:T(8,128)(2,1)}), bf16[16,24,6144]{2,1,0:T(8,128)(2,1)}, u32[]{:S(2)}, u32[]{:S(2)}) async-start(bf16[16,24,6144]{2,1,0:T(8,128)(2,1)} %bitcast.85), calls=%async_computation.1 | async-start | bytes 9437184 | tf_op jit(solution)/shard_map/all_to_all | solution.py:172
  251.8 6.9 %collective-permute-start.11 = (bf16[6,6144]{1,0:T(8,128)(2,1)S(1)}, bf16[6,6144]{1,0:T(8,128)(2,1)S(1)}, u32[]{:S(2)}, u32[]{:S(2)}) collective-permute-start(bf16[6,6144]{1,0:T(8,128)(2,1)S(1)} %get-tuple-element.16), channel_id=1, source_target_pairs={{0,4},{4,8},{8,12},{12,0},{1,5},{5,9},{9,13},{13,1},{2,6},{6,10},{... | collective-permute-start | bytes 221192 | tf_op jit(solution)/shard_map/ppermute | solution.py:181
  253.2 6.6 %collective-permute-start.10 = (bf16[6,6144]{1,0:T(8,128)(2,1)S(1)}, bf16[6,6144]{1,0:T(8,128)(2,1)S(1)}, u32[]{:S(2)}, u32[]{:S(2)}) collective-permute-start(bf16[6,6144]{1,0:T(8,128)(2,1)S(1)} %get-tuple-element.17), channel_id=1, source_target_pairs={{0,8},{4,12},{8,0},{12,4},{1,9},{5,13},{9,1},{13,5},{2,10},{6,14},... | collective-permute-start | bytes 221192 | tf_op jit(solution)/shard_map/ppermute | solution.py:181
  255.9 4.6 %collective-permute-start.9 = (bf16[6,6144]{1,0:T(8,128)(2,1)S(1)}, bf16[6,6144]{1,0:T(8,128)(2,1)S(1)}, u32[]{:S(2)}, u32[]{:S(2)}) collective-permute-start(bf16[6,6144]{1,0:T(8,128)(2,1)S(1)} %get-tuple-element.18), channel_id=1, source_target_pairs={{0,12},{4,0},{8,4},{12,8},{1,13},{5,1},{9,5},{13,9},{2,14},{6,2},{... | collective-permute-start | bytes 221192 | tf_op jit(solution)/shard_map/ppermute | solution.py:181
Sparse Core Ops, SparseCore 0:
  90.6 52.7 all-gather.1

commit v9 on v8

--- a/solution.py
+++ b/solution.py
@@ -147,16 +147,19 @@
     slot_range = jnp.arange(capacity, dtype=jnp.int32)
     hits = (slot[:, :, None] == slot_range) & (names[:, :, None] > 0)
     shift = (xi + jnp.arange(nx, dtype=jnp.int32)) % nx
-    hits = jnp.take(hits, shift, axis=1)
-    gate_cols = jnp.take(gate_cols, shift, axis=1)
     send = jnp.einsum(
-        "rec,rd->ecd", hits.astype(jnp.bfloat16), normed, preferred_element_type=jnp.float32
+        "rec,rd->ecd",
+        jnp.take(hits, shift, axis=1).astype(jnp.bfloat16),
+        normed,
+        preferred_element_type=jnp.float32,
     ).astype(jnp.bfloat16)
 
     arrived = [send[0]] + [
         lax.ppermute(send[k], "x", [(i, (i + k) % nx) for i in range(nx)]) for k in range(1, nx)
     ]
-    arrived = jnp.concatenate(arrived, axis=0)
+    arrived = jnp.stack(arrived)
+    arrived = jnp.take(arrived, (xi - jnp.arange(nx, dtype=jnp.int32)) % nx, axis=0)
+    arrived = arrived.reshape(experts * capacity, model_width)
     rows = lax.all_gather(arrived, ("c", "y", "z"), axis=0, tiled=True)
     gate_up_weight = jnp.concatenate([gate_weight, up_weight], axis=1)
     line_rows = rows.shape[0] // nc
@@ -167,25 +170,15 @@
     own_out = expert_rows(own_rows, gate_up_weight, down_weight)
     summed = (own_out.astype(jnp.float32) + other_back.astype(jnp.float32)).astype(jnp.bfloat16)
 
-    lines = summed.reshape(-1, experts * capacity, model_width)
-    summed = jnp.sum(
-        lax.all_to_all(lines, ("y", "z"), split_axis=0, concat_axis=0, tiled=True).astype(
-            jnp.float32
-        ),
-        axis=0,
-    )
-    summed = summed.reshape(experts, capacity, model_width).astype(jnp.bfloat16)
-    returned = jnp.stack(
-        [summed[0]]
-        + [
-            lax.ppermute(summed[k], "x", [(i, (i - k) % nx) for i in range(nx)])
-            for k in range(1, nx)
-        ]
+    lines = summed.reshape(-1, capacity, model_width)
+    spread = lax.all_to_all(lines, ("y", "z", "x"), split_axis=0, concat_axis=0, tiled=True)
+    returned = jnp.sum(
+        spread.reshape(-1, experts, capacity, model_width).astype(jnp.float32), axis=0
     )
 
     weights = jnp.where(hits, gate_cols[:, :, None], 0.0)
     moe = jnp.einsum(
-        "rec,ecd->rd", weights, returned.astype(jnp.float32), precision=lax.Precision.HIGHEST
+        "rec,ecd->rd", weights, returned, precision=lax.Precision.HIGHEST
     )
     return (hidden_state + moe).astype(jnp.bfloat16)
 

time: 271 us -> 290 us (1.070); the launches traced: 270 us -> 285 us
  local copies, waits for them, and re-layouts: 10.9 us -> 21.1 us
  waiting for transfers between devices: 156 us -> 160 us
    reshape x0 -> x1, local copies, waits for them, and re-layouts: none -> 7.71 us  [per_device(): lines = summed.reshape(-1, capacity, model_width)]
    all_to_all x1, waiting for transfers between devices: 70.9 us -> 78.5 us  [per_device(): lax.all_to_all(lines, ('y', 'z', 'x'), split_axis=0, concat_axis=0, tiled...]
    ppermute x3 -> x0, starting transfers between devices: 5.6 us -> none  [per_device(): lax.ppermute(summed[k], 'x', [(i, (i - k) % nx) for i in range(nx)])]
    gather x2 -> x3, local copies, waits for them, and re-layouts: 1.13 us -> 4.69 us  [the longest x2 4.13 us: per_device(): jnp.take(arrived, (xi - jnp.arange(nx, dtype=jnp.int32)) % nx, axis=0)]
    all_to_all x1, starting transfers between devices: 7.51 us -> 10.8 us  [per_device(): lax.all_to_all(lines, ('y', 'z', 'x'), split_axis=0, concat_axis=0, tiled...]
    ppermute x3 -> x0, waiting for transfers between devices: 3.09 us -> none  [per_device(): lax.ppermute(summed[k], 'x', [(i, (i - k) % nx) for i in range(nx)])]
  transfers between devices with their start and end apart: 15 -> 12, of which waited for: 14 -> 11; matrix products, arithmetic and copies ran while one was open for 9% -> 8% of each run, Pallas kernels for 0% -> 0%
where the time goes in v9:
time: 290 us; the launch traced here: 285 us
  waiting for transfers between devices  160 us (55%)
  matrix products  43.9 us (15%)
  starting transfers between devices  26.4 us (9%)
  local copies, waits for them, and re-layouts  21.1 us (7%)
  other arithmetic  19.9 us (7%)
  between operations  13.7 us (5%)
    all_to_all x1, waiting for transfers between devices, per_device(): lax.all_to_all(lines, ('y', 'z', 'x'), split_axis=0, concat_axis=0, tiled...  78.5 us
    all_gather x1, waiting for transfers between devices, per_device(): rows = lax.all_gather(arrived, ('c', 'y', 'z'), axis=0, tiled=True)  46.9 us
    all_to_all x1, waiting for transfers between devices, per_device(): lax.all_to_all(blocks, ('x', 'y'), split_axis=0, concat_axis=0, tiled=True)  19.5 us
    dot_general x2, matrix products, expert_rows(): both = jnp.dot(rows, gate_up_weight, preferred_element_type=jnp.float32)  12.3 us
    all_to_all x1, starting transfers between devices, per_device(): lax.all_to_all(lines, ('y', 'z', 'x'), split_axis=0, concat_axis=0, tiled...  10.8 us
    dot_general x2, matrix products, expert_rows(): jnp.dot(activated, down_weight, preferred_element_type=jnp.float32)  9.57 us
    reshape x1, local copies, waits for them, and re-layouts, per_device(): lines = summed.reshape(-1, capacity, model_width)  7.71 us
    all_to_all x1, starting transfers between devices, per_device(): lax.all_to_all(blocks, ('x', 'y'), split_axis=0, concat_axis=0, tiled=True)  7.41 us
  transfers between devices with their start and end apart: 12, of which 11 were waited for; matrix products, arithmetic and copies ran while one was open for 8% of the time, Pallas kernels for 0%

profile of v9, /device:TPU:112, one launch (start us, length us, event | category | flops | bytes accessed | tf_op | source)
XLA Modules:
  0.0 285.0 jit_solution(3154981503667748879)
XLA Ops:
  6.6 1.0 reduce-window.8
  7.6 1.9 fusion.8
  9.5 0.7 fusion.36
  10.3 2.5 fusion.13
  13.1 0.7 fusion.27
  13.8 1.3 collective-permute-start
  15.1 0.9 multiply_cosine_fusion.1
  16.1 4.4 %fusion.15 = f32[128,384]{0,1:T(8,128)S(1)} fusion(bf16[6144,384]{1,0:T(8,128)(2,1)} %param.11, bf16[128,6144]{1,0:T(8,128)(2,1)S(1)} %copy-done.1, f32[128]{0:T(128)S(1)} %add_rsqrt_fusion.1), kind=kOutput, calls=%fused_computation.29 | convolution fusion | flops 606339072 | bytes 6488576 | tf_op jit(solution)/shard_map/dot_general | solution.py:83
  21.2 1.0 copy.33
  22.3 1.6 subtract_convert_fusion
  23.9 0.8 select_bitcast_fusion.1
  24.9 1.2 collective-permute-done.1
  26.2 2.5 collective-permute-start.3
  28.8 3.7 %collective-permute-done.4 = bf16[2,2,128,128]{3,2,1,0:T(8,128)(2,1)S(1)} collective-permute-done((bf16[2,2,128,128]{3,2,1,0:T(8,128)(2,1)S(1)}, bf16[2,2,128,128]{3,2,1,0:T(8,128)(2,1)S(1)}, u32[]{:S(2)}, u32[]{:S(2)}) %collective-permute-start.4) | collective-permute-done | bytes 131104 | tf_op jit(solution)/shard_map/ppermute | solution.py:101
  32.5 1.6 collective-permute-done.3
  34.1 2.0 collective-permute-done.2
  36.2 0.7 fusion.63
  36.9 1.9 fusion.66
  38.8 2.6 multiply_select_fusion
  41.4 2.5 fusion.11
  43.9 4.5 %fusion.1 = bf16[16,8,6144]{2,1,0:T(8,128)(2,1)} fusion(bf16[128,384]{0,1:T(8,128)(2,1)S(1)} %bitcast.86, bf16[384,6144]{1,0:T(8,128)(2,1)} %param.13), kind=kOutput, calls=%fused_computation.8 | convolution fusion | flops 604766208 | bytes 6389760 | tf_op jit(solution)/shard_map/dot_general | solution.py:127
  48.4 7.4 %all-to-all-start = ((bf16[16,8,6144]{2,1,0:T(8,128)(2,1)}), bf16[16,8,6144]{2,1,0:T(8,128)(2,1)}, u32[]{:S(2)}, u32[]{:S(2)}) async-start(bf16[16,8,6144]{2,1,0:T(8,128)(2,1)} %fusion.1), calls=%async_computation | async-start | bytes 3145728 | tf_op jit(solution)/shard_map/all_to_all | solution.py:130
  57.0 19.5 %all-to-all-done = bf16[16,8,6144]{2,1,0:T(8,128)(2,1)} async-done(((bf16[16,8,6144]{2,1,0:T(8,128)(2,1)}), bf16[16,8,6144]{2,1,0:T(8,128)(2,1)}, u32[]{:S(2)}, u32[]{:S(2)}) %all-to-all-start) | async-done | bytes 1572896 | tf_op jit(solution)/shard_map/all_to_all | solution.py:130
  76.5 1.6 convert_reduce_fusion.1
  78.2 1.1 multiply_reduce_fusion
  79.2 1.0 multiply_convert_fusion
  80.6 1.4 collective-permute-start.7
  82.1 1.7 collective-permute-start.6
  83.7 0.9 collective-permute-start.5
  85.3 2.9 %collective-permute-done.6 = bf16[6,6144]{1,0:T(8,128)(2,1)S(1)} collective-permute-done((bf16[6,6144]{1,0:T(8,128)(2,1)S(1)}, bf16[6,6144]{1,0:T(8,128)(2,1)S(1)}, u32[]{:S(2)}, u32[]{:S(2)}) %collective-permute-start.6) | collective-permute-done | bytes 73760 | tf_op jit(solution)/shard_map/ppermute | solution.py:158
  88.2 1.4 collective-permute-done.5
  89.6 0.9 pad_maximum_fusion
  90.4 2.3 gather_fusion.1
  92.7 1.8 gather.12
  94.5 1.8 broadcast_select_fusion
  96.4 4.0 %constant_dynamic-update-slice_fusion.1 = bf16[6144,512]{1,0:T(8,128)(2,1)} fusion(bf16[6144,256]{1,0:T(8,128)(2,1)} %param.17), kind=kLoop, calls=%fused_computation.83 | loop fusion | bytes 6291456
  100.4 2.0 constant_dynamic-update-slice_fusion
  102.3 46.9 %all-gather.2.cloned.1.call-done = bf16[768,6144]{1,0:T(8,128)(2,1)} async-done(((bf16[24,6144]{1,0:T(8,128)(2,1)}), bf16[768,6144]{1,0:T(8,128)(2,1)}) %all-gather.2.cloned.1.call-update) | async-done | bytes 9437200 | tf_op jit(solution)/shard_map/all_gather | solution.py:163
  149.2 6.2 %fusion.4 = f32[384,512]{1,0:T(8,128)S(1)} fusion(bf16[6144,512]{1,0:T(8,128)(2,1)} %constant_dynamic-update-slice_fusion, bf16[768,6144]{1,0:T(8,128)(2,1)} %all-gather.2.cloned.1.call-done, s32[]{:T(128)S(6)} %select_n.179), kind=kOutput, calls=%fused_computation.13 | convolution fusion | flops 2415919104 | bytes 11796484 | tf_op jit(solution)/shard_map/dot_general | solution.py:45
  155.5 3.5 %convolution_convert_fusion = bf16[384,6144]{1,0:T(8,128)(2,1)} fusion(bf16[384,256]{1,0:T(8,128)(2,1)S(1)} %fusion.17, bf16[256,6144]{1,0:T(8,128)(2,1)S(1)} %copy-done), kind=kOutput, calls=%fused_computation.5 | convolution fusion | flops 1210318848 | bytes 8060928 | tf_op jit(solution)/shard_map/dot_general | solution.py:49
  159.3 6.2 %fusion.6 = f32[384,512]{1,0:T(8,128)S(1)} fusion(bf16[6144,512]{1,0:T(8,128)(2,1)} %constant_dynamic-update-slice_fusion, bf16[768,6144]{1,0:T(8,128)(2,1)} %all-gather.2.cloned.1.call-done, s32[]{:T(128)S(6)} %select_n.178), kind=kOutput, calls=%fused_computation.15 | convolution fusion | flops 2415919104 | bytes 11796484 | tf_op jit(solution)/shard_map/dot_general | solution.py:45
  165.6 1.7 collective-permute-done.8
  167.3 6.0 %add_convert_fusion = bf16[384,6144]{1,0:T(8,128)(2,1)} fusion(bf16[384,6144]{1,0:T(8,128)(2,1)} %collective-permute-done.8, bf16[384,256]{1,0:T(8,128)(2,1)S(1)} %fusion.18, bf16[256,6144]{1,0:T(8,128)(2,1)S(1)} %copy-done), kind=kOutput, calls=%fused_computation.4 | convolution fusion | flops 1219756032 | bytes 12779520 | tf_op jit(solution)/shard_map/dot_general | solution.py:49
  173.3 7.7 %reshape.514 = bf16[64,6,6144]{2,1,0:T(8,128)(2,1)} reshape(bf16[384,6144]{1,0:T(8,128)(2,1)} %add_convert_fusion) | data formatting | bytes 9437184 | tf_op jit(solution)/shard_map/reshape | solution.py:173
  181.1 10.8 %all-to-all-start.1 = ((bf16[64,6,6144]{2,1,0:T(8,128)(2,1)}), bf16[64,6,6144]{2,1,0:T(8,128)(2,1)}, u32[]{:S(2)}, u32[]{:S(2)}) async-start(bf16[64,6,6144]{2,1,0:T(8,128)(2,1)} %reshape.514), calls=%async_computation.1 | async-start | bytes 12582912 | tf_op jit(solution)/shard_map/all_to_all | solution.py:174
  192.2 78.5 %all-to-all-done.1 = bf16[64,6,6144]{2,1,0:T(8,128)(2,1)} async-done(((bf16[64,6,6144]{2,1,0:T(8,128)(2,1)}), bf16[64,6,6144]{2,1,0:T(8,128)(2,1)}, u32[]{:S(2)}, u32[]{:S(2)}) %all-to-all-start.1) | async-done | bytes 4718624 | tf_op jit(solution)/shard_map/all_to_all | solution.py:174
  270.6 4.4 %convert_reduce_fusion = f32[4,6,6144]{2,1,0:T(8,128)S(1)} fusion(bf16[16,4,6,6144]{3,2,1,0:T(8,128)(2,1)} %bitcast.36), kind=kLoop, calls=%fused_computation.3 | loop fusion | flops 4571136 | bytes 5308416 | tf_op jit(solution)/shard_map/reduce_sum | solution.py:175
  275.0 3.2 %fusion.3 = bf16[8,6144]{1,0:T(8,128)(2,1)} fusion(f32[4,6,6144]{2,1,0:T(8,128)S(1)} %convert_reduce_fusion, f32[8,6144]{1,0:T(8,128)S(1)} %convert_reduce_fusion.1, bf16[128,6144]{1,0:T(8,128)(2,1)} %param.10, s32[]{:T(128)S(6)} %select_n.152, f32[8,4]{0,1:T(4,128)S(1)} %select_reduce_fusion, s32[8,4]{0,1:T(4,128)S(1)} %convert_subtract_fusion, ...), kind=kOutput, calls=%fused_computation.12 | convolution fusion | flops 14352960 | bytes 983332 | tf_op jit(solution)/shard_map/rec,ecd->rd/dot_general | solution.py:180
  (59 shorter events, 4.8 us)
Async XLA Ops:
  6.5 149.0 %copy-start = (bf16[256,6144]{1,0:T(8,128)(2,1)S(1)}, bf16[256,6144]{1,0:T(8,128)(2,1)}, u32[]{:S(2)}) copy-start(bf16[256,6144]{1,0:T(8,128)(2,1)} %param.19) | copy-start | bytes 9437188
  7.6 8.5 %copy-start.1 = (bf16[128,6144]{1,0:T(8,128)(2,1)S(1)}, bf16[128,6144]{1,0:T(8,128)(2,1)}, u32[]{:S(2)}) copy-start(bf16[128,6144]{1,0:T(8,128)(2,1)} %param.10) | copy-start | bytes 4718596
  13.8 10.2 %collective-permute-start = (bf16[128,128]{1,0:T(8,128)(2,1)}, bf16[128,128]{1,0:T(8,128)(2,1)}, u32[]{:S(2)}, u32[]{:S(2)}) collective-permute-start(bf16[128,128]{1,0:T(8,128)(2,1)} %fusion.27), channel_id=1, source_target_pairs={{0,1},{1,0},{2,3},{3,2},{4,5},{5,4},{6,7},{7,6},{8,9},{9,8},{10,11... | collective-permute-start | bytes 98312 | tf_op jit(solution)/shard_map/ppermute | solution.py:92
  24.7 1.3 collective-permute-start.1
  26.1 6.4 %collective-permute-start.4 = (bf16[2,2,128,128]{3,2,1,0:T(8,128)(2,1)S(1)}, bf16[2,2,128,128]{3,2,1,0:T(8,128)(2,1)S(1)}, u32[]{:S(2)}, u32[]{:S(2)}) collective-permute-start(bf16[2,2,128,128]{3,2,1,0:T(8,128)(2,1)S(1)} %maximum_select_fusion.1), channel_id=1, source_target_pairs={{0,32},{32,64},{64,96},{96,0},{1,33},{33,65},{65,97},{97,1},{2,34}... | collective-permute-start | bytes 393224 | tf_op jit(solution)/shard_map/ppermute | solution.py:101
  26.2 8.0 %collective-permute-start.3 = (bf16[2,2,128,128]{3,2,1,0:T(8,128)(2,1)S(1)}, bf16[2,2,128,128]{3,2,1,0:T(8,128)(2,1)S(1)}, u32[]{:S(2)}, u32[]{:S(2)}) collective-permute-start(bf16[2,2,128,128]{3,2,1,0:T(8,128)(2,1)S(1)} %maximum_select_fusion.1), channel_id=1, source_target_pairs={{0,64},{32,96},{64,0},{96,32},{1,65},{33,97},{65,1},{97,33},{2,66}... | collective-permute-start | bytes 393224 | tf_op jit(solution)/shard_map/ppermute | solution.py:101
  28.6 7.5 %collective-permute-start.2 = (bf16[2,2,128,128]{3,2,1,0:T(8,128)(2,1)S(1)}, bf16[2,2,128,128]{3,2,1,0:T(8,128)(2,1)S(1)}, u32[]{:S(2)}, u32[]{:S(2)}) collective-permute-start(bf16[2,2,128,128]{3,2,1,0:T(8,128)(2,1)S(1)} %maximum_select_fusion.1), channel_id=1, source_target_pairs={{0,96},{32,0},{64,32},{96,64},{1,97},{33,1},{65,33},{97,65},{2,98}... | collective-permute-start | bytes 393224 | tf_op jit(solution)/shard_map/ppermute | solution.py:101
  48.4 7.6 %copy-start.3 = (s32[8,2]{0,1:T(2,128)S(1)}, s32[8,2]{0,1:T(2,128)}, u32[]{:S(2)}) copy-start(s32[8,2]{0,1:T(2,128)} %param.15) | copy-start | bytes 196
  48.4 28.1 %all-to-all-start = ((bf16[16,8,6144]{2,1,0:T(8,128)(2,1)}), bf16[16,8,6144]{2,1,0:T(8,128)(2,1)}, u32[]{:S(2)}, u32[]{:S(2)}) async-start(bf16[16,8,6144]{2,1,0:T(8,128)(2,1)} %fusion.1), calls=%async_computation | async-start | bytes 3145728 | tf_op jit(solution)/shard_map/all_to_all | solution.py:130
  55.8 93.4 %all-gather.2.cloned.1.call-start = ((), (), s32[]{:S(2)}) async-start(), calls=%async_computation.2 | async-start | bytes 9732096 | tf_op jit(solution)/shard_map/all_gather | solution.py:163
  80.6 4.7 %collective-permute-start.7 = (bf16[6,6144]{1,0:T(8,128)(2,1)S(1)}, bf16[6,6144]{1,0:T(8,128)(2,1)S(1)}, u32[]{:S(2)}, u32[]{:S(2)}) collective-permute-start(bf16[6,6144]{1,0:T(8,128)(2,1)S(1)} %get-tuple-element.12), channel_id=1, source_target_pairs={{0,12},{4,0},{8,4},{12,8},{1,13},{5,1},{9,5},{13,9},{2,14},{6,2},{... | collective-permute-start | bytes 221192 | tf_op jit(solution)/shard_map/ppermute | solution.py:158
  82.1 6.1 %collective-permute-start.6 = (bf16[6,6144]{1,0:T(8,128)(2,1)S(1)}, bf16[6,6144]{1,0:T(8,128)(2,1)S(1)}, u32[]{:S(2)}, u32[]{:S(2)}) collective-permute-start(bf16[6,6144]{1,0:T(8,128)(2,1)S(1)} %get-tuple-element.13), channel_id=1, source_target_pairs={{0,8},{4,12},{8,0},{12,4},{1,9},{5,13},{9,1},{13,5},{2,10},{6,14},... | collective-permute-start | bytes 221192 | tf_op jit(solution)/shard_map/ppermute | solution.py:158
  83.7 5.8 %collective-permute-start.5 = (bf16[6,6144]{1,0:T(8,128)(2,1)S(1)}, bf16[6,6144]{1,0:T(8,128)(2,1)S(1)}, u32[]{:S(2)}, u32[]{:S(2)}) collective-permute-start(bf16[6,6144]{1,0:T(8,128)(2,1)S(1)} %get-tuple-element.14), channel_id=1, source_target_pairs={{0,4},{4,8},{8,12},{12,0},{1,5},{5,9},{9,13},{13,1},{2,6},{6,10},{... | collective-permute-start | bytes 221192 | tf_op jit(solution)/shard_map/ppermute | solution.py:158
  96.3 4.0 %copy-start.2 = (bf16[6144,256]{1,0:T(8,128)(2,1)S(1)}, bf16[6144,256]{1,0:T(8,128)(2,1)}, u32[]{:S(2)}) copy-start(bf16[6144,256]{1,0:T(8,128)(2,1)} %param.18) | copy-start | bytes 9437188
  159.0 8.3 %collective-permute-start.8 = (bf16[384,6144]{1,0:T(8,128)(2,1)}, bf16[384,6144]{1,0:T(8,128)(2,1)}, u32[]{:S(2)}, u32[]{:S(2)}) collective-permute-start(bf16[384,6144]{1,0:T(8,128)(2,1)} %convolution_convert_fusion), channel_id=1, source_target_pairs={{0,16},{16,0},{1,17},{17,1},{2,18},{18,2},{3,19},{19,3},{4,20},{20... | collective-permute-start | bytes 14155784 | tf_op jit(solution)/shard_map/ppermute | solution.py:169
  181.1 10.8 %copy-start.4 = (bf16[6144,4]{0,1:T(4,128)(2,1)S(1)}, bf16[6144,4]{0,1:T(4,128)(2,1)}, u32[]{:S(2)}) copy-start(bf16[6144,4]{0,1:T(4,128)(2,1)} %param.16) | copy-start | bytes 147460
  181.1 89.6 %all-to-all-start.1 = ((bf16[64,6,6144]{2,1,0:T(8,128)(2,1)}), bf16[64,6,6144]{2,1,0:T(8,128)(2,1)}, u32[]{:S(2)}, u32[]{:S(2)}) async-start(bf16[64,6,6144]{2,1,0:T(8,128)(2,1)} %reshape.514), calls=%async_computation.1 | async-start | bytes 12582912 | tf_op jit(solution)/shard_map/all_to_all | solution.py:174
Sparse Core Ops, SparseCore 0:
  96.5 52.7 all-gather.1

commit v10 on v8

--- a/solution.py
+++ b/solution.py
@@ -157,7 +157,7 @@
         lax.ppermute(send[k], "x", [(i, (i + k) % nx) for i in range(nx)]) for k in range(1, nx)
     ]
     arrived = jnp.concatenate(arrived, axis=0)
-    rows = lax.all_gather(arrived, ("c", "y", "z"), axis=0, tiled=True)
+    rows = lax.all_gather(arrived, ("c", "z", "y"), axis=0, tiled=True)
     gate_up_weight = jnp.concatenate([gate_weight, up_weight], axis=1)
     line_rows = rows.shape[0] // nc
     other_rows = lax.dynamic_slice_in_dim(rows, (1 - ci) * line_rows, line_rows, 0)
@@ -169,7 +169,7 @@
 
     lines = summed.reshape(-1, experts * capacity, model_width)
     summed = jnp.sum(
-        lax.all_to_all(lines, ("y", "z"), split_axis=0, concat_axis=0, tiled=True).astype(
+        lax.all_to_all(lines, ("z", "y"), split_axis=0, concat_axis=0, tiled=True).astype(
             jnp.float32
         ),
         axis=0,

time: 271 us -> 272 us (level)
  the two profiles are of different devices: /device:TPU:112 before, /device:TPU:0 now
where the time goes in v10:
time: 272 us; the launch traced here: 271 us
  waiting for transfers between devices  156 us (57%)
  matrix products  43.2 us (16%)
  starting transfers between devices  29.3 us (11%)
  other arithmetic  17.7 us (7%)
  between operations  13.7 us (5%)
  local copies, waits for them, and re-layouts  10.9 us (4%)
    all_to_all x1, waiting for transfers between devices, per_device(): lax.all_to_all(lines, ('z', 'y'), split_axis=0, concat_axis=0, tiled=True)  70.5 us
    all_gather x1, waiting for transfers between devices, per_device(): rows = lax.all_gather(arrived, ('c', 'z', 'y'), axis=0, tiled=True)  46.8 us
    all_to_all x1, waiting for transfers between devices, per_device(): lax.all_to_all(blocks, ('x', 'y'), split_axis=0, concat_axis=0, tiled=True)  22.3 us
    dot_general x2, matrix products, expert_rows(): both = jnp.dot(rows, gate_up_weight, preferred_element_type=jnp.float32)  12.3 us
    dot_general x2, matrix products, expert_rows(): jnp.dot(activated, down_weight, preferred_element_type=jnp.float32)  9.52 us
    all_to_all x1, starting transfers between devices, per_device(): lax.all_to_all(blocks, ('x', 'y'), split_axis=0, concat_axis=0, tiled=True)  6.92 us
    ppermute x3, starting transfers between devices, per_device(): lax.ppermute(pair, 'z', [(i, (i - k) % nz) for i in range(nz)])  6.58 us
    ppermute x3, starting transfers between devices, per_device(): lax.ppermute(summed[k], 'x', [(i, (i - k) % nx) for i in range(nx)])  5.69 us
  transfers between devices with their start and end apart: 15, of which 13 were waited for; matrix products, arithmetic and copies ran while one was open for 9% of the time, Pallas kernels for 0%

profile of v10, /device:TPU:0, one launch (start us, length us, event | category | flops | bytes accessed | tf_op | source)
XLA Modules:
  0.0 270.7 jit_solution(15587182854501100450)
XLA Ops:
  6.6 1.0 reduce-window.8
  7.6 1.9 fusion.8
  10.3 2.5 fusion.13
  13.8 1.7 collective-permute-start
  15.5 0.9 multiply_cosine_fusion.1
  16.5 4.4 %fusion.15 = f32[128,384]{0,1:T(8,128)S(1)} fusion(bf16[6144,384]{1,0:T(8,128)(2,1)} %param.11, bf16[128,6144]{1,0:T(8,128)(2,1)S(1)} %copy-done.1, f32[128]{0:T(128)S(1)} %add_rsqrt_fusion.1), kind=kOutput, calls=%fused_computation.28 | convolution fusion | flops 606339072 | bytes 6488576 | tf_op jit(solution)/shard_map/dot_general | solution.py:83
  21.7 1.0 copy.33
  22.7 1.6 subtract_convert_fusion
  24.3 0.8 select_bitcast_fusion.1
  25.3 1.2 collective-permute-done.1
  26.5 2.0 collective-permute-start.4
  28.5 3.6 %collective-permute-start.3 = (bf16[2,2,128,128]{3,2,1,0:T(8,128)(2,1)S(1)}, bf16[2,2,128,128]{3,2,1,0:T(8,128)(2,1)S(1)}, u32[]{:S(2)}, u32[]{:S(2)}) collective-permute-start(bf16[2,2,128,128]{3,2,1,0:T(8,128)(2,1)S(1)} %maximum_select_fusion.1), channel_id=1, source_target_pairs={{0,64},{32,96},{64,0},{96,32},{1,65},{33,97},{65,1},{97,33},{2,66}... | collective-permute-start | bytes 393224 | tf_op jit(solution)/shard_map/ppermute | solution.py:101
  32.1 1.0 collective-permute-start.2
  33.3 1.1 collective-permute-done.4
  34.4 4.0 %collective-permute-done.3 = bf16[2,2,128,128]{3,2,1,0:T(8,128)(2,1)S(1)} collective-permute-done((bf16[2,2,128,128]{3,2,1,0:T(8,128)(2,1)S(1)}, bf16[2,2,128,128]{3,2,1,0:T(8,128)(2,1)S(1)}, u32[]{:S(2)}, u32[]{:S(2)}) %collective-permute-start.3) | collective-permute-done | bytes 131104 | tf_op jit(solution)/shard_map/ppermute | solution.py:101
  39.2 1.9 fusion.74
  41.1 2.6 multiply_select_fusion
  43.7 2.5 fusion.11
  46.2 4.5 %fusion.1 = bf16[16,8,6144]{2,1,0:T(8,128)(2,1)} fusion(bf16[128,384]{0,1:T(8,128)(2,1)S(1)} %bitcast.93, bf16[384,6144]{1,0:T(8,128)(2,1)} %param.13), kind=kOutput, calls=%fused_computation.7 | convolution fusion | flops 604766208 | bytes 6389760 | tf_op jit(solution)/shard_map/dot_general | solution.py:127
  50.7 6.9 %all-to-all-start = ((bf16[16,8,6144]{2,1,0:T(8,128)(2,1)}), bf16[16,8,6144]{2,1,0:T(8,128)(2,1)}, u32[]{:S(2)}, u32[]{:S(2)}) async-start(bf16[16,8,6144]{2,1,0:T(8,128)(2,1)} %fusion.1), calls=%async_computation | async-start | bytes 3145728 | tf_op jit(solution)/shard_map/all_to_all | solution.py:130
  58.6 22.3 %all-to-all-done = bf16[16,8,6144]{2,1,0:T(8,128)(2,1)} async-done(((bf16[16,8,6144]{2,1,0:T(8,128)(2,1)}), bf16[16,8,6144]{2,1,0:T(8,128)(2,1)}, u32[]{:S(2)}, u32[]{:S(2)}) %all-to-all-start) | async-done | bytes 1572896 | tf_op jit(solution)/shard_map/all_to_all | solution.py:130
  80.9 1.6 convert_reduce_fusion
  82.6 1.1 multiply_reduce_fusion
  83.6 1.0 multiply_convert_fusion
  85.0 0.9 collective-permute-start.7
  86.4 1.3 collective-permute-start.5
  87.7 2.0 collective-permute-done.7
  89.7 2.4 collective-permute-done.6
  92.1 1.0 collective-permute-done.5
  93.1 0.9 pad_maximum_fusion
  94.0 4.0 %constant_dynamic-update-slice_fusion.1 = bf16[6144,512]{1,0:T(8,128)(2,1)} fusion(bf16[6144,256]{1,0:T(8,128)(2,1)} %param.17), kind=kLoop, calls=%fused_computation.93 | loop fusion | bytes 6291456
  98.0 2.0 constant_dynamic-update-slice_fusion
  100.0 46.8 %all-gather.2.cloned.1.call-done = bf16[768,6144]{1,0:T(8,128)(2,1)} async-done(((bf16[24,6144]{1,0:T(8,128)(2,1)}), bf16[768,6144]{1,0:T(8,128)(2,1)}) %all-gather.2.cloned.1.call-update) | async-done | bytes 9437200 | tf_op jit(solution)/shard_map/all_gather | solution.py:160
  146.7 6.2 %fusion.4 = f32[384,512]{1,0:T(8,128)S(1)} fusion(bf16[6144,512]{1,0:T(8,128)(2,1)} %constant_dynamic-update-slice_fusion, bf16[768,6144]{1,0:T(8,128)(2,1)} %all-gather.2.cloned.1.call-done, s32[]{:T(128)S(6)} %select_n.150), kind=kOutput, calls=%fused_computation.12 | convolution fusion | flops 2415919104 | bytes 11796484 | tf_op jit(solution)/shard_map/dot_general | solution.py:45
  153.0 3.5 %convolution_convert_fusion = bf16[384,6144]{1,0:T(8,128)(2,1)} fusion(bf16[384,256]{1,0:T(8,128)(2,1)S(1)} %fusion.17, bf16[256,6144]{1,0:T(8,128)(2,1)S(1)} %copy-done), kind=kOutput, calls=%fused_computation.4 | convolution fusion | flops 1210318848 | bytes 8060928 | tf_op jit(solution)/shard_map/dot_general | solution.py:49
  156.8 6.2 %fusion.6 = f32[384,512]{1,0:T(8,128)S(1)} fusion(bf16[6144,512]{1,0:T(8,128)(2,1)} %constant_dynamic-update-slice_fusion, bf16[768,6144]{1,0:T(8,128)(2,1)} %all-gather.2.cloned.1.call-done, s32[]{:T(128)S(6)} %select_n.149), kind=kOutput, calls=%fused_computation.14 | convolution fusion | flops 2415919104 | bytes 11796484 | tf_op jit(solution)/shard_map/dot_general | solution.py:45
  163.1 1.7 collective-permute-done.8
  164.8 6.0 %add_convert_fusion = bf16[384,6144]{1,0:T(8,128)(2,1)} fusion(bf16[384,6144]{1,0:T(8,128)(2,1)} %collective-permute-done.8, bf16[384,256]{1,0:T(8,128)(2,1)S(1)} %fusion.18, bf16[256,6144]{1,0:T(8,128)(2,1)S(1)} %copy-done), kind=kOutput, calls=%fused_computation.3 | convolution fusion | flops 1219756032 | bytes 12779520 | tf_op jit(solution)/shard_map/dot_general | solution.py:49
  170.8 5.4 %all-to-all-start.1 = ((bf16[16,24,6144]{2,1,0:T(8,128)(2,1)}), bf16[16,24,6144]{2,1,0:T(8,128)(2,1)}, u32[]{:S(2)}, u32[]{:S(2)}) async-start(bf16[16,24,6144]{2,1,0:T(8,128)(2,1)} %bitcast.85), calls=%async_computation.1 | async-start | bytes 9437184 | tf_op jit(solution)/shard_map/all_to_all | solution.py:172
  177.0 70.5 %all-to-all-done.1 = bf16[16,24,6144]{2,1,0:T(8,128)(2,1)} async-done(((bf16[16,24,6144]{2,1,0:T(8,128)(2,1)}), bf16[16,24,6144]{2,1,0:T(8,128)(2,1)}, u32[]{:S(2)}, u32[]{:S(2)}) %all-to-all-start.1) | async-done | bytes 4718624 | tf_op jit(solution)/shard_map/all_to_all | solution.py:172
  247.5 3.9 %reduce_sum.112 = bf16[24,6144]{1,0:T(8,128)(2,1)} reduce(bf16[16,24,6144]{2,1,0:T(8,128)(2,1)} %all-to-all-done.1, bf16[]{:T(256)} %constant.129.clone.1), dimensions={0}, to_apply=%region_15.16 | reduce | flops 2211840 | bytes 5013506 | tf_op jit(solution)/shard_map/reduce_sum | solution.py:171
  251.4 1.2 slice_bitcast_fusion
  252.6 1.6 collective-permute-start.11
  254.1 2.7 collective-permute-start.10
  256.8 1.5 collective-permute-start.9
  258.4 1.2 collective-permute-done.11
  259.5 1.2 collective-permute-done.10
  261.4 2.5 fusion.3
  (59 shorter events, 7.8 us)
Async XLA Ops:
  6.5 146.5 %copy-start = (bf16[256,6144]{1,0:T(8,128)(2,1)S(1)}, bf16[256,6144]{1,0:T(8,128)(2,1)}, u32[]{:S(2)}) copy-start(bf16[256,6144]{1,0:T(8,128)(2,1)} %param.19) | copy-start | bytes 9437188
  7.6 8.9 %copy-start.1 = (bf16[128,6144]{1,0:T(8,128)(2,1)S(1)}, bf16[128,6144]{1,0:T(8,128)(2,1)}, u32[]{:S(2)}) copy-start(bf16[128,6144]{1,0:T(8,128)(2,1)} %param.10) | copy-start | bytes 4718596
  13.8 10.6 %collective-permute-start = (bf16[128,128]{1,0:T(8,128)(2,1)}, bf16[128,128]{1,0:T(8,128)(2,1)}, u32[]{:S(2)}, u32[]{:S(2)}) collective-permute-start(bf16[128,128]{1,0:T(8,128)(2,1)} %fusion.34), channel_id=1, source_target_pairs={{0,1},{1,0},{2,3},{3,2},{4,5},{5,4},{6,7},{7,6},{8,9},{9,8},{10,11... | collective-permute-start | bytes 98312 | tf_op jit(solution)/shard_map/ppermute | solution.py:92
  25.1 1.3 collective-permute-start.1
  26.5 7.9 %collective-permute-start.4 = (bf16[2,2,128,128]{3,2,1,0:T(8,128)(2,1)S(1)}, bf16[2,2,128,128]{3,2,1,0:T(8,128)(2,1)S(1)}, u32[]{:S(2)}, u32[]{:S(2)}) collective-permute-start(bf16[2,2,128,128]{3,2,1,0:T(8,128)(2,1)S(1)} %maximum_select_fusion.1), channel_id=1, source_target_pairs={{0,32},{32,64},{64,96},{96,0},{1,33},{33,65},{65,97},{97,1},{2,34}... | collective-permute-start | bytes 393224 | tf_op jit(solution)/shard_map/ppermute | solution.py:101
  28.5 9.9 %collective-permute-start.3 = (bf16[2,2,128,128]{3,2,1,0:T(8,128)(2,1)S(1)}, bf16[2,2,128,128]{3,2,1,0:T(8,128)(2,1)S(1)}, u32[]{:S(2)}, u32[]{:S(2)}) collective-permute-start(bf16[2,2,128,128]{3,2,1,0:T(8,128)(2,1)S(1)} %maximum_select_fusion.1), channel_id=1, source_target_pairs={{0,64},{32,96},{64,0},{96,32},{1,65},{33,97},{65,1},{97,33},{2,66}... | collective-permute-start | bytes 393224 | tf_op jit(solution)/shard_map/ppermute | solution.py:101
  32.1 6.3 %collective-permute-start.2 = (bf16[2,2,128,128]{3,2,1,0:T(8,128)(2,1)S(1)}, bf16[2,2,128,128]{3,2,1,0:T(8,128)(2,1)S(1)}, u32[]{:S(2)}, u32[]{:S(2)}) collective-permute-start(bf16[2,2,128,128]{3,2,1,0:T(8,128)(2,1)S(1)} %maximum_select_fusion.1), channel_id=1, source_target_pairs={{0,96},{32,0},{64,32},{96,64},{1,97},{33,1},{65,33},{97,65},{2,98}... | collective-permute-start | bytes 393224 | tf_op jit(solution)/shard_map/ppermute | solution.py:101
  50.7 7.0 %copy-start.3 = (s32[8,2]{0,1:T(2,128)S(1)}, s32[8,2]{0,1:T(2,128)}, u32[]{:S(2)}) copy-start(s32[8,2]{0,1:T(2,128)} %param.15) | copy-start | bytes 196
  50.7 30.2 %all-to-all-start = ((bf16[16,8,6144]{2,1,0:T(8,128)(2,1)}), bf16[16,8,6144]{2,1,0:T(8,128)(2,1)}, u32[]{:S(2)}, u32[]{:S(2)}) async-start(bf16[16,8,6144]{2,1,0:T(8,128)(2,1)} %fusion.1), calls=%async_computation | async-start | bytes 3145728 | tf_op jit(solution)/shard_map/all_to_all | solution.py:130
  57.6 89.1 %all-gather.2.cloned.1.call-start = ((), (), s32[]{:S(2)}) async-start(), calls=%async_computation.2 | async-start | bytes 9732096 | tf_op jit(solution)/shard_map/all_gather | solution.py:160
  85.0 4.7 %collective-permute-start.7 = (bf16[6,6144]{1,0:T(8,128)(2,1)S(1)}, bf16[6,6144]{1,0:T(8,128)(2,1)S(1)}, u32[]{:S(2)}, u32[]{:S(2)}) collective-permute-start(bf16[6,6144]{1,0:T(8,128)(2,1)S(1)} %get-tuple-element.12), channel_id=1, source_target_pairs={{0,12},{4,0},{8,4},{12,8},{1,13},{5,1},{9,5},{13,9},{2,14},{6,2},{... | collective-permute-start | bytes 221192 | tf_op jit(solution)/shard_map/ppermute | solution.py:157
  85.9 6.2 %collective-permute-start.6 = (bf16[6,6144]{1,0:T(8,128)(2,1)S(1)}, bf16[6,6144]{1,0:T(8,128)(2,1)S(1)}, u32[]{:S(2)}, u32[]{:S(2)}) collective-permute-start(bf16[6,6144]{1,0:T(8,128)(2,1)S(1)} %get-tuple-element.13), channel_id=1, source_target_pairs={{0,8},{4,12},{8,0},{12,4},{1,9},{5,13},{9,1},{13,5},{2,10},{6,14},... | collective-permute-start | bytes 221192 | tf_op jit(solution)/shard_map/ppermute | solution.py:157
  86.4 6.7 %collective-permute-start.5 = (bf16[6,6144]{1,0:T(8,128)(2,1)S(1)}, bf16[6,6144]{1,0:T(8,128)(2,1)S(1)}, u32[]{:S(2)}, u32[]{:S(2)}) collective-permute-start(bf16[6,6144]{1,0:T(8,128)(2,1)S(1)} %get-tuple-element.14), channel_id=1, source_target_pairs={{0,4},{4,8},{8,12},{12,0},{1,5},{5,9},{9,13},{13,1},{2,6},{6,10},{... | collective-permute-start | bytes 221192 | tf_op jit(solution)/shard_map/ppermute | solution.py:157
  94.0 4.0 %copy-start.2 = (bf16[6144,256]{1,0:T(8,128)(2,1)S(1)}, bf16[6144,256]{1,0:T(8,128)(2,1)}, u32[]{:S(2)}) copy-start(bf16[6144,256]{1,0:T(8,128)(2,1)} %param.18) | copy-start | bytes 9437188
  156.6 8.3 %collective-permute-start.8 = (bf16[384,6144]{1,0:T(8,128)(2,1)}, bf16[384,6144]{1,0:T(8,128)(2,1)}, u32[]{:S(2)}, u32[]{:S(2)}) collective-permute-start(bf16[384,6144]{1,0:T(8,128)(2,1)} %convolution_convert_fusion), channel_id=1, source_target_pairs={{0,16},{16,0},{1,17},{17,1},{2,18},{18,2},{3,19},{19,3},{4,20},{20... | collective-permute-start | bytes 14155784 | tf_op jit(solution)/shard_map/ppermute | solution.py:166
  170.8 5.4 %copy-start.4 = (bf16[6144,4]{0,1:T(4,128)(2,1)S(1)}, bf16[6144,4]{0,1:T(4,128)(2,1)}, u32[]{:S(2)}) copy-start(bf16[6144,4]{0,1:T(4,128)(2,1)} %param.16) | copy-start | bytes 147460
  170.8 76.7 %all-to-all-start.1 = ((bf16[16,24,6144]{2,1,0:T(8,128)(2,1)}), bf16[16,24,6144]{2,1,0:T(8,128)(2,1)}, u32[]{:S(2)}, u32[]{:S(2)}) async-start(bf16[16,24,6144]{2,1,0:T(8,128)(2,1)} %bitcast.85), calls=%async_computation.1 | async-start | bytes 9437184 | tf_op jit(solution)/shard_map/all_to_all | solution.py:172
  252.6 6.9 %collective-permute-start.11 = (bf16[6,6144]{1,0:T(8,128)(2,1)S(1)}, bf16[6,6144]{1,0:T(8,128)(2,1)S(1)}, u32[]{:S(2)}, u32[]{:S(2)}) collective-permute-start(bf16[6,6144]{1,0:T(8,128)(2,1)S(1)} %get-tuple-element.16), channel_id=1, source_target_pairs={{0,4},{4,8},{8,12},{12,0},{1,5},{5,9},{9,13},{13,1},{2,6},{6,10},{... | collective-permute-start | bytes 221192 | tf_op jit(solution)/shard_map/ppermute | solution.py:181
  254.1 6.6 %collective-permute-start.10 = (bf16[6,6144]{1,0:T(8,128)(2,1)S(1)}, bf16[6,6144]{1,0:T(8,128)(2,1)S(1)}, u32[]{:S(2)}, u32[]{:S(2)}) collective-permute-start(bf16[6,6144]{1,0:T(8,128)(2,1)S(1)} %get-tuple-element.17), channel_id=1, source_target_pairs={{0,8},{4,12},{8,0},{12,4},{1,9},{5,13},{9,1},{13,5},{2,10},{6,14},... | collective-permute-start | bytes 221192 | tf_op jit(solution)/shard_map/ppermute | solution.py:181
  256.8 4.6 %collective-permute-start.9 = (bf16[6,6144]{1,0:T(8,128)(2,1)S(1)}, bf16[6,6144]{1,0:T(8,128)(2,1)S(1)}, u32[]{:S(2)}, u32[]{:S(2)}) collective-permute-start(bf16[6,6144]{1,0:T(8,128)(2,1)S(1)} %get-tuple-element.18), channel_id=1, source_target_pairs={{0,12},{4,0},{8,4},{12,8},{1,13},{5,1},{9,5},{13,9},{2,14},{6,2},{... | collective-permute-start | bytes 221192 | tf_op jit(solution)/shard_map/ppermute | solution.py:181
Sparse Core Ops, SparseCore 0:
  94.1 52.5 all-gather.1

commit v11 on v8

--- a/solution.py
+++ b/solution.py
@@ -96,7 +96,7 @@
     nz = lax.axis_size("z")
     core_swap = [(i, i ^ 1) for i in range(nc)]
     other_core = lax.ppermute(both, "c", core_swap)
-    pair = jnp.where(ci == 0, jnp.stack([both, other_core]), jnp.stack([other_core, both]))
+    pair = jnp.stack([both, other_core])
     ring = [pair] + [
         lax.ppermute(pair, "z", [(i, (i - k) % nz) for i in range(nz)]) for k in range(1, nz)
     ]
@@ -104,7 +104,8 @@
     key_piece = gathered[0]
     value_piece = gathered[1]
     ring_range = jnp.arange(nz, dtype=jnp.int32)
-    shard_of = ((zi + ring_range) % nz)[:, None] * nc + jnp.arange(nc, dtype=jnp.int32)[None, :]
+    core_order = (ci + jnp.arange(nc, dtype=jnp.int32)) % nc
+    shard_of = ((zi + ring_range) % nz)[:, None] * nc + core_order[None, :]
     key_places = (
         shard_of[:, :, None] * tok_dev + jnp.arange(tok_dev, dtype=jnp.int32)[None, None, :]
     ).reshape(-1)

time: 271 us -> 272 us (level)
  transfers between devices with their start and end apart: 15 -> 15, of which waited for: 14 -> 13; matrix products, arithmetic and copies ran while one was open for 9% -> 9% of each run, Pallas kernels for 0% -> 0%
where the time goes in v11:
time: 272 us; the launch traced here: 271 us
  waiting for transfers between devices  155 us (57%)
  matrix products  43.1 us (16%)
  starting transfers between devices  30.1 us (11%)
  other arithmetic  18.9 us (7%)
  between operations  13.7 us (5%)
  local copies, waits for them, and re-layouts  10.9 us (4%)
    all_to_all x1, waiting for transfers between devices, per_device(): lax.all_to_all(lines, ('y', 'z'), split_axis=0, concat_axis=0, tiled=True)  70.8 us
    all_gather x1, waiting for transfers between devices, per_device(): rows = lax.all_gather(arrived, ('c', 'y', 'z'), axis=0, tiled=True)  46.9 us
    all_to_all x1, waiting for transfers between devices, per_device(): lax.all_to_all(blocks, ('x', 'y'), split_axis=0, concat_axis=0, tiled=True)  20.3 us
    dot_general x2, matrix products, expert_rows(): both = jnp.dot(rows, gate_up_weight, preferred_element_type=jnp.float32)  12.3 us
    dot_general x2, matrix products, expert_rows(): jnp.dot(activated, down_weight, preferred_element_type=jnp.float32)  9.52 us
    all_to_all x1, starting transfers between devices, per_device(): lax.all_to_all(lines, ('y', 'z'), split_axis=0, concat_axis=0, tiled=True)  7.51 us
    all_to_all x1, starting transfers between devices, per_device(): lax.all_to_all(blocks, ('x', 'y'), split_axis=0, concat_axis=0, tiled=True)  7.41 us
    ppermute x3, waiting for transfers between devices, per_device(): lax.ppermute(pair, 'z', [(i, (i - k) % nz) for i in range(nz)])  5.88 us
  transfers between devices with their start and end apart: 15, of which 13 were waited for; matrix products, arithmetic and copies ran while one was open for 9% of the time, Pallas kernels for 0%

profile of v11, /device:TPU:112, one launch (start us, length us, event | category | flops | bytes accessed | tf_op | source)
XLA Modules:
  0.0 271.3 jit_solution(13044541730865081883)
XLA Ops:
  6.6 1.0 reduce-window.8
  7.6 1.9 fusion.8
  9.5 0.7 fusion.47
  10.3 2.5 fusion.13
  13.8 1.3 collective-permute-start
  15.7 0.9 multiply_cosine_fusion.1
  16.6 4.4 %fusion.15 = f32[128,384]{0,1:T(8,128)S(1)} fusion(bf16[6144,384]{1,0:T(8,128)(2,1)} %param.11, bf16[128,6144]{1,0:T(8,128)(2,1)S(1)} %copy-done.1, f32[128]{0:T(128)S(1)} %add_rsqrt_fusion.1), kind=kOutput, calls=%fused_computation.28 | convolution fusion | flops 606339072 | bytes 6488576 | tf_op jit(solution)/shard_map/dot_general | solution.py:83
  21.8 1.0 copy.33
  23.5 1.6 subtract_convert_fusion
  25.2 0.8 select_bitcast_fusion.1
  26.2 1.2 collective-permute-done.1
  28.0 3.2 %collective-permute-start.4 = (bf16[2,2,128,128]{3,2,1,0:T(8,128)(2,1)S(1)}, bf16[2,2,128,128]{3,2,1,0:T(8,128)(2,1)S(1)}, u32[]{:S(2)}, u32[]{:S(2)}) collective-permute-start(bf16[2,2,128,128]{3,2,1,0:T(8,128)(2,1)S(1)} %get-tuple-element.22), channel_id=1, source_target_pairs={{0,32},{32,64},{64,96},{96,0},{1,33},{33,65},{65,97},{97,1},{2,34}... | collective-permute-start | bytes 393224 | tf_op jit(solution)/shard_map/ppermute | solution.py:101
  31.4 3.9 %collective-permute-done.3 = bf16[2,2,128,128]{3,2,1,0:T(8,128)(2,1)S(1)} collective-permute-done((bf16[2,2,128,128]{3,2,1,0:T(8,128)(2,1)S(1)}, bf16[2,2,128,128]{3,2,1,0:T(8,128)(2,1)S(1)}, u32[]{:S(2)}, u32[]{:S(2)}) %collective-permute-start.3) | collective-permute-done | bytes 131104 | tf_op jit(solution)/shard_map/ppermute | solution.py:101
  35.3 1.9 collective-permute-done.2
  37.3 0.7 fusion.73
  38.1 1.9 fusion.75
  40.0 2.6 multiply_select_fusion
  42.5 2.5 fusion.11
  45.1 4.5 %fusion.1 = bf16[16,8,6144]{2,1,0:T(8,128)(2,1)} fusion(bf16[128,384]{0,1:T(8,128)(2,1)S(1)} %bitcast.90, bf16[384,6144]{1,0:T(8,128)(2,1)} %param.13), kind=kOutput, calls=%fused_computation.7 | convolution fusion | flops 604766208 | bytes 6389760 | tf_op jit(solution)/shard_map/dot_general | solution.py:128
  49.6 7.4 %all-to-all-start = ((bf16[16,8,6144]{2,1,0:T(8,128)(2,1)}), bf16[16,8,6144]{2,1,0:T(8,128)(2,1)}, u32[]{:S(2)}, u32[]{:S(2)}) async-start(bf16[16,8,6144]{2,1,0:T(8,128)(2,1)} %fusion.1), calls=%async_computation | async-start | bytes 3145728 | tf_op jit(solution)/shard_map/all_to_all | solution.py:131
  57.9 20.3 %all-to-all-done = bf16[16,8,6144]{2,1,0:T(8,128)(2,1)} async-done(((bf16[16,8,6144]{2,1,0:T(8,128)(2,1)}), bf16[16,8,6144]{2,1,0:T(8,128)(2,1)}, u32[]{:S(2)}, u32[]{:S(2)}) %all-to-all-start) | async-done | bytes 1572896 | tf_op jit(solution)/shard_map/all_to_all | solution.py:131
  78.2 1.6 convert_reduce_fusion
  79.8 1.1 multiply_reduce_fusion
  80.9 1.0 multiply_convert_fusion
  82.3 1.2 collective-permute-start.7
  83.5 1.7 collective-permute-start.6
  85.2 1.1 collective-permute-start.5
  87.0 2.6 collective-permute-done.6
  89.6 1.4 collective-permute-done.5
  91.0 0.9 pad_maximum_fusion
  91.9 4.0 %constant_dynamic-update-slice_fusion.1 = bf16[6144,512]{1,0:T(8,128)(2,1)} fusion(bf16[6144,256]{1,0:T(8,128)(2,1)} %param.17), kind=kLoop, calls=%fused_computation.92 | loop fusion | bytes 6291456
  96.0 2.0 constant_dynamic-update-slice_fusion
  97.9 46.9 %all-gather.2.cloned.1.call-done = bf16[768,6144]{1,0:T(8,128)(2,1)} async-done(((bf16[24,6144]{1,0:T(8,128)(2,1)}), bf16[768,6144]{1,0:T(8,128)(2,1)}) %all-gather.2.cloned.1.call-update) | async-done | bytes 9437200 | tf_op jit(solution)/shard_map/all_gather | solution.py:161
  144.8 6.2 %fusion.4 = f32[384,512]{1,0:T(8,128)S(1)} fusion(bf16[6144,512]{1,0:T(8,128)(2,1)} %constant_dynamic-update-slice_fusion, bf16[768,6144]{1,0:T(8,128)(2,1)} %all-gather.2.cloned.1.call-done, s32[]{:T(128)S(6)} %select_n.138), kind=kOutput, calls=%fused_computation.12 | convolution fusion | flops 2415919104 | bytes 11796484 | tf_op jit(solution)/shard_map/dot_general | solution.py:45
  151.1 3.5 %convolution_convert_fusion = bf16[384,6144]{1,0:T(8,128)(2,1)} fusion(bf16[384,256]{1,0:T(8,128)(2,1)S(1)} %fusion.17, bf16[256,6144]{1,0:T(8,128)(2,1)S(1)} %copy-done), kind=kOutput, calls=%fused_computation.4 | convolution fusion | flops 1210318848 | bytes 8060928 | tf_op jit(solution)/shard_map/dot_general | solution.py:49
  154.9 6.2 %fusion.6 = f32[384,512]{1,0:T(8,128)S(1)} fusion(bf16[6144,512]{1,0:T(8,128)(2,1)} %constant_dynamic-update-slice_fusion, bf16[768,6144]{1,0:T(8,128)(2,1)} %all-gather.2.cloned.1.call-done, s32[]{:T(128)S(6)} %select_n.137), kind=kOutput, calls=%fused_computation.14 | convolution fusion | flops 2415919104 | bytes 11796484 | tf_op jit(solution)/shard_map/dot_general | solution.py:45
  161.2 1.7 collective-permute-done.8
  162.9 6.0 %add_convert_fusion = bf16[384,6144]{1,0:T(8,128)(2,1)} fusion(bf16[384,6144]{1,0:T(8,128)(2,1)} %collective-permute-done.8, bf16[384,256]{1,0:T(8,128)(2,1)S(1)} %fusion.18, bf16[256,6144]{1,0:T(8,128)(2,1)S(1)} %copy-done), kind=kOutput, calls=%fused_computation.3 | convolution fusion | flops 1219756032 | bytes 12779520 | tf_op jit(solution)/shard_map/dot_general | solution.py:49
  168.9 7.5 %all-to-all-start.1 = ((bf16[16,24,6144]{2,1,0:T(8,128)(2,1)}), bf16[16,24,6144]{2,1,0:T(8,128)(2,1)}, u32[]{:S(2)}, u32[]{:S(2)}) async-start(bf16[16,24,6144]{2,1,0:T(8,128)(2,1)} %bitcast.84), calls=%async_computation.1 | async-start | bytes 9437184 | tf_op jit(solution)/shard_map/all_to_all | solution.py:173
  177.2 70.8 %all-to-all-done.1 = bf16[16,24,6144]{2,1,0:T(8,128)(2,1)} async-done(((bf16[16,24,6144]{2,1,0:T(8,128)(2,1)}), bf16[16,24,6144]{2,1,0:T(8,128)(2,1)}, u32[]{:S(2)}, u32[]{:S(2)}) %all-to-all-start.1) | async-done | bytes 4718624 | tf_op jit(solution)/shard_map/all_to_all | solution.py:173
  248.1 3.9 %reduce_sum.112 = bf16[24,6144]{1,0:T(8,128)(2,1)} reduce(bf16[16,24,6144]{2,1,0:T(8,128)(2,1)} %all-to-all-done.1, bf16[]{:T(256)} %constant.137.clone.1), dimensions={0}, to_apply=%region_15.16 | reduce | flops 2211840 | bytes 5013506 | tf_op jit(solution)/shard_map/reduce_sum | solution.py:172
  252.0 1.2 slice_bitcast_fusion
  253.2 1.5 collective-permute-start.11
  254.7 2.7 collective-permute-start.10
  257.4 1.5 collective-permute-start.9
  258.9 1.2 collective-permute-done.11
  260.1 1.1 collective-permute-done.10
  262.0 2.5 fusion.3
  (59 shorter events, 8.5 us)
Async XLA Ops:
  6.5 144.6 %copy-start = (bf16[256,6144]{1,0:T(8,128)(2,1)S(1)}, bf16[256,6144]{1,0:T(8,128)(2,1)}, u32[]{:S(2)}) copy-start(bf16[256,6144]{1,0:T(8,128)(2,1)} %param.19) | copy-start | bytes 9437188
  7.6 9.0 %copy-start.1 = (bf16[128,6144]{1,0:T(8,128)(2,1)S(1)}, bf16[128,6144]{1,0:T(8,128)(2,1)}, u32[]{:S(2)}) copy-start(bf16[128,6144]{1,0:T(8,128)(2,1)} %param.10) | copy-start | bytes 4718596
  13.8 11.4 %collective-permute-start = (bf16[128,128]{1,0:T(8,128)(2,1)}, bf16[128,128]{1,0:T(8,128)(2,1)}, u32[]{:S(2)}, u32[]{:S(2)}) collective-permute-start(bf16[128,128]{1,0:T(8,128)(2,1)} %fusion.34), channel_id=1, source_target_pairs={{0,1},{1,0},{2,3},{3,2},{4,5},{5,4},{6,7},{7,6},{8,9},{9,8},{10,11... | collective-permute-start | bytes 98312 | tf_op jit(solution)/shard_map/ppermute | solution.py:92
  26.0 1.3 collective-permute-start.1
  27.3 8.0 %collective-permute-start.3 = (bf16[2,2,128,128]{3,2,1,0:T(8,128)(2,1)S(1)}, bf16[2,2,128,128]{3,2,1,0:T(8,128)(2,1)S(1)}, u32[]{:S(2)}, u32[]{:S(2)}) collective-permute-start(bf16[2,2,128,128]{3,2,1,0:T(8,128)(2,1)S(1)} %get-tuple-element.22), channel_id=1, source_target_pairs={{0,64},{32,96},{64,0},{96,32},{1,65},{33,97},{65,1},{97,33},{2,66}... | collective-permute-start | bytes 393224 | tf_op jit(solution)/shard_map/ppermute | solution.py:101
  28.0 9.3 %collective-permute-start.2 = (bf16[2,2,128,128]{3,2,1,0:T(8,128)(2,1)S(1)}, bf16[2,2,128,128]{3,2,1,0:T(8,128)(2,1)S(1)}, u32[]{:S(2)}, u32[]{:S(2)}) collective-permute-start(bf16[2,2,128,128]{3,2,1,0:T(8,128)(2,1)S(1)} %get-tuple-element.22), channel_id=1, source_target_pairs={{0,96},{32,0},{64,32},{96,64},{1,97},{33,1},{65,33},{97,65},{2,98}... | collective-permute-start | bytes 393224 | tf_op jit(solution)/shard_map/ppermute | solution.py:101
  28.0 9.3 %collective-permute-start.4 = (bf16[2,2,128,128]{3,2,1,0:T(8,128)(2,1)S(1)}, bf16[2,2,128,128]{3,2,1,0:T(8,128)(2,1)S(1)}, u32[]{:S(2)}, u32[]{:S(2)}) collective-permute-start(bf16[2,2,128,128]{3,2,1,0:T(8,128)(2,1)S(1)} %get-tuple-element.22), channel_id=1, source_target_pairs={{0,32},{32,64},{64,96},{96,0},{1,33},{33,65},{65,97},{97,1},{2,34}... | collective-permute-start | bytes 393224 | tf_op jit(solution)/shard_map/ppermute | solution.py:101
  49.6 7.5 %copy-start.3 = (s32[8,2]{0,1:T(2,128)S(1)}, s32[8,2]{0,1:T(2,128)}, u32[]{:S(2)}) copy-start(s32[8,2]{0,1:T(2,128)} %param.15) | copy-start | bytes 196
  49.6 28.6 %all-to-all-start = ((bf16[16,8,6144]{2,1,0:T(8,128)(2,1)}), bf16[16,8,6144]{2,1,0:T(8,128)(2,1)}, u32[]{:S(2)}, u32[]{:S(2)}) async-start(bf16[16,8,6144]{2,1,0:T(8,128)(2,1)} %fusion.1), calls=%async_computation | async-start | bytes 3145728 | tf_op jit(solution)/shard_map/all_to_all | solution.py:131
  57.0 87.8 %all-gather.2.cloned.1.call-start = ((), (), s32[]{:S(2)}) async-start(), calls=%async_computation.2 | async-start | bytes 9732096 | tf_op jit(solution)/shard_map/all_gather | solution.py:161
  82.3 4.7 %collective-permute-start.7 = (bf16[6,6144]{1,0:T(8,128)(2,1)S(1)}, bf16[6,6144]{1,0:T(8,128)(2,1)S(1)}, u32[]{:S(2)}, u32[]{:S(2)}) collective-permute-start(bf16[6,6144]{1,0:T(8,128)(2,1)S(1)} %get-tuple-element.12), channel_id=1, source_target_pairs={{0,12},{4,0},{8,4},{12,8},{1,13},{5,1},{9,5},{13,9},{2,14},{6,2},{... | collective-permute-start | bytes 221192 | tf_op jit(solution)/shard_map/ppermute | solution.py:158
  83.5 6.1 %collective-permute-start.6 = (bf16[6,6144]{1,0:T(8,128)(2,1)S(1)}, bf16[6,6144]{1,0:T(8,128)(2,1)S(1)}, u32[]{:S(2)}, u32[]{:S(2)}) collective-permute-start(bf16[6,6144]{1,0:T(8,128)(2,1)S(1)} %get-tuple-element.13), channel_id=1, source_target_pairs={{0,8},{4,12},{8,0},{12,4},{1,9},{5,13},{9,1},{13,5},{2,10},{6,14},... | collective-permute-start | bytes 221192 | tf_op jit(solution)/shard_map/ppermute | solution.py:158
  85.2 5.8 %collective-permute-start.5 = (bf16[6,6144]{1,0:T(8,128)(2,1)S(1)}, bf16[6,6144]{1,0:T(8,128)(2,1)S(1)}, u32[]{:S(2)}, u32[]{:S(2)}) collective-permute-start(bf16[6,6144]{1,0:T(8,128)(2,1)S(1)} %get-tuple-element.14), channel_id=1, source_target_pairs={{0,4},{4,8},{8,12},{12,0},{1,5},{5,9},{9,13},{13,1},{2,6},{6,10},{... | collective-permute-start | bytes 221192 | tf_op jit(solution)/shard_map/ppermute | solution.py:158
  91.9 4.0 %copy-start.2 = (bf16[6144,256]{1,0:T(8,128)(2,1)S(1)}, bf16[6144,256]{1,0:T(8,128)(2,1)}, u32[]{:S(2)}) copy-start(bf16[6144,256]{1,0:T(8,128)(2,1)} %param.18) | copy-start | bytes 9437188
  154.6 8.3 %collective-permute-start.8 = (bf16[384,6144]{1,0:T(8,128)(2,1)}, bf16[384,6144]{1,0:T(8,128)(2,1)}, u32[]{:S(2)}, u32[]{:S(2)}) collective-permute-start(bf16[384,6144]{1,0:T(8,128)(2,1)} %convolution_convert_fusion), channel_id=1, source_target_pairs={{0,16},{16,0},{1,17},{17,1},{2,18},{18,2},{3,19},{19,3},{4,20},{20... | collective-permute-start | bytes 14155784 | tf_op jit(solution)/shard_map/ppermute | solution.py:167
  168.9 7.5 %copy-start.4 = (bf16[6144,4]{0,1:T(4,128)(2,1)S(1)}, bf16[6144,4]{0,1:T(4,128)(2,1)}, u32[]{:S(2)}) copy-start(bf16[6144,4]{0,1:T(4,128)(2,1)} %param.16) | copy-start | bytes 147460
  168.9 79.2 %all-to-all-start.1 = ((bf16[16,24,6144]{2,1,0:T(8,128)(2,1)}), bf16[16,24,6144]{2,1,0:T(8,128)(2,1)}, u32[]{:S(2)}, u32[]{:S(2)}) async-start(bf16[16,24,6144]{2,1,0:T(8,128)(2,1)} %bitcast.84), calls=%async_computation.1 | async-start | bytes 9437184 | tf_op jit(solution)/shard_map/all_to_all | solution.py:173
  253.2 6.9 %collective-permute-start.11 = (bf16[6,6144]{1,0:T(8,128)(2,1)S(1)}, bf16[6,6144]{1,0:T(8,128)(2,1)S(1)}, u32[]{:S(2)}, u32[]{:S(2)}) collective-permute-start(bf16[6,6144]{1,0:T(8,128)(2,1)S(1)} %get-tuple-element.16), channel_id=1, source_target_pairs={{0,4},{4,8},{8,12},{12,0},{1,5},{5,9},{9,13},{13,1},{2,6},{6,10},{... | collective-permute-start | bytes 221192 | tf_op jit(solution)/shard_map/ppermute | solution.py:182
  254.7 6.6 %collective-permute-start.10 = (bf16[6,6144]{1,0:T(8,128)(2,1)S(1)}, bf16[6,6144]{1,0:T(8,128)(2,1)S(1)}, u32[]{:S(2)}, u32[]{:S(2)}) collective-permute-start(bf16[6,6144]{1,0:T(8,128)(2,1)S(1)} %get-tuple-element.17), channel_id=1, source_target_pairs={{0,8},{4,12},{8,0},{12,4},{1,9},{5,13},{9,1},{13,5},{2,10},{6,14},... | collective-permute-start | bytes 221192 | tf_op jit(solution)/shard_map/ppermute | solution.py:182
  257.4 4.6 %collective-permute-start.9 = (bf16[6,6144]{1,0:T(8,128)(2,1)S(1)}, bf16[6,6144]{1,0:T(8,128)(2,1)S(1)}, u32[]{:S(2)}, u32[]{:S(2)}) collective-permute-start(bf16[6,6144]{1,0:T(8,128)(2,1)S(1)} %get-tuple-element.18), channel_id=1, source_target_pairs={{0,12},{4,0},{8,4},{12,8},{1,13},{5,1},{9,5},{13,9},{2,14},{6,2},{... | collective-permute-start | bytes 221192 | tf_op jit(solution)/shard_map/ppermute | solution.py:182
Sparse Core Ops, SparseCore 0:
  92.0 52.7 all-gather.1

commit v12 on v8

--- a/solution.py
+++ b/solution.py
@@ -183,10 +183,14 @@
         ]
     )
 
-    weights = jnp.where(hits, gate_cols[:, :, None], 0.0)
-    moe = jnp.einsum(
-        "rec,ecd->rd", weights, returned.astype(jnp.float32), precision=lax.Precision.HIGHEST
-    )
+    chosen = jnp.take(matches, shift, axis=2)[:, :, :, None] & hits[:, None, :, :]
+    picked_rows = jnp.einsum(
+        "rkec,ecd->rkd",
+        chosen.astype(jnp.bfloat16),
+        returned,
+        preferred_element_type=jnp.float32,
+    )
+    moe = jnp.sum(gates[:, :, None] * picked_rows, axis=1)
     return (hidden_state + moe).astype(jnp.bfloat16)
 
 

time: 271 us -> 270 us (level)
  no operation moved by 1% of the time
where the time goes in v12:
time: 270 us; the launch traced here: 269 us
  waiting for transfers between devices  156 us (58%)
  matrix products  41.1 us (15%)
  starting transfers between devices  28.8 us (11%)
  other arithmetic  19.3 us (7%)
  between operations  13.7 us (5%)
  local copies, waits for them, and re-layouts  10.9 us (4%)
    all_to_all x1, waiting for transfers between devices, per_device(): lax.all_to_all(lines, ('y', 'z'), split_axis=0, concat_axis=0, tiled=True)  70.8 us
    all_gather x1, waiting for transfers between devices, per_device(): rows = lax.all_gather(arrived, ('c', 'y', 'z'), axis=0, tiled=True)  46.9 us
    all_to_all x1, waiting for transfers between devices, per_device(): lax.all_to_all(blocks, ('x', 'y'), split_axis=0, concat_axis=0, tiled=True)  19.6 us
    dot_general x2, matrix products, expert_rows(): both = jnp.dot(rows, gate_up_weight, preferred_element_type=jnp.float32)  12.3 us
    dot_general x2, matrix products, expert_rows(): jnp.dot(activated, down_weight, preferred_element_type=jnp.float32)  9.52 us
    all_to_all x1, starting transfers between devices, per_device(): lax.all_to_all(lines, ('y', 'z'), split_axis=0, concat_axis=0, tiled=True)  7.51 us
    all_to_all x1, starting transfers between devices, per_device(): lax.all_to_all(blocks, ('x', 'y'), split_axis=0, concat_axis=0, tiled=True)  7.41 us
    ppermute x3, waiting for transfers between devices, per_device(): lax.ppermute(pair, 'z', [(i, (i - k) % nz) for i in range(nz)])  7.29 us
  transfers between devices with their start and end apart: 15, of which 14 were waited for; matrix products, arithmetic and copies ran while one was open for 9% of the time, Pallas kernels for 0%

profile of v12, /device:TPU:112, one launch (start us, length us, event | category | flops | bytes accessed | tf_op | source)
XLA Modules:
  0.0 269.3 jit_solution(18011405974231716415)
XLA Ops:
  6.6 1.0 reduce-window.8
  7.6 1.9 fusion.7
  9.5 0.7 fusion.38
  10.3 2.5 fusion.13
  13.8 1.3 collective-permute-start
  15.1 0.9 multiply_cosine_fusion.1
  16.1 4.4 %fusion.15 = f32[128,384]{0,1:T(8,128)S(1)} fusion(bf16[6144,384]{1,0:T(8,128)(2,1)} %param.11, bf16[128,6144]{1,0:T(8,128)(2,1)S(1)} %copy-done.1, f32[128]{0:T(128)S(1)} %add_rsqrt_fusion.1), kind=kOutput, calls=%fused_computation.28 | convolution fusion | flops 606339072 | bytes 6488576 | tf_op jit(solution)/shard_map/dot_general | solution.py:83
  21.2 1.0 copy.34
  22.3 1.6 subtract_convert_fusion
  23.9 0.8 select_bitcast_fusion.1
  24.9 1.2 collective-permute-done.1
  26.2 2.5 collective-permute-start.3
  28.8 3.7 %collective-permute-done.4 = bf16[2,2,128,128]{3,2,1,0:T(8,128)(2,1)S(1)} collective-permute-done((bf16[2,2,128,128]{3,2,1,0:T(8,128)(2,1)S(1)}, bf16[2,2,128,128]{3,2,1,0:T(8,128)(2,1)S(1)}, u32[]{:S(2)}, u32[]{:S(2)}) %collective-permute-start.4) | collective-permute-done | bytes 131104 | tf_op jit(solution)/shard_map/ppermute | solution.py:101
  32.5 1.6 collective-permute-done.3
  34.1 2.0 collective-permute-done.2
  36.9 1.9 fusion.62
  38.8 2.6 multiply_select_fusion
  41.4 2.5 fusion.11
  43.9 4.5 %fusion.1 = bf16[16,8,6144]{2,1,0:T(8,128)(2,1)} fusion(bf16[128,384]{0,1:T(8,128)(2,1)S(1)} %bitcast.93, bf16[384,6144]{1,0:T(8,128)(2,1)} %param.13), kind=kOutput, calls=%fused_computation.7 | convolution fusion | flops 604766208 | bytes 6389760 | tf_op jit(solution)/shard_map/dot_general | solution.py:127
  48.4 7.4 %all-to-all-start = ((bf16[16,8,6144]{2,1,0:T(8,128)(2,1)}), bf16[16,8,6144]{2,1,0:T(8,128)(2,1)}, u32[]{:S(2)}, u32[]{:S(2)}) async-start(bf16[16,8,6144]{2,1,0:T(8,128)(2,1)} %fusion.1), calls=%async_computation | async-start | bytes 3145728 | tf_op jit(solution)/shard_map/all_to_all | solution.py:130
  56.9 19.6 %all-to-all-done = bf16[16,8,6144]{2,1,0:T(8,128)(2,1)} async-done(((bf16[16,8,6144]{2,1,0:T(8,128)(2,1)}), bf16[16,8,6144]{2,1,0:T(8,128)(2,1)}, u32[]{:S(2)}, u32[]{:S(2)}) %all-to-all-start) | async-done | bytes 1572896 | tf_op jit(solution)/shard_map/all_to_all | solution.py:130
  76.5 1.6 convert_reduce_fusion
  78.2 1.1 multiply_reduce_fusion
  79.2 1.0 multiply_convert_fusion
  80.6 1.4 collective-permute-start.7
  82.0 1.7 collective-permute-start.6
  83.6 0.9 collective-permute-start.5
  85.2 2.9 %collective-permute-done.6 = bf16[6,6144]{1,0:T(8,128)(2,1)S(1)} collective-permute-done((bf16[6,6144]{1,0:T(8,128)(2,1)S(1)}, bf16[6,6144]{1,0:T(8,128)(2,1)S(1)}, u32[]{:S(2)}, u32[]{:S(2)}) %collective-permute-start.6) | collective-permute-done | bytes 73760 | tf_op jit(solution)/shard_map/ppermute | solution.py:157
  88.1 1.4 collective-permute-done.5
  89.5 0.9 pad_maximum_fusion
  90.4 4.0 %constant_dynamic-update-slice_fusion.1 = bf16[6144,512]{1,0:T(8,128)(2,1)} fusion(bf16[6144,256]{1,0:T(8,128)(2,1)} %param.17), kind=kLoop, calls=%fused_computation.88 | loop fusion | bytes 6291456
  94.4 2.0 constant_dynamic-update-slice_fusion
  96.4 46.9 %all-gather.2.cloned.1.call-done = bf16[768,6144]{1,0:T(8,128)(2,1)} async-done(((bf16[24,6144]{1,0:T(8,128)(2,1)}), bf16[768,6144]{1,0:T(8,128)(2,1)}) %all-gather.2.cloned.1.call-update) | async-done | bytes 9437200 | tf_op jit(solution)/shard_map/all_gather | solution.py:160
  143.3 6.2 %fusion.3 = f32[384,512]{1,0:T(8,128)S(1)} fusion(bf16[6144,512]{1,0:T(8,128)(2,1)} %constant_dynamic-update-slice_fusion, bf16[768,6144]{1,0:T(8,128)(2,1)} %all-gather.2.cloned.1.call-done, s32[]{:T(128)S(6)} %select_n.144), kind=kOutput, calls=%fused_computation.11 | convolution fusion | flops 2415919104 | bytes 11796484 | tf_op jit(solution)/shard_map/dot_general | solution.py:45
  149.6 3.5 %convolution_convert_fusion = bf16[384,6144]{1,0:T(8,128)(2,1)} fusion(bf16[384,256]{1,0:T(8,128)(2,1)S(1)} %fusion.17, bf16[256,6144]{1,0:T(8,128)(2,1)S(1)} %copy-done), kind=kOutput, calls=%fused_computation.4 | convolution fusion | flops 1210318848 | bytes 8060928 | tf_op jit(solution)/shard_map/dot_general | solution.py:49
  153.3 6.2 %fusion.5 = f32[384,512]{1,0:T(8,128)S(1)} fusion(bf16[6144,512]{1,0:T(8,128)(2,1)} %constant_dynamic-update-slice_fusion, bf16[768,6144]{1,0:T(8,128)(2,1)} %all-gather.2.cloned.1.call-done, s32[]{:T(128)S(6)} %select_n.143), kind=kOutput, calls=%fused_computation.13 | convolution fusion | flops 2415919104 | bytes 11796484 | tf_op jit(solution)/shard_map/dot_general | solution.py:45
  159.6 1.7 collective-permute-done.8
  161.3 6.0 %add_convert_fusion = bf16[384,6144]{1,0:T(8,128)(2,1)} fusion(bf16[384,6144]{1,0:T(8,128)(2,1)} %collective-permute-done.8, bf16[384,256]{1,0:T(8,128)(2,1)S(1)} %fusion.18, bf16[256,6144]{1,0:T(8,128)(2,1)S(1)} %copy-done), kind=kOutput, calls=%fused_computation.3 | convolution fusion | flops 1219756032 | bytes 12779520 | tf_op jit(solution)/shard_map/dot_general | solution.py:49
  167.3 7.5 %all-to-all-start.1 = ((bf16[16,24,6144]{2,1,0:T(8,128)(2,1)}), bf16[16,24,6144]{2,1,0:T(8,128)(2,1)}, u32[]{:S(2)}, u32[]{:S(2)}) async-start(bf16[16,24,6144]{2,1,0:T(8,128)(2,1)} %bitcast.85), calls=%async_computation.1 | async-start | bytes 9437184 | tf_op jit(solution)/shard_map/all_to_all | solution.py:172
  175.7 70.8 %all-to-all-done.1 = bf16[16,24,6144]{2,1,0:T(8,128)(2,1)} async-done(((bf16[16,24,6144]{2,1,0:T(8,128)(2,1)}), bf16[16,24,6144]{2,1,0:T(8,128)(2,1)}, u32[]{:S(2)}, u32[]{:S(2)}) %all-to-all-start.1) | async-done | bytes 4718624 | tf_op jit(solution)/shard_map/all_to_all | solution.py:172
  246.5 3.9 %reduce_sum.111 = bf16[24,6144]{1,0:T(8,128)(2,1)} reduce(bf16[16,24,6144]{2,1,0:T(8,128)(2,1)} %all-to-all-done.1, bf16[]{:T(256)} %constant.128.clone.1), dimensions={0}, to_apply=%region_14.15 | reduce | flops 2211840 | bytes 5013506 | tf_op jit(solution)/shard_map/reduce_sum | solution.py:171
  250.4 1.2 slice_bitcast_fusion
  251.6 1.5 collective-permute-start.11
  253.2 2.7 collective-permute-start.10
  255.8 1.5 collective-permute-start.9
  257.3 1.3 collective-permute-done.11
  258.6 1.1 collective-permute-done.10
  260.9 1.6 add_convert_fusion.1
  (61 shorter events, 7.9 us)
Async XLA Ops:
  6.5 143.0 %copy-start = (bf16[256,6144]{1,0:T(8,128)(2,1)S(1)}, bf16[256,6144]{1,0:T(8,128)(2,1)}, u32[]{:S(2)}) copy-start(bf16[256,6144]{1,0:T(8,128)(2,1)} %param.19) | copy-start | bytes 9437188
  7.6 8.5 %copy-start.1 = (bf16[128,6144]{1,0:T(8,128)(2,1)S(1)}, bf16[128,6144]{1,0:T(8,128)(2,1)}, u32[]{:S(2)}) copy-start(bf16[128,6144]{1,0:T(8,128)(2,1)} %param.10) | copy-start | bytes 4718596
  13.8 10.2 %collective-permute-start = (bf16[128,128]{1,0:T(8,128)(2,1)}, bf16[128,128]{1,0:T(8,128)(2,1)}, u32[]{:S(2)}, u32[]{:S(2)}) collective-permute-start(bf16[128,128]{1,0:T(8,128)(2,1)} %fusion.33), channel_id=1, source_target_pairs={{0,1},{1,0},{2,3},{3,2},{4,5},{5,4},{6,7},{7,6},{8,9},{9,8},{10,11... | collective-permute-start | bytes 98312 | tf_op jit(solution)/shard_map/ppermute | solution.py:92
  24.7 1.3 collective-permute-start.1
  26.1 6.4 %collective-permute-start.4 = (bf16[2,2,128,128]{3,2,1,0:T(8,128)(2,1)S(1)}, bf16[2,2,128,128]{3,2,1,0:T(8,128)(2,1)S(1)}, u32[]{:S(2)}, u32[]{:S(2)}) collective-permute-start(bf16[2,2,128,128]{3,2,1,0:T(8,128)(2,1)S(1)} %maximum_select_fusion.1), channel_id=1, source_target_pairs={{0,32},{32,64},{64,96},{96,0},{1,33},{33,65},{65,97},{97,1},{2,34}... | collective-permute-start | bytes 393224 | tf_op jit(solution)/shard_map/ppermute | solution.py:101
  26.2 8.0 %collective-permute-start.3 = (bf16[2,2,128,128]{3,2,1,0:T(8,128)(2,1)S(1)}, bf16[2,2,128,128]{3,2,1,0:T(8,128)(2,1)S(1)}, u32[]{:S(2)}, u32[]{:S(2)}) collective-permute-start(bf16[2,2,128,128]{3,2,1,0:T(8,128)(2,1)S(1)} %maximum_select_fusion.1), channel_id=1, source_target_pairs={{0,64},{32,96},{64,0},{96,32},{1,65},{33,97},{65,1},{97,33},{2,66}... | collective-permute-start | bytes 393224 | tf_op jit(solution)/shard_map/ppermute | solution.py:101
  28.6 7.5 %collective-permute-start.2 = (bf16[2,2,128,128]{3,2,1,0:T(8,128)(2,1)S(1)}, bf16[2,2,128,128]{3,2,1,0:T(8,128)(2,1)S(1)}, u32[]{:S(2)}, u32[]{:S(2)}) collective-permute-start(bf16[2,2,128,128]{3,2,1,0:T(8,128)(2,1)S(1)} %maximum_select_fusion.1), channel_id=1, source_target_pairs={{0,96},{32,0},{64,32},{96,64},{1,97},{33,1},{65,33},{97,65},{2,98}... | collective-permute-start | bytes 393224 | tf_op jit(solution)/shard_map/ppermute | solution.py:101
  48.4 7.5 %copy-start.3 = (s32[8,2]{0,1:T(2,128)S(1)}, s32[8,2]{0,1:T(2,128)}, u32[]{:S(2)}) copy-start(s32[8,2]{0,1:T(2,128)} %param.15) | copy-start | bytes 196
  48.4 28.1 %all-to-all-start = ((bf16[16,8,6144]{2,1,0:T(8,128)(2,1)}), bf16[16,8,6144]{2,1,0:T(8,128)(2,1)}, u32[]{:S(2)}, u32[]{:S(2)}) async-start(bf16[16,8,6144]{2,1,0:T(8,128)(2,1)} %fusion.1), calls=%async_computation | async-start | bytes 3145728 | tf_op jit(solution)/shard_map/all_to_all | solution.py:130
  55.8 87.4 %all-gather.2.cloned.1.call-start = ((), (), s32[]{:S(2)}) async-start(), calls=%async_computation.2 | async-start | bytes 9732096 | tf_op jit(solution)/shard_map/all_gather | solution.py:160
  80.6 4.7 %collective-permute-start.7 = (bf16[6,6144]{1,0:T(8,128)(2,1)S(1)}, bf16[6,6144]{1,0:T(8,128)(2,1)S(1)}, u32[]{:S(2)}, u32[]{:S(2)}) collective-permute-start(bf16[6,6144]{1,0:T(8,128)(2,1)S(1)} %get-tuple-element.12), channel_id=1, source_target_pairs={{0,12},{4,0},{8,4},{12,8},{1,13},{5,1},{9,5},{13,9},{2,14},{6,2},{... | collective-permute-start | bytes 221192 | tf_op jit(solution)/shard_map/ppermute | solution.py:157
  82.0 6.1 %collective-permute-start.6 = (bf16[6,6144]{1,0:T(8,128)(2,1)S(1)}, bf16[6,6144]{1,0:T(8,128)(2,1)S(1)}, u32[]{:S(2)}, u32[]{:S(2)}) collective-permute-start(bf16[6,6144]{1,0:T(8,128)(2,1)S(1)} %get-tuple-element.13), channel_id=1, source_target_pairs={{0,8},{4,12},{8,0},{12,4},{1,9},{5,13},{9,1},{13,5},{2,10},{6,14},... | collective-permute-start | bytes 221192 | tf_op jit(solution)/shard_map/ppermute | solution.py:157
  83.6 5.8 %collective-permute-start.5 = (bf16[6,6144]{1,0:T(8,128)(2,1)S(1)}, bf16[6,6144]{1,0:T(8,128)(2,1)S(1)}, u32[]{:S(2)}, u32[]{:S(2)}) collective-permute-start(bf16[6,6144]{1,0:T(8,128)(2,1)S(1)} %get-tuple-element.14), channel_id=1, source_target_pairs={{0,4},{4,8},{8,12},{12,0},{1,5},{5,9},{9,13},{13,1},{2,6},{6,10},{... | collective-permute-start | bytes 221192 | tf_op jit(solution)/shard_map/ppermute | solution.py:157
  90.4 4.0 %copy-start.2 = (bf16[6144,256]{1,0:T(8,128)(2,1)S(1)}, bf16[6144,256]{1,0:T(8,128)(2,1)}, u32[]{:S(2)}) copy-start(bf16[6144,256]{1,0:T(8,128)(2,1)} %param.18) | copy-start | bytes 9437188
  153.1 8.3 %collective-permute-start.8 = (bf16[384,6144]{1,0:T(8,128)(2,1)}, bf16[384,6144]{1,0:T(8,128)(2,1)}, u32[]{:S(2)}, u32[]{:S(2)}) collective-permute-start(bf16[384,6144]{1,0:T(8,128)(2,1)} %convolution_convert_fusion), channel_id=1, source_target_pairs={{0,16},{16,0},{1,17},{17,1},{2,18},{18,2},{3,19},{19,3},{4,20},{20... | collective-permute-start | bytes 14155784 | tf_op jit(solution)/shard_map/ppermute | solution.py:166
  167.3 8.2 %copy-start.4 = (bf16[6144,4]{0,1:T(4,128)(2,1)S(1)}, bf16[6144,4]{0,1:T(4,128)(2,1)}, u32[]{:S(2)}) copy-start(bf16[6144,4]{0,1:T(4,128)(2,1)} %param.16) | copy-start | bytes 147460
  167.3 79.2 %all-to-all-start.1 = ((bf16[16,24,6144]{2,1,0:T(8,128)(2,1)}), bf16[16,24,6144]{2,1,0:T(8,128)(2,1)}, u32[]{:S(2)}, u32[]{:S(2)}) async-start(bf16[16,24,6144]{2,1,0:T(8,128)(2,1)} %bitcast.85), calls=%async_computation.1 | async-start | bytes 9437184 | tf_op jit(solution)/shard_map/all_to_all | solution.py:172
  251.6 6.9 %collective-permute-start.11 = (bf16[6,6144]{1,0:T(8,128)(2,1)S(1)}, bf16[6,6144]{1,0:T(8,128)(2,1)S(1)}, u32[]{:S(2)}, u32[]{:S(2)}) collective-permute-start(bf16[6,6144]{1,0:T(8,128)(2,1)S(1)} %get-tuple-element.16), channel_id=1, source_target_pairs={{0,4},{4,8},{8,12},{12,0},{1,5},{5,9},{9,13},{13,1},{2,6},{6,10},{... | collective-permute-start | bytes 221192 | tf_op jit(solution)/shard_map/ppermute | solution.py:181
  253.2 6.6 %collective-permute-start.10 = (bf16[6,6144]{1,0:T(8,128)(2,1)S(1)}, bf16[6,6144]{1,0:T(8,128)(2,1)S(1)}, u32[]{:S(2)}, u32[]{:S(2)}) collective-permute-start(bf16[6,6144]{1,0:T(8,128)(2,1)S(1)} %get-tuple-element.17), channel_id=1, source_target_pairs={{0,8},{4,12},{8,0},{12,4},{1,9},{5,13},{9,1},{13,5},{2,10},{6,14},... | collective-permute-start | bytes 221192 | tf_op jit(solution)/shard_map/ppermute | solution.py:181
  255.8 4.6 %collective-permute-start.9 = (bf16[6,6144]{1,0:T(8,128)(2,1)S(1)}, bf16[6,6144]{1,0:T(8,128)(2,1)S(1)}, u32[]{:S(2)}, u32[]{:S(2)}) collective-permute-start(bf16[6,6144]{1,0:T(8,128)(2,1)S(1)} %get-tuple-element.18), channel_id=1, source_target_pairs={{0,12},{4,0},{8,4},{12,8},{1,13},{5,1},{9,5},{13,9},{2,14},{6,2},{... | collective-permute-start | bytes 221192 | tf_op jit(solution)/shard_map/ppermute | solution.py:181
Sparse Core Ops, SparseCore 0:
  90.5 52.7 all-gather.1

commit v13 on v8

--- a/solution.py
+++ b/solution.py
@@ -80,10 +80,6 @@
     positions = shard * tok_dev + jnp.arange(tok_dev, dtype=jnp.int32)
     document, in_document = doc_layout(doc_lengths, positions)
     normed_in = rms_rows(tokens).astype(jnp.bfloat16)
-    queries = jnp.dot(normed_in, query_weight, preferred_element_type=jnp.float32).reshape(
-        tok_dev, per_group, head_dim
-    )
-    queries = rotate(queries, in_document).astype(jnp.bfloat16)
     half_part = jnp.dot(normed_in, key_value_weight, preferred_element_type=jnp.float32)
     rotated = rotate(half_part[:, None, :], in_document)[:, 0, :]
     holds_keys = group % 2 == 0
@@ -100,6 +96,11 @@
     ring = [pair] + [
         lax.ppermute(pair, "z", [(i, (i - k) % nz) for i in range(nz)]) for k in range(1, nz)
     ]
+    query_in, unused = lax.optimization_barrier((normed_in, pair))
+    queries = jnp.dot(query_in, query_weight, preferred_element_type=jnp.float32).reshape(
+        tok_dev, per_group, head_dim
+    )
+    queries = rotate(queries, in_document).astype(jnp.bfloat16)
     gathered = jnp.stack(ring).transpose(2, 0, 1, 3, 4).reshape(2, -1, head_dim)
     key_piece = gathered[0]
     value_piece = gathered[1]

time: 271 us -> 269 us (level)
  waiting for transfers between devices: 156 us -> 150 us
  other arithmetic: 17.7 us -> 22 us
    ppermute x3, waiting for transfers between devices: 7.29 us -> 0.01 us  [per_device(): lax.ppermute(pair, 'z', [(i, (i - k) % nz) for i in range(nz)])]
    unnamed x13 -> x19, local copies, waits for them, and re-layouts: 5.19 us -> 6.34 us
  transfers between devices with their start and end apart: 15 -> 15, of which waited for: 14 -> 12; matrix products, arithmetic and copies ran while one was open for 9% -> 9% of each run, Pallas kernels for 0% -> 0%
where the time goes in v13:
time: 269 us; the launch traced here: 268 us
  waiting for transfers between devices  150 us (56%)
  matrix products  41.7 us (16%)
  starting transfers between devices  28.7 us (11%)
  other arithmetic  22 us (8%)
  between operations  13.7 us (5%)
  local copies, waits for them, and re-layouts  12.1 us (4%)
    all_to_all x1, waiting for transfers between devices, per_device(): lax.all_to_all(lines, ('y', 'z'), split_axis=0, concat_axis=0, tiled=True)  70.8 us
    all_gather x1, waiting for transfers between devices, per_device(): rows = lax.all_gather(arrived, ('c', 'y', 'z'), axis=0, tiled=True)  47.5 us
    all_to_all x1, waiting for transfers between devices, per_device(): lax.all_to_all(blocks, ('x', 'y'), split_axis=0, concat_axis=0, tiled=True)  19.7 us
    dot_general x2, matrix products, expert_rows(): both = jnp.dot(rows, gate_up_weight, preferred_element_type=jnp.float32)  12.3 us
    dot_general x2, matrix products, expert_rows(): jnp.dot(activated, down_weight, preferred_element_type=jnp.float32)  9.52 us
    all_to_all x1, starting transfers between devices, per_device(): lax.all_to_all(lines, ('y', 'z'), split_axis=0, concat_axis=0, tiled=True)  7.51 us
    all_to_all x1, starting transfers between devices, per_device(): lax.all_to_all(blocks, ('x', 'y'), split_axis=0, concat_axis=0, tiled=True)  7.41 us
    unnamed x19, local copies, waits for them, and re-layouts  6.34 us
  transfers between devices with their start and end apart: 15, of which 12 were waited for; matrix products, arithmetic and copies ran while one was open for 9% of the time, Pallas kernels for 0%

profile of v13, /device:TPU:112, one launch (start us, length us, event | category | flops | bytes accessed | tf_op | source)
XLA Modules:
  0.0 267.9 jit_solution(9980513326121093377)
XLA Ops:
  6.6 1.0 reduce-window.8
  7.6 1.9 fusion.8
  9.5 0.7 fusion.43
  10.3 1.8 fusion.9
  12.0 1.1 copy-done.1
  14.2 1.4 collective-permute-start
  15.8 0.8 compare_and_fusion
  16.6 1.6 collective-permute-done
  18.8 1.0 multiply_cosine_fusion
  20.7 2.5 collective-permute-start.3
  23.2 4.8 %fusion.72 = f32[128,384]{0,1:T(8,128)S(1)} fusion(bf16[128,6144]{1,0:T(8,128)(2,1)} %copy-done.1, bf16[6144,384]{1,0:T(8,128)(2,1)} %param.11), kind=kOutput, calls=%fused_computation.144 | convolution fusion | flops 603979776 | bytes 6488064 | tf_op jit(solution)/shard_map/dot_general | solution.py:100
  28.8 1.0 copy.33
  29.8 1.6 subtract_convert_fusion
  31.4 1.0 maximum_select_fusion.1
  32.4 1.1 maximum_bitcast_fusion
  34.3 2.0 fusion.70
  36.3 2.5 multiply_select_fusion
  38.8 2.5 fusion.11
  41.4 4.5 %fusion.1 = bf16[16,8,6144]{2,1,0:T(8,128)(2,1)} fusion(bf16[128,384]{0,1:T(8,128)(2,1)S(1)} %bitcast.95, bf16[384,6144]{1,0:T(8,128)(2,1)} %param.13), kind=kOutput, calls=%fused_computation.7 | convolution fusion | flops 604766208 | bytes 6389760 | tf_op jit(solution)/shard_map/dot_general | solution.py:128
  45.9 7.4 %all-to-all-start = ((bf16[16,8,6144]{2,1,0:T(8,128)(2,1)}), bf16[16,8,6144]{2,1,0:T(8,128)(2,1)}, u32[]{:S(2)}, u32[]{:S(2)}) async-start(bf16[16,8,6144]{2,1,0:T(8,128)(2,1)} %fusion.1), calls=%async_computation | async-start | bytes 3145728 | tf_op jit(solution)/shard_map/all_to_all | solution.py:131
  54.2 19.7 %all-to-all-done = bf16[16,8,6144]{2,1,0:T(8,128)(2,1)} async-done(((bf16[16,8,6144]{2,1,0:T(8,128)(2,1)}), bf16[16,8,6144]{2,1,0:T(8,128)(2,1)}, u32[]{:S(2)}, u32[]{:S(2)}) %all-to-all-start) | async-done | bytes 1572896 | tf_op jit(solution)/shard_map/all_to_all | solution.py:131
  74.0 1.6 convert_reduce_fusion
  75.6 1.1 multiply_reduce_fusion
  76.7 1.0 multiply_convert_fusion
  78.1 1.4 collective-permute-start.7
  79.5 1.7 collective-permute-start.6
  81.2 0.9 collective-permute-start.5
  82.8 2.9 %collective-permute-done.6 = bf16[6,6144]{1,0:T(8,128)(2,1)S(1)} collective-permute-done((bf16[6,6144]{1,0:T(8,128)(2,1)S(1)}, bf16[6,6144]{1,0:T(8,128)(2,1)S(1)}, u32[]{:S(2)}, u32[]{:S(2)}) %collective-permute-start.6) | collective-permute-done | bytes 73760 | tf_op jit(solution)/shard_map/ppermute | solution.py:158
  85.6 1.4 collective-permute-done.5
  87.0 0.9 pad_maximum_fusion
  87.9 4.0 %constant_dynamic-update-slice_fusion.1 = bf16[6144,512]{1,0:T(8,128)(2,1)} fusion(bf16[6144,256]{1,0:T(8,128)(2,1)} %param.17), kind=kLoop, calls=%fused_computation.91 | loop fusion | bytes 6291456
  91.9 2.0 constant_dynamic-update-slice_fusion
  93.9 47.5 %all-gather.2.cloned.1.call-done = bf16[768,6144]{1,0:T(8,128)(2,1)} async-done(((bf16[24,6144]{1,0:T(8,128)(2,1)}), bf16[768,6144]{1,0:T(8,128)(2,1)}) %all-gather.2.cloned.1.call-update) | async-done | bytes 9437200 | tf_op jit(solution)/shard_map/all_gather | solution.py:161
  141.4 6.2 %fusion.4 = f32[384,512]{1,0:T(8,128)S(1)} fusion(bf16[6144,512]{1,0:T(8,128)(2,1)} %constant_dynamic-update-slice_fusion, bf16[768,6144]{1,0:T(8,128)(2,1)} %all-gather.2.cloned.1.call-done, s32[]{:T(128)S(6)} %select_n.150), kind=kOutput, calls=%fused_computation.12 | convolution fusion | flops 2415919104 | bytes 11796484 | tf_op jit(solution)/shard_map/dot_general | solution.py:45
  147.7 3.5 %convolution_convert_fusion = bf16[384,6144]{1,0:T(8,128)(2,1)} fusion(bf16[384,256]{1,0:T(8,128)(2,1)S(1)} %fusion.13, bf16[256,6144]{1,0:T(8,128)(2,1)S(1)} %copy-done), kind=kOutput, calls=%fused_computation.4 | convolution fusion | flops 1210318848 | bytes 8060928 | tf_op jit(solution)/shard_map/dot_general | solution.py:49
  151.4 6.2 %fusion.6 = f32[384,512]{1,0:T(8,128)S(1)} fusion(bf16[6144,512]{1,0:T(8,128)(2,1)} %constant_dynamic-update-slice_fusion, bf16[768,6144]{1,0:T(8,128)(2,1)} %all-gather.2.cloned.1.call-done, s32[]{:T(128)S(6)} %select_n.149), kind=kOutput, calls=%fused_computation.14 | convolution fusion | flops 2415919104 | bytes 11796484 | tf_op jit(solution)/shard_map/dot_general | solution.py:45
  157.7 1.7 collective-permute-done.8
  159.4 6.0 %add_convert_fusion = bf16[384,6144]{1,0:T(8,128)(2,1)} fusion(bf16[384,6144]{1,0:T(8,128)(2,1)} %collective-permute-done.8, bf16[384,256]{1,0:T(8,128)(2,1)S(1)} %fusion.14, bf16[256,6144]{1,0:T(8,128)(2,1)S(1)} %copy-done), kind=kOutput, calls=%fused_computation.3 | convolution fusion | flops 1219756032 | bytes 12779520 | tf_op jit(solution)/shard_map/dot_general | solution.py:49
  165.4 7.5 %all-to-all-start.1 = ((bf16[16,24,6144]{2,1,0:T(8,128)(2,1)}), bf16[16,24,6144]{2,1,0:T(8,128)(2,1)}, u32[]{:S(2)}, u32[]{:S(2)}) async-start(bf16[16,24,6144]{2,1,0:T(8,128)(2,1)} %bitcast.87), calls=%async_computation.1 | async-start | bytes 9437184 | tf_op jit(solution)/shard_map/all_to_all | solution.py:173
  173.8 70.8 %all-to-all-done.1 = bf16[16,24,6144]{2,1,0:T(8,128)(2,1)} async-done(((bf16[16,24,6144]{2,1,0:T(8,128)(2,1)}), bf16[16,24,6144]{2,1,0:T(8,128)(2,1)}, u32[]{:S(2)}, u32[]{:S(2)}) %all-to-all-start.1) | async-done | bytes 4718624 | tf_op jit(solution)/shard_map/all_to_all | solution.py:173
  244.6 3.9 %reduce_sum.112 = bf16[24,6144]{1,0:T(8,128)(2,1)} reduce(bf16[16,24,6144]{2,1,0:T(8,128)(2,1)} %all-to-all-done.1, bf16[]{:T(256)} %constant.129.clone.1), dimensions={0}, to_apply=%region_15.16 | reduce | flops 2211840 | bytes 5013506 | tf_op jit(solution)/shard_map/reduce_sum | solution.py:172
  248.5 1.2 slice_bitcast_fusion
  249.7 1.5 collective-permute-start.11
  251.2 2.8 %collective-permute-start.10 = (bf16[6,6144]{1,0:T(8,128)(2,1)S(1)}, bf16[6,6144]{1,0:T(8,128)(2,1)S(1)}, u32[]{:S(2)}, u32[]{:S(2)}) collective-permute-start(bf16[6,6144]{1,0:T(8,128)(2,1)S(1)} %get-tuple-element.19), channel_id=1, source_target_pairs={{0,8},{4,12},{8,0},{12,4},{1,9},{5,13},{9,1},{13,5},{2,10},{6,14},... | collective-permute-start | bytes 221192 | tf_op jit(solution)/shard_map/ppermute | solution.py:182
  254.0 1.4 collective-permute-start.9
  255.5 1.2 collective-permute-done.11
  256.7 1.2 collective-permute-done.10
  258.6 2.5 fusion.3
  (66 shorter events, 8.5 us)
Async XLA Ops:
  6.5 141.1 %copy-start = (bf16[256,6144]{1,0:T(8,128)(2,1)S(1)}, bf16[256,6144]{1,0:T(8,128)(2,1)}, u32[]{:S(2)}) copy-start(bf16[256,6144]{1,0:T(8,128)(2,1)} %param.19) | copy-start | bytes 9437188
  7.6 5.6 %copy-start.3 = (bf16[6144,128]{1,0:T(8,128)(2,1)S(1)}, bf16[6144,128]{1,0:T(8,128)(2,1)}, u32[]{:S(2)}) copy-start(bf16[6144,128]{1,0:T(8,128)(2,1)} %param.12) | copy-start | bytes 4718596
  12.0 1.2 copy-start.1
  14.2 4.0 %collective-permute-start = (bf16[128,128]{1,0:T(8,128)(2,1)S(1)}, bf16[128,128]{1,0:T(8,128)(2,1)S(1)}, u32[]{:S(2)}, u32[]{:S(2)}) collective-permute-start(bf16[128,128]{1,0:T(8,128)(2,1)S(1)} %fusion.30), channel_id=1, source_target_pairs={{0,1},{1,0},{2,3},{3,2},{4,5},{5,4},{6,7},{7,6},{8,9},{9,8},{10,11... | collective-permute-start | bytes 98312 | tf_op jit(solution)/shard_map/ppermute | solution.py:88
  18.8 1.3 collective-permute-start.1
  20.1 7.9 %copy-start.5 = (bf16[2,128,128]{2,1,0:T(8,128)(2,1)}, bf16[2,128,128]{2,1,0:T(8,128)(2,1)S(1)}, u32[]{:S(2)}) copy-start(bf16[2,128,128]{2,1,0:T(8,128)(2,1)S(1)} %collective-permute-done.1) | copy-start | bytes 196612
  20.7 11.7 %collective-permute-start.4 = (bf16[2,2,128,128]{3,2,1,0:T(8,128)(2,1)}, bf16[2,2,128,128]{3,2,1,0:T(8,128)(2,1)}, u32[]{:S(2)}, u32[]{:S(2)}) collective-permute-start(bf16[2,2,128,128]{3,2,1,0:T(8,128)(2,1)} %maximum_select_fusion), channel_id=1, source_target_pairs={{0,32},{32,64},{64,96},{96,0},{1,33},{33,65},{65,97},{97,1},{2,34}... | collective-permute-start | bytes 393224 | tf_op jit(solution)/shard_map/ppermute | solution.py:97
  20.7 11.7 %collective-permute-start.3 = (bf16[2,2,128,128]{3,2,1,0:T(8,128)(2,1)}, bf16[2,2,128,128]{3,2,1,0:T(8,128)(2,1)}, u32[]{:S(2)}, u32[]{:S(2)}) collective-permute-start(bf16[2,2,128,128]{3,2,1,0:T(8,128)(2,1)} %maximum_select_fusion), channel_id=1, source_target_pairs={{0,64},{32,96},{64,0},{96,32},{1,65},{33,97},{65,1},{97,33},{2,66}... | collective-permute-start | bytes 393224 | tf_op jit(solution)/shard_map/ppermute | solution.py:97
  23.2 9.2 %collective-permute-start.2 = (bf16[2,2,128,128]{3,2,1,0:T(8,128)(2,1)}, bf16[2,2,128,128]{3,2,1,0:T(8,128)(2,1)}, u32[]{:S(2)}, u32[]{:S(2)}) collective-permute-start(bf16[2,2,128,128]{3,2,1,0:T(8,128)(2,1)} %maximum_select_fusion), channel_id=1, source_target_pairs={{0,96},{32,0},{64,32},{96,64},{1,97},{33,1},{65,33},{97,65},{2,98}... | collective-permute-start | bytes 393224 | tf_op jit(solution)/shard_map/ppermute | solution.py:97
  31.4 4.9 %copy-start.4 = (pred[128,1024]{1,0:T(8,128)(4,1)S(1)}, pred[128,1024]{1,0:T(8,128)(4,1)}, u32[]{:S(2)}) copy-start(pred[128,1024]{1,0:T(8,128)(4,1)} %compare_and_fusion) | copy-start | bytes 393220
  45.9 7.5 %copy-start.6 = (s32[8,2]{0,1:T(2,128)S(1)}, s32[8,2]{0,1:T(2,128)}, u32[]{:S(2)}) copy-start(s32[8,2]{0,1:T(2,128)} %param.15) | copy-start | bytes 196
  45.9 28.1 %all-to-all-start = ((bf16[16,8,6144]{2,1,0:T(8,128)(2,1)}), bf16[16,8,6144]{2,1,0:T(8,128)(2,1)}, u32[]{:S(2)}, u32[]{:S(2)}) async-start(bf16[16,8,6144]{2,1,0:T(8,128)(2,1)} %fusion.1), calls=%async_computation | async-start | bytes 3145728 | tf_op jit(solution)/shard_map/all_to_all | solution.py:131
  53.3 88.1 %all-gather.2.cloned.1.call-start = ((), (), s32[]{:S(2)}) async-start(), calls=%async_computation.2 | async-start | bytes 9732096 | tf_op jit(solution)/shard_map/all_gather | solution.py:161
  78.1 4.7 %collective-permute-start.7 = (bf16[6,6144]{1,0:T(8,128)(2,1)S(1)}, bf16[6,6144]{1,0:T(8,128)(2,1)S(1)}, u32[]{:S(2)}, u32[]{:S(2)}) collective-permute-start(bf16[6,6144]{1,0:T(8,128)(2,1)S(1)} %get-tuple-element.14), channel_id=1, source_target_pairs={{0,12},{4,0},{8,4},{12,8},{1,13},{5,1},{9,5},{13,9},{2,14},{6,2},{... | collective-permute-start | bytes 221192 | tf_op jit(solution)/shard_map/ppermute | solution.py:158
  79.5 6.1 %collective-permute-start.6 = (bf16[6,6144]{1,0:T(8,128)(2,1)S(1)}, bf16[6,6144]{1,0:T(8,128)(2,1)S(1)}, u32[]{:S(2)}, u32[]{:S(2)}) collective-permute-start(bf16[6,6144]{1,0:T(8,128)(2,1)S(1)} %get-tuple-element.15), channel_id=1, source_target_pairs={{0,8},{4,12},{8,0},{12,4},{1,9},{5,13},{9,1},{13,5},{2,10},{6,14},... | collective-permute-start | bytes 221192 | tf_op jit(solution)/shard_map/ppermute | solution.py:158
  81.2 5.8 %collective-permute-start.5 = (bf16[6,6144]{1,0:T(8,128)(2,1)S(1)}, bf16[6,6144]{1,0:T(8,128)(2,1)S(1)}, u32[]{:S(2)}, u32[]{:S(2)}) collective-permute-start(bf16[6,6144]{1,0:T(8,128)(2,1)S(1)} %get-tuple-element.16), channel_id=1, source_target_pairs={{0,4},{4,8},{8,12},{12,0},{1,5},{5,9},{9,13},{13,1},{2,6},{6,10},{... | collective-permute-start | bytes 221192 | tf_op jit(solution)/shard_map/ppermute | solution.py:158
  87.9 4.0 %copy-start.2 = (bf16[6144,256]{1,0:T(8,128)(2,1)S(1)}, bf16[6144,256]{1,0:T(8,128)(2,1)}, u32[]{:S(2)}) copy-start(bf16[6144,256]{1,0:T(8,128)(2,1)} %param.18) | copy-start | bytes 9437188
  151.2 8.3 %collective-permute-start.8 = (bf16[384,6144]{1,0:T(8,128)(2,1)}, bf16[384,6144]{1,0:T(8,128)(2,1)}, u32[]{:S(2)}, u32[]{:S(2)}) collective-permute-start(bf16[384,6144]{1,0:T(8,128)(2,1)} %convolution_convert_fusion), channel_id=1, source_target_pairs={{0,16},{16,0},{1,17},{17,1},{2,18},{18,2},{3,19},{19,3},{4,20},{20... | collective-permute-start | bytes 14155784 | tf_op jit(solution)/shard_map/ppermute | solution.py:167
  165.4 7.5 %copy-start.7 = (bf16[6144,4]{0,1:T(4,128)(2,1)S(1)}, bf16[6144,4]{0,1:T(4,128)(2,1)}, u32[]{:S(2)}) copy-start(bf16[6144,4]{0,1:T(4,128)(2,1)} %param.16) | copy-start | bytes 147460
  165.4 79.2 %all-to-all-start.1 = ((bf16[16,24,6144]{2,1,0:T(8,128)(2,1)}), bf16[16,24,6144]{2,1,0:T(8,128)(2,1)}, u32[]{:S(2)}, u32[]{:S(2)}) async-start(bf16[16,24,6144]{2,1,0:T(8,128)(2,1)} %bitcast.87), calls=%async_computation.1 | async-start | bytes 9437184 | tf_op jit(solution)/shard_map/all_to_all | solution.py:173
  249.7 6.9 %collective-permute-start.11 = (bf16[6,6144]{1,0:T(8,128)(2,1)S(1)}, bf16[6,6144]{1,0:T(8,128)(2,1)S(1)}, u32[]{:S(2)}, u32[]{:S(2)}) collective-permute-start(bf16[6,6144]{1,0:T(8,128)(2,1)S(1)} %get-tuple-element.18), channel_id=1, source_target_pairs={{0,4},{4,8},{8,12},{12,0},{1,5},{5,9},{9,13},{13,1},{2,6},{6,10},{... | collective-permute-start | bytes 221192 | tf_op jit(solution)/shard_map/ppermute | solution.py:182
  251.2 6.6 %collective-permute-start.10 = (bf16[6,6144]{1,0:T(8,128)(2,1)S(1)}, bf16[6,6144]{1,0:T(8,128)(2,1)S(1)}, u32[]{:S(2)}, u32[]{:S(2)}) collective-permute-start(bf16[6,6144]{1,0:T(8,128)(2,1)S(1)} %get-tuple-element.19), channel_id=1, source_target_pairs={{0,8},{4,12},{8,0},{12,4},{1,9},{5,13},{9,1},{13,5},{2,10},{6,14},... | collective-permute-start | bytes 221192 | tf_op jit(solution)/shard_map/ppermute | solution.py:182
  254.0 4.6 %collective-permute-start.9 = (bf16[6,6144]{1,0:T(8,128)(2,1)S(1)}, bf16[6,6144]{1,0:T(8,128)(2,1)S(1)}, u32[]{:S(2)}, u32[]{:S(2)}) collective-permute-start(bf16[6,6144]{1,0:T(8,128)(2,1)S(1)} %get-tuple-element.20), channel_id=1, source_target_pairs={{0,12},{4,0},{8,4},{12,8},{1,13},{5,1},{9,5},{13,9},{2,14},{6,2},{... | collective-permute-start | bytes 221192 | tf_op jit(solution)/shard_map/ppermute | solution.py:182
Sparse Core Ops, SparseCore 0:
  88.0 53.3 all-gather.1

commit v14 on v13

--- a/solution.py
+++ b/solution.py
@@ -97,7 +97,13 @@
         lax.ppermute(pair, "z", [(i, (i - k) % nz) for i in range(nz)]) for k in range(1, nz)
     ]
     query_in, unused = lax.optimization_barrier((normed_in, pair))
-    queries = jnp.dot(query_in, query_weight, preferred_element_type=jnp.float32).reshape(
+    first_head = jnp.dot(
+        normed_in, query_weight[:, :head_dim], preferred_element_type=jnp.float32
+    )
+    other_heads = jnp.dot(
+        query_in, query_weight[:, head_dim:], preferred_element_type=jnp.float32
+    )
+    queries = jnp.concatenate([first_head, other_heads], axis=1).reshape(
         tok_dev, per_group, head_dim
     )
     queries = rotate(queries, in_document).astype(jnp.bfloat16)

time: 269 us -> 268 us (level)
    dot_general x1 -> x2, matrix products: 4.75 us -> 5.58 us  [the longest x1 2.94 us: per_device(): jnp.dot(query_in, query_weight[:, head_dim:], preferred_element_type=jnp....]
  transfers between devices with their start and end apart: 15 -> 15, of which waited for: 12 -> 11; matrix products, arithmetic and copies ran while one was open for 9% -> 10% of each run, Pallas kernels for 0% -> 0%
where the time goes in v14:
time: 268 us; the launch traced here: 267 us
  waiting for transfers between devices  148 us (55%)
  matrix products  42.5 us (16%)
  starting transfers between devices  28.6 us (11%)
  other arithmetic  22.9 us (9%)
  between operations  13.7 us (5%)
  local copies, waits for them, and re-layouts  11 us (4%)
    all_to_all x1, waiting for transfers between devices, per_device(): lax.all_to_all(lines, ('y', 'z'), split_axis=0, concat_axis=0, tiled=True)  70.9 us
    all_gather x1, waiting for transfers between devices, per_device(): rows = lax.all_gather(arrived, ('c', 'y', 'z'), axis=0, tiled=True)  47.5 us
    all_to_all x1, waiting for transfers between devices, per_device(): lax.all_to_all(blocks, ('x', 'y'), split_axis=0, concat_axis=0, tiled=True)  19.7 us
    dot_general x2, matrix products, expert_rows(): both = jnp.dot(rows, gate_up_weight, preferred_element_type=jnp.float32)  12.3 us
    dot_general x2, matrix products, expert_rows(): jnp.dot(activated, down_weight, preferred_element_type=jnp.float32)  9.52 us
    all_to_all x1, starting transfers between devices, per_device(): lax.all_to_all(lines, ('y', 'z'), split_axis=0, concat_axis=0, tiled=True)  7.51 us
    all_to_all x1, starting transfers between devices, per_device(): lax.all_to_all(blocks, ('x', 'y'), split_axis=0, concat_axis=0, tiled=True)  7.4 us
    ppermute x3, starting transfers between devices, per_device(): lax.ppermute(summed[k], 'x', [(i, (i - k) % nx) for i in range(nx)])  5.6 us
  transfers between devices with their start and end apart: 15, of which 11 were waited for; matrix products, arithmetic and copies ran while one was open for 10% of the time, Pallas kernels for 0%

profile of v14, /device:TPU:112, one launch (start us, length us, event | category | flops | bytes accessed | tf_op | source)
XLA Modules:
  0.0 267.0 jit_solution(15781837747614814460)
XLA Ops:
  6.6 1.0 reduce-window.8
  7.6 1.9 fusion.8
  9.5 0.7 fusion.47
  10.3 1.8 fusion.9
  13.0 1.4 collective-permute-start
  14.6 2.6 fusion.13
  17.3 0.8 compare_and_fusion
  18.8 1.0 multiply_cosine_fusion
  20.7 2.5 collective-permute-start.3
  23.1 2.9 %fusion.10 = f32[128,256]{1,0:T(8,128)S(1)} fusion(bf16[128,6144]{1,0:T(8,128)(2,1)} %copy-done.1, bf16[6144,384]{1,0:T(8,128)(2,1)} %param.11), kind=kOutput, calls=%fused_computation.21 | convolution fusion | flops 402653184 | bytes 4849664 | tf_op jit(solution)/shard_map/dot_general | solution.py:103
  26.1 0.9 pad_maximum_fusion.1
  27.9 1.0 copy.36
  28.9 1.6 subtract_convert_fusion
  30.5 1.0 maximum_select_fusion.1
  31.5 1.1 maximum_bitcast_fusion
  33.4 2.0 fusion.74
  35.4 2.5 multiply_select_fusion
  37.9 2.5 fusion.15
  40.5 4.5 %fusion.1 = bf16[16,8,6144]{2,1,0:T(8,128)(2,1)} fusion(bf16[128,384]{0,1:T(8,128)(2,1)S(1)} %bitcast.95, bf16[384,6144]{1,0:T(8,128)(2,1)} %param.13), kind=kOutput, calls=%fused_computation.7 | convolution fusion | flops 604766208 | bytes 6389760 | tf_op jit(solution)/shard_map/dot_general | solution.py:134
  45.0 7.4 %all-to-all-start = ((bf16[16,8,6144]{2,1,0:T(8,128)(2,1)}), bf16[16,8,6144]{2,1,0:T(8,128)(2,1)}, u32[]{:S(2)}, u32[]{:S(2)}) async-start(bf16[16,8,6144]{2,1,0:T(8,128)(2,1)} %fusion.1), calls=%async_computation | async-start | bytes 3145728 | tf_op jit(solution)/shard_map/all_to_all | solution.py:137
  53.4 19.7 %all-to-all-done = bf16[16,8,6144]{2,1,0:T(8,128)(2,1)} async-done(((bf16[16,8,6144]{2,1,0:T(8,128)(2,1)}), bf16[16,8,6144]{2,1,0:T(8,128)(2,1)}, u32[]{:S(2)}, u32[]{:S(2)}) %all-to-all-start) | async-done | bytes 1572896 | tf_op jit(solution)/shard_map/all_to_all | solution.py:137
  73.1 1.6 convert_reduce_fusion
  74.7 1.1 multiply_reduce_fusion
  75.8 1.0 multiply_convert_fusion
  77.2 1.4 collective-permute-start.7
  78.6 1.7 collective-permute-start.6
  80.3 0.9 collective-permute-start.5
  81.9 2.9 %collective-permute-done.6 = bf16[6,6144]{1,0:T(8,128)(2,1)S(1)} collective-permute-done((bf16[6,6144]{1,0:T(8,128)(2,1)S(1)}, bf16[6,6144]{1,0:T(8,128)(2,1)S(1)}, u32[]{:S(2)}, u32[]{:S(2)}) %collective-permute-start.6) | collective-permute-done | bytes 73760 | tf_op jit(solution)/shard_map/ppermute | solution.py:164
  84.7 1.4 collective-permute-done.5
  86.1 0.9 pad_maximum_fusion
  87.0 4.0 %constant_dynamic-update-slice_fusion.1 = bf16[6144,512]{1,0:T(8,128)(2,1)} fusion(bf16[6144,256]{1,0:T(8,128)(2,1)} %param.17), kind=kLoop, calls=%fused_computation.96 | loop fusion | bytes 6291456
  91.0 2.0 constant_dynamic-update-slice_fusion
  93.0 47.5 %all-gather.2.cloned.1.call-done = bf16[768,6144]{1,0:T(8,128)(2,1)} async-done(((bf16[24,6144]{1,0:T(8,128)(2,1)}), bf16[768,6144]{1,0:T(8,128)(2,1)}) %all-gather.2.cloned.1.call-update) | async-done | bytes 9437200 | tf_op jit(solution)/shard_map/all_gather | solution.py:167
  140.5 6.2 %fusion.4 = f32[384,512]{1,0:T(8,128)S(1)} fusion(bf16[6144,512]{1,0:T(8,128)(2,1)} %constant_dynamic-update-slice_fusion, bf16[768,6144]{1,0:T(8,128)(2,1)} %all-gather.2.cloned.1.call-done, s32[]{:T(128)S(6)} %select_n.150), kind=kOutput, calls=%fused_computation.12 | convolution fusion | flops 2415919104 | bytes 11796484 | tf_op jit(solution)/shard_map/dot_general | solution.py:45
  146.8 3.5 %convolution_convert_fusion = bf16[384,6144]{1,0:T(8,128)(2,1)} fusion(bf16[384,256]{1,0:T(8,128)(2,1)S(1)} %fusion.17, bf16[256,6144]{1,0:T(8,128)(2,1)S(1)} %copy-done), kind=kOutput, calls=%fused_computation.4 | convolution fusion | flops 1210318848 | bytes 8060928 | tf_op jit(solution)/shard_map/dot_general | solution.py:49
  150.5 6.2 %fusion.6 = f32[384,512]{1,0:T(8,128)S(1)} fusion(bf16[6144,512]{1,0:T(8,128)(2,1)} %constant_dynamic-update-slice_fusion, bf16[768,6144]{1,0:T(8,128)(2,1)} %all-gather.2.cloned.1.call-done, s32[]{:T(128)S(6)} %select_n.149), kind=kOutput, calls=%fused_computation.14 | convolution fusion | flops 2415919104 | bytes 11796484 | tf_op jit(solution)/shard_map/dot_general | solution.py:45
  156.8 1.7 collective-permute-done.8
  158.5 6.0 %add_convert_fusion = bf16[384,6144]{1,0:T(8,128)(2,1)} fusion(bf16[384,6144]{1,0:T(8,128)(2,1)} %collective-permute-done.8, bf16[384,256]{1,0:T(8,128)(2,1)S(1)} %fusion.18, bf16[256,6144]{1,0:T(8,128)(2,1)S(1)} %copy-done), kind=kOutput, calls=%fused_computation.3 | convolution fusion | flops 1219756032 | bytes 12779520 | tf_op jit(solution)/shard_map/dot_general | solution.py:49
  164.5 7.5 %all-to-all-start.1 = ((bf16[16,24,6144]{2,1,0:T(8,128)(2,1)}), bf16[16,24,6144]{2,1,0:T(8,128)(2,1)}, u32[]{:S(2)}, u32[]{:S(2)}) async-start(bf16[16,24,6144]{2,1,0:T(8,128)(2,1)} %bitcast.87), calls=%async_computation.1 | async-start | bytes 9437184 | tf_op jit(solution)/shard_map/all_to_all | solution.py:179
  172.9 70.9 %all-to-all-done.1 = bf16[16,24,6144]{2,1,0:T(8,128)(2,1)} async-done(((bf16[16,24,6144]{2,1,0:T(8,128)(2,1)}), bf16[16,24,6144]{2,1,0:T(8,128)(2,1)}, u32[]{:S(2)}, u32[]{:S(2)}) %all-to-all-start.1) | async-done | bytes 4718624 | tf_op jit(solution)/shard_map/all_to_all | solution.py:179
  243.8 3.9 %reduce_sum.112 = bf16[24,6144]{1,0:T(8,128)(2,1)} reduce(bf16[16,24,6144]{2,1,0:T(8,128)(2,1)} %all-to-all-done.1, bf16[]{:T(256)} %constant.129.clone.1), dimensions={0}, to_apply=%region_15.16 | reduce | flops 2211840 | bytes 5013506 | tf_op jit(solution)/shard_map/reduce_sum | solution.py:178
  247.7 1.2 slice_bitcast_fusion
  248.9 1.5 collective-permute-start.11
  250.4 2.7 %collective-permute-start.10 = (bf16[6,6144]{1,0:T(8,128)(2,1)S(1)}, bf16[6,6144]{1,0:T(8,128)(2,1)S(1)}, u32[]{:S(2)}, u32[]{:S(2)}) collective-permute-start(bf16[6,6144]{1,0:T(8,128)(2,1)S(1)} %get-tuple-element.19), channel_id=1, source_target_pairs={{0,8},{4,12},{8,0},{12,4},{1,9},{5,13},{9,1},{13,5},{2,10},{6,14},... | collective-permute-start | bytes 221192 | tf_op jit(solution)/shard_map/ppermute | solution.py:188
  253.0 1.5 collective-permute-start.9
  254.6 1.3 collective-permute-done.11
  255.9 1.1 collective-permute-done.10
  257.7 2.5 fusion.3
  (69 shorter events, 8.7 us)
Async XLA Ops:
  6.5 140.2 %copy-start = (bf16[256,6144]{1,0:T(8,128)(2,1)S(1)}, bf16[256,6144]{1,0:T(8,128)(2,1)}, u32[]{:S(2)}) copy-start(bf16[256,6144]{1,0:T(8,128)(2,1)} %param.19) | copy-start | bytes 9437188
  7.6 4.5 %copy-start.3 = (bf16[6144,128]{1,0:T(8,128)(2,1)S(1)}, bf16[6144,128]{1,0:T(8,128)(2,1)}, u32[]{:S(2)}) copy-start(bf16[6144,128]{1,0:T(8,128)(2,1)} %param.12) | copy-start | bytes 4718596
  12.0 5.2 %copy-start.1 = (bf16[128,6144]{1,0:T(8,128)(2,1)}, bf16[128,6144]{1,0:T(8,128)(2,1)S(1)}, u32[]{:S(2)}) copy-start(bf16[128,6144]{1,0:T(8,128)(2,1)S(1)} %fusion.9) | copy-start | bytes 4718596
  13.0 5.1 %collective-permute-start = (bf16[128,128]{1,0:T(8,128)(2,1)S(1)}, bf16[128,128]{1,0:T(8,128)(2,1)S(1)}, u32[]{:S(2)}, u32[]{:S(2)}) collective-permute-start(bf16[128,128]{1,0:T(8,128)(2,1)S(1)} %fusion.34), channel_id=1, source_target_pairs={{0,1},{1,0},{2,3},{3,2},{4,5},{5,4},{6,7},{7,6},{8,9},{9,8},{10,11... | collective-permute-start | bytes 98312 | tf_op jit(solution)/shard_map/ppermute | solution.py:88
  18.7 1.3 collective-permute-start.1
  20.0 6.1 %copy-start.5 = (bf16[2,128,128]{2,1,0:T(8,128)(2,1)}, bf16[2,128,128]{2,1,0:T(8,128)(2,1)S(1)}, u32[]{:S(2)}) copy-start(bf16[2,128,128]{2,1,0:T(8,128)(2,1)S(1)} %collective-permute-done.1) | copy-start | bytes 196612
  20.7 10.8 %collective-permute-start.4 = (bf16[2,2,128,128]{3,2,1,0:T(8,128)(2,1)}, bf16[2,2,128,128]{3,2,1,0:T(8,128)(2,1)}, u32[]{:S(2)}, u32[]{:S(2)}) collective-permute-start(bf16[2,2,128,128]{3,2,1,0:T(8,128)(2,1)} %maximum_select_fusion), channel_id=1, source_target_pairs={{0,32},{32,64},{64,96},{96,0},{1,33},{33,65},{65,97},{97,1},{2,34}... | collective-permute-start | bytes 393224 | tf_op jit(solution)/shard_map/ppermute | solution.py:97
  20.7 10.8 %collective-permute-start.3 = (bf16[2,2,128,128]{3,2,1,0:T(8,128)(2,1)}, bf16[2,2,128,128]{3,2,1,0:T(8,128)(2,1)}, u32[]{:S(2)}, u32[]{:S(2)}) collective-permute-start(bf16[2,2,128,128]{3,2,1,0:T(8,128)(2,1)} %maximum_select_fusion), channel_id=1, source_target_pairs={{0,64},{32,96},{64,0},{96,32},{1,65},{33,97},{65,1},{97,33},{2,66}... | collective-permute-start | bytes 393224 | tf_op jit(solution)/shard_map/ppermute | solution.py:97
  23.1 8.4 %collective-permute-start.2 = (bf16[2,2,128,128]{3,2,1,0:T(8,128)(2,1)}, bf16[2,2,128,128]{3,2,1,0:T(8,128)(2,1)}, u32[]{:S(2)}, u32[]{:S(2)}) collective-permute-start(bf16[2,2,128,128]{3,2,1,0:T(8,128)(2,1)} %maximum_select_fusion), channel_id=1, source_target_pairs={{0,96},{32,0},{64,32},{96,64},{1,97},{33,1},{65,33},{97,65},{2,98}... | collective-permute-start | bytes 393224 | tf_op jit(solution)/shard_map/ppermute | solution.py:97
  30.5 4.9 %copy-start.4 = (pred[128,1024]{1,0:T(8,128)(4,1)S(1)}, pred[128,1024]{1,0:T(8,128)(4,1)}, u32[]{:S(2)}) copy-start(pred[128,1024]{1,0:T(8,128)(4,1)} %compare_and_fusion) | copy-start | bytes 393220
  45.0 7.5 %copy-start.6 = (s32[8,2]{0,1:T(2,128)S(1)}, s32[8,2]{0,1:T(2,128)}, u32[]{:S(2)}) copy-start(s32[8,2]{0,1:T(2,128)} %param.15) | copy-start | bytes 196
  45.0 28.1 %all-to-all-start = ((bf16[16,8,6144]{2,1,0:T(8,128)(2,1)}), bf16[16,8,6144]{2,1,0:T(8,128)(2,1)}, u32[]{:S(2)}, u32[]{:S(2)}) async-start(bf16[16,8,6144]{2,1,0:T(8,128)(2,1)} %fusion.1), calls=%async_computation | async-start | bytes 3145728 | tf_op jit(solution)/shard_map/all_to_all | solution.py:137
  52.4 88.1 %all-gather.2.cloned.1.call-start = ((), (), s32[]{:S(2)}) async-start(), calls=%async_computation.2 | async-start | bytes 9732096 | tf_op jit(solution)/shard_map/all_gather | solution.py:167
  77.2 4.7 %collective-permute-start.7 = (bf16[6,6144]{1,0:T(8,128)(2,1)S(1)}, bf16[6,6144]{1,0:T(8,128)(2,1)S(1)}, u32[]{:S(2)}, u32[]{:S(2)}) collective-permute-start(bf16[6,6144]{1,0:T(8,128)(2,1)S(1)} %get-tuple-element.14), channel_id=1, source_target_pairs={{0,12},{4,0},{8,4},{12,8},{1,13},{5,1},{9,5},{13,9},{2,14},{6,2},{... | collective-permute-start | bytes 221192 | tf_op jit(solution)/shard_map/ppermute | solution.py:164
  78.6 6.1 %collective-permute-start.6 = (bf16[6,6144]{1,0:T(8,128)(2,1)S(1)}, bf16[6,6144]{1,0:T(8,128)(2,1)S(1)}, u32[]{:S(2)}, u32[]{:S(2)}) collective-permute-start(bf16[6,6144]{1,0:T(8,128)(2,1)S(1)} %get-tuple-element.15), channel_id=1, source_target_pairs={{0,8},{4,12},{8,0},{12,4},{1,9},{5,13},{9,1},{13,5},{2,10},{6,14},... | collective-permute-start | bytes 221192 | tf_op jit(solution)/shard_map/ppermute | solution.py:164
  80.3 5.8 %collective-permute-start.5 = (bf16[6,6144]{1,0:T(8,128)(2,1)S(1)}, bf16[6,6144]{1,0:T(8,128)(2,1)S(1)}, u32[]{:S(2)}, u32[]{:S(2)}) collective-permute-start(bf16[6,6144]{1,0:T(8,128)(2,1)S(1)} %get-tuple-element.16), channel_id=1, source_target_pairs={{0,4},{4,8},{8,12},{12,0},{1,5},{5,9},{9,13},{13,1},{2,6},{6,10},{... | collective-permute-start | bytes 221192 | tf_op jit(solution)/shard_map/ppermute | solution.py:164
  87.0 4.0 %copy-start.2 = (bf16[6144,256]{1,0:T(8,128)(2,1)S(1)}, bf16[6144,256]{1,0:T(8,128)(2,1)}, u32[]{:S(2)}) copy-start(bf16[6144,256]{1,0:T(8,128)(2,1)} %param.18) | copy-start | bytes 9437188
  150.3 8.3 %collective-permute-start.8 = (bf16[384,6144]{1,0:T(8,128)(2,1)}, bf16[384,6144]{1,0:T(8,128)(2,1)}, u32[]{:S(2)}, u32[]{:S(2)}) collective-permute-start(bf16[384,6144]{1,0:T(8,128)(2,1)} %convolution_convert_fusion), channel_id=1, source_target_pairs={{0,16},{16,0},{1,17},{17,1},{2,18},{18,2},{3,19},{19,3},{4,20},{20... | collective-permute-start | bytes 14155784 | tf_op jit(solution)/shard_map/ppermute | solution.py:173
  164.5 7.5 %copy-start.7 = (bf16[6144,4]{0,1:T(4,128)(2,1)S(1)}, bf16[6144,4]{0,1:T(4,128)(2,1)}, u32[]{:S(2)}) copy-start(bf16[6144,4]{0,1:T(4,128)(2,1)} %param.16) | copy-start | bytes 147460
  164.5 79.3 %all-to-all-start.1 = ((bf16[16,24,6144]{2,1,0:T(8,128)(2,1)}), bf16[16,24,6144]{2,1,0:T(8,128)(2,1)}, u32[]{:S(2)}, u32[]{:S(2)}) async-start(bf16[16,24,6144]{2,1,0:T(8,128)(2,1)} %bitcast.87), calls=%async_computation.1 | async-start | bytes 9437184 | tf_op jit(solution)/shard_map/all_to_all | solution.py:179
  248.9 6.9 %collective-permute-start.11 = (bf16[6,6144]{1,0:T(8,128)(2,1)S(1)}, bf16[6,6144]{1,0:T(8,128)(2,1)S(1)}, u32[]{:S(2)}, u32[]{:S(2)}) collective-permute-start(bf16[6,6144]{1,0:T(8,128)(2,1)S(1)} %get-tuple-element.18), channel_id=1, source_target_pairs={{0,4},{4,8},{8,12},{12,0},{1,5},{5,9},{9,13},{13,1},{2,6},{6,10},{... | collective-permute-start | bytes 221192 | tf_op jit(solution)/shard_map/ppermute | solution.py:188
  250.4 6.6 %collective-permute-start.10 = (bf16[6,6144]{1,0:T(8,128)(2,1)S(1)}, bf16[6,6144]{1,0:T(8,128)(2,1)S(1)}, u32[]{:S(2)}, u32[]{:S(2)}) collective-permute-start(bf16[6,6144]{1,0:T(8,128)(2,1)S(1)} %get-tuple-element.19), channel_id=1, source_target_pairs={{0,8},{4,12},{8,0},{12,4},{1,9},{5,13},{9,1},{13,5},{2,10},{6,14},... | collective-permute-start | bytes 221192 | tf_op jit(solution)/shard_map/ppermute | solution.py:188
  253.0 4.6 %collective-permute-start.9 = (bf16[6,6144]{1,0:T(8,128)(2,1)S(1)}, bf16[6,6144]{1,0:T(8,128)(2,1)S(1)}, u32[]{:S(2)}, u32[]{:S(2)}) collective-permute-start(bf16[6,6144]{1,0:T(8,128)(2,1)S(1)} %get-tuple-element.20), channel_id=1, source_target_pairs={{0,12},{4,0},{8,4},{12,8},{1,13},{5,1},{9,5},{13,9},{2,14},{6,2},{... | collective-permute-start | bytes 221192 | tf_op jit(solution)/shard_map/ppermute | solution.py:188
Sparse Core Ops, SparseCore 0:
  87.1 53.3 all-gather.1
